TPU v7x, 256 devices: a whole 4x4x8 slice. The times are simulated.
256 devices in a mesh: rows: 128 (over y, x, z), cols: 2 (over core).
Axes of the slice: x: 4, y: 4, z: 8, core: 2. Of those that a mesh axis runs over, the one named last changes fastest.
Arguments:
- matrix: bfloat16 [128, 524288], P('cols', 'rows'), may hold values from -6 to 6
- signs: int32 [524288], P('rows'), may hold values 0 or 1
- samples: int32 [256, 256], replicated, may hold values from 0 to 524287, as said below
- owners: int32 [256, 1], replicated, may hold values from 0 to 127; in each aligned block of 256 rows (0 to 255, 256 to 511, ...) at most 4 rows name the same one
Outputs:
- factors: float32 [512, 128, 128], P('rows', 'cols')
Inputs may be any that keep to these rules, and one draw needn't show every extreme that they name: samples[b, q] = s * 4096 + ((q + b) % 128) * 32 + u with s = q // 2 and 0 <= u < 32. `owners`: every index of rows owns at least one block and at most 4; some index owns exactly 4.
All inputs are finite; a program needn't handle non-finite values. No bound on the sum of `signs` on one device may be relied on, other than what follows from the above.
Results may differ from a plain program's by a relative error of at most 0.0003.
Values sent between devices are 32-bit elements; how exact they have to be, the bound alone decides.
No kernel may reach another device: no remote copies, remote signals or barrier semaphores. Data moves between devices by JAX's collectives and lax.ppermute only.
A program may use at most 64 MiB of HBM per device.

v0:
```python
import math

import jax
import jax.numpy as jnp
from jax import lax
from jax.sharding import PartitionSpec as P

HB = 128
SKETCH_ROW_COUNT = 256
CAPB = 4


def swapped(value, axis, distance):
    return lax.ppermute(value, axis, [(i, i ^ 1 << distance) for i in range(lax.axis_size(axis))])


def walsh_sign_matrix(order):
    index_row = jnp.arange(order, dtype=jnp.int32)
    parity = jnp.zeros((order, order), jnp.int32)
    for bit_place in range(order.bit_length() - 1):
        both = jnp.bitwise_and(index_row[:, None], index_row[None, :])
        parity = parity + jnp.bitwise_and(jnp.right_shift(both, bit_place), 1)
    return (1 - 2 * (parity % 2)).astype(jnp.float32)


def bundle_for_holders(placing, rows_picked, row_devices):
    outgoing = jnp.einsum("kb,bps->kps", placing, rows_picked, precision=lax.Precision.HIGHEST)
    return outgoing.reshape(row_devices, CAPB, rows_picked.shape[1], rows_picked.shape[2])


def deliver_direct(current, samples, placing, processor_number, row_devices, shard_rows):
    per_shard = samples.shape[1] // row_devices
    own_samples = (
        lax.dynamic_slice_in_dim(samples, processor_number * per_shard, per_shard, 1)
        - processor_number * shard_rows
    )
    chosen = jnp.transpose(current[:, own_samples], (1, 2, 0))
    outgoing = bundle_for_holders(placing, chosen, row_devices)
    return lax.all_to_all(outgoing, "rows", split_axis=0, concat_axis=0, tiled=True)


def per_device(matrix, signs, samples, owners):
    slab_width = matrix.shape[0]
    shard_rows = matrix.shape[1]
    row_devices = lax.axis_size("rows")
    processor_number = lax.axis_index("rows")
    flips = (1 - 2 * signs).astype(jnp.bfloat16)
    flipped = matrix * flips[None, :]
    table = walsh_sign_matrix(HB).astype(jnp.bfloat16)
    scale = 1.0 / math.sqrt(HB * row_devices)
    local_mix = jnp.einsum(
        "ij,cbj->cbi",
        table,
        flipped.reshape(slab_width, shard_rows // HB, HB),
        preferred_element_type=jnp.float32,
    )
    current = local_mix.reshape(slab_width, shard_rows) * scale
    owner_list = owners[:, 0]
    block_total = owner_list.shape[0]
    positions = jnp.arange(block_total, dtype=jnp.int32)
    preceding_rows = jnp.logical_and(
        owner_list[None, :] == owner_list[:, None], positions[None, :] < positions[:, None]
    )
    ranks = jnp.sum(preceding_rows.astype(jnp.int32), axis=1)
    slots = owner_list * CAPB + ranks
    placing = (jnp.arange(row_devices * CAPB, dtype=jnp.int32)[:, None] == slots[None, :]).astype(
        jnp.float32
    )
    per_shard = samples.shape[1] // row_devices
    for section_bit in range(row_devices.bit_length() - 1):
        partner = swapped(current, "rows", section_bit)
        bit_value = jnp.bitwise_and(jnp.right_shift(processor_number, section_bit), 1)
        current = jnp.where(bit_value == 1, partner - current, current + partner)
    arriving = deliver_direct(current, samples, placing, processor_number, row_devices, shard_rows)
    received = jnp.transpose(arriving, (1, 0, 2, 3)).reshape(
        CAPB, row_devices * per_shard, slab_width
    )
    whole_rows = lax.all_gather(received, "cols", axis=2, tiled=True)
    window_width = whole_rows.shape[2]
    gram_product = (
        jnp.einsum("sqi,sqk->sik", whole_rows, whole_rows, precision=lax.Precision.HIGHEST)
        / SKETCH_ROW_COUNT
    )
    owned_total = jnp.sum((owner_list == processor_number).astype(jnp.int32))
    live = jnp.arange(CAPB, dtype=jnp.int32) < owned_total
    identity = jnp.eye(window_width, dtype=jnp.float32)
    safe = jnp.where(live[:, None, None], gram_product, identity[None, :, :])
    upper = jnp.swapaxes(jnp.linalg.cholesky(safe), -1, -2)
    upper = jnp.where(live[:, None, None], upper, jnp.zeros_like(upper))
    column_start = lax.axis_index("cols") * slab_width
    return lax.dynamic_slice_in_dim(upper, column_start, slab_width, 1)


def solution(mesh):
    in_specs = (P("cols", "rows"), P("rows"), P(), P())
    out_specs = P("rows", "cols", None)
    return jax.shard_map(
        per_device, mesh=mesh, in_specs=in_specs, out_specs=out_specs, check_vma=False
    )
```

profile of v0, /device:TPU:1, one launch (start us, length us, event | category | flops | bytes accessed | tf_op | source)
XLA Modules:
  0.0 354.6 jit_solution(2170922908704120128)
XLA Ops:
  0.0 0.7 subtract_convert_fusion
  0.7 1.1 multiply_bitcast_fusion
  2.9 2.6 collective-permute-start
  5.4 2.0 copy.60
  7.4 19.9 %collective-permute-done = f32[64,4096]{1,0:T(8,128)S(1)} collective-permute-done((f32[64,4096]{1,0:T(8,128)S(1)}, f32[64,4096]{1,0:T(8,128)S(1)}, u32[]{:S(2)}, u32[]{:S(2)}) %collective-permute-start) | collective-permute-done | bytes 1048608 | tf_op jit(solution)/shard_map/ppermute | solution.py:14
  27.3 1.9 copy.59
  29.2 2.4 add_select_fusion.6
  31.6 1.6 copy.63
  33.2 3.9 %collective-permute-start.1 = (f32[64,4096]{1,0:T(8,128)}, f32[64,4096]{1,0:T(8,128)S(1)}, u32[]{:S(2)}, u32[]{:S(2)}) collective-permute-start(f32[64,4096]{1,0:T(8,128)} %copy.63), channel_id=1, source_target_pairs={{0,4},{2,6},{4,0},{6,2},{8,12},{10,14},{12,8},{14,10},{16,20},{18,... | collective-permute-start | bytes 3145736 | tf_op jit(solution)/shard_map/ppermute | solution.py:14
  37.1 45.3 %collective-permute-done.1 = f32[64,4096]{1,0:T(8,128)S(1)} collective-permute-done((f32[64,4096]{1,0:T(8,128)}, f32[64,4096]{1,0:T(8,128)S(1)}, u32[]{:S(2)}, u32[]{:S(2)}) %collective-permute-start.1) | collective-permute-done | bytes 1048608 | tf_op jit(solution)/shard_map/ppermute | solution.py:14
  82.4 1.9 copy.64
  84.3 3.1 add_select_fusion.5
  87.4 2.2 copy.66
  89.6 6.6 %collective-permute-start.2 = (f32[64,4096]{1,0:T(8,128)S(1)}, f32[64,4096]{1,0:T(8,128)S(1)}, u32[]{:S(2)}, u32[]{:S(2)}) collective-permute-start(f32[64,4096]{1,0:T(8,128)S(1)} %copy.66), channel_id=1, source_target_pairs={{0,8},{2,10},{4,12},{6,14},{8,0},{10,2},{12,4},{14,6},{16,24},{18,... | collective-permute-start | bytes 3145736 | tf_op jit(solution)/shard_map/ppermute | solution.py:14
  96.2 45.5 %collective-permute-done.2 = f32[64,4096]{1,0:T(8,128)S(1)} collective-permute-done((f32[64,4096]{1,0:T(8,128)S(1)}, f32[64,4096]{1,0:T(8,128)S(1)}, u32[]{:S(2)}, u32[]{:S(2)}) %collective-permute-start.2) | collective-permute-done | bytes 1048608 | tf_op jit(solution)/shard_map/ppermute | solution.py:14
  141.7 2.0 copy.67
  143.7 2.4 add_select_fusion.4
  146.1 1.6 copy.69
  147.7 1.2 collective-permute-start.3
  148.9 22.2 %collective-permute-done.3 = f32[64,4096]{1,0:T(8,128)S(1)} collective-permute-done((f32[64,4096]{1,0:T(8,128)}, f32[64,4096]{1,0:T(8,128)S(1)}, u32[]{:S(2)}, u32[]{:S(2)}) %collective-permute-start.3) | collective-permute-done | bytes 1048608 | tf_op jit(solution)/shard_map/ppermute | solution.py:14
  171.1 1.9 copy.70
  173.0 3.1 add_select_fusion.3
  176.1 3.2 copy.72
  179.2 2.6 collective-permute-start.4
  181.8 21.4 %collective-permute-done.4 = f32[64,4096]{1,0:T(8,128)S(1)} collective-permute-done((f32[64,4096]{1,0:T(8,128)}, f32[64,4096]{1,0:T(8,128)S(1)}, u32[]{:S(2)}, u32[]{:S(2)}) %collective-permute-start.4) | collective-permute-done | bytes 1048608 | tf_op jit(solution)/shard_map/ppermute | solution.py:14
  203.2 2.0 copy.73
  205.2 3.2 add_select_fusion.2
  208.4 2.2 copy.75
  210.6 1.4 collective-permute-start.5
  211.9 20.1 %collective-permute-done.5 = f32[64,4096]{1,0:T(8,128)S(1)} collective-permute-done((f32[64,4096]{1,0:T(8,128)S(1)}, f32[64,4096]{1,0:T(8,128)S(1)}, u32[]{:S(2)}, u32[]{:S(2)}) %collective-permute-start.5) | collective-permute-done | bytes 1048608 | tf_op jit(solution)/shard_map/ppermute | solution.py:14
  232.1 1.9 copy.76
  234.0 2.4 add_select_fusion.1
  236.5 1.6 copy.78
  238.1 2.9 collective-permute-start.6
  240.9 1.0 compare_select_fusion
  242.3 0.6 fusion.24
  243.0 17.4 %collective-permute-done.6 = f32[64,4096]{1,0:T(8,128)S(1)} collective-permute-done((f32[64,4096]{1,0:T(8,128)}, f32[64,4096]{1,0:T(8,128)S(1)}, u32[]{:S(2)}, u32[]{:S(2)}) %collective-permute-start.6) | collective-permute-done | bytes 1048608 | tf_op jit(solution)/shard_map/ppermute | solution.py:14
  260.4 1.9 copy.79
  262.3 2.4 add_select_fusion
  264.8 1.0 gather_fusion
  266.7 1.2 reshape.55
  267.8 15.9 %all-to-all-start = ((f32[128,1,512]{2,1,0:T(1,128)}), f32[128,1,512]{2,1,0:T(1,128)S(1)}, u32[]{:S(2)}, u32[]{:S(2)}) async-start(f32[128,1,512]{2,1,0:T(1,128)} %reshape.55), calls=%async_computation | async-start | bytes 524288 | tf_op jit(solution)/shard_map/all_to_all | solution.py:39
  283.7 0.7 iota_compare_fusion.6
  284.4 11.8 %all-to-all-done = f32[128,1,512]{2,1,0:T(1,128)S(1)} async-done(((f32[128,1,512]{2,1,0:T(1,128)}), f32[128,1,512]{2,1,0:T(1,128)S(1)}, u32[]{:S(2)}, u32[]{:S(2)}) %all-to-all-start) | async-done | bytes 262176 | tf_op jit(solution)/shard_map/all_to_all | solution.py:39
  296.8 1.3 reduce.6
  298.5 7.2 %all_gather.3 = f32[4,256,128]{1,2,0:T(8,128)S(1)} all-gather(f32[4,256,64]{1,2,0:T(8,128)S(1)} %copy.85), channel_id=1, replica_groups=mesh['rows'=128,'cols'=2] {'cols'}, dimensions={2}, use_global_device_ids=true | all-gather | bytes 786432 | tf_op jit(solution)/shard_map/all_gather | solution.py:78
  306.6 46.9 %custom-call.4 = f32[4,128,128]{2,1,0:T(8,128)S(1)} custom-call(f32[4,128,128]{2,1,0:T(8,128)S(1)} %fusion.2), custom_call_target="Cholesky" | custom-call | tf_op jit(solution)/shard_map/jit(cholesky)/cholesky | solution.py:88
  353.9 0.8 fusion.7
  (30 shorter events, 4.5 us)
Async XLA Ops:
  2.9 24.4 %collective-permute-start = (f32[64,4096]{1,0:T(8,128)S(1)}, f32[64,4096]{1,0:T(8,128)S(1)}, u32[]{:S(2)}, u32[]{:S(2)}) collective-permute-start(f32[64,4096]{1,0:T(8,128)S(1)} %bitcast.35), channel_id=1, source_target_pairs={{0,2},{2,0},{4,6},{6,4},{8,10},{10,8},{12,14},{14,12},{16,18},{18,... | collective-permute-start | bytes 3145736 | tf_op jit(solution)/shard_map/ppermute | solution.py:14
  33.2 49.2 %collective-permute-start.1 = (f32[64,4096]{1,0:T(8,128)}, f32[64,4096]{1,0:T(8,128)S(1)}, u32[]{:S(2)}, u32[]{:S(2)}) collective-permute-start(f32[64,4096]{1,0:T(8,128)} %copy.63), channel_id=1, source_target_pairs={{0,4},{2,6},{4,0},{6,2},{8,12},{10,14},{12,8},{14,10},{16,20},{18,... | collective-permute-start | bytes 3145736 | tf_op jit(solution)/shard_map/ppermute | solution.py:14
  89.6 52.1 %collective-permute-start.2 = (f32[64,4096]{1,0:T(8,128)S(1)}, f32[64,4096]{1,0:T(8,128)S(1)}, u32[]{:S(2)}, u32[]{:S(2)}) collective-permute-start(f32[64,4096]{1,0:T(8,128)S(1)} %copy.66), channel_id=1, source_target_pairs={{0,8},{2,10},{4,12},{6,14},{8,0},{10,2},{12,4},{14,6},{16,24},{18,... | collective-permute-start | bytes 3145736 | tf_op jit(solution)/shard_map/ppermute | solution.py:14
  147.7 23.4 %collective-permute-start.3 = (f32[64,4096]{1,0:T(8,128)}, f32[64,4096]{1,0:T(8,128)S(1)}, u32[]{:S(2)}, u32[]{:S(2)}) collective-permute-start(f32[64,4096]{1,0:T(8,128)} %copy.69), channel_id=1, source_target_pairs={{0,16},{2,18},{4,20},{6,22},{8,24},{10,26},{12,28},{14,30},{16,0},... | collective-permute-start | bytes 3145736 | tf_op jit(solution)/shard_map/ppermute | solution.py:14
  179.2 26.0 %copy-start.1 = (f32[64,4096]{0,1:T(8,128)S(1)}, f32[64,4096]{0,1:T(8,128)}, u32[]{:S(2)}) copy-start(f32[64,4096]{0,1:T(8,128)} %add_select_fusion.3) | copy-start | bytes 3145732
  179.2 24.0 %collective-permute-start.4 = (f32[64,4096]{1,0:T(8,128)}, f32[64,4096]{1,0:T(8,128)S(1)}, u32[]{:S(2)}, u32[]{:S(2)}) collective-permute-start(f32[64,4096]{1,0:T(8,128)} %copy.72), channel_id=1, source_target_pairs={{0,32},{2,34},{4,36},{6,38},{8,40},{10,42},{12,44},{14,46},{16,48}... | collective-permute-start | bytes 3145736 | tf_op jit(solution)/shard_map/ppermute | solution.py:14
  210.6 21.5 %collective-permute-start.5 = (f32[64,4096]{1,0:T(8,128)S(1)}, f32[64,4096]{1,0:T(8,128)S(1)}, u32[]{:S(2)}, u32[]{:S(2)}) collective-permute-start(f32[64,4096]{1,0:T(8,128)S(1)} %copy.75), channel_id=1, source_target_pairs={{0,64},{2,66},{4,68},{6,70},{8,72},{10,74},{12,76},{14,78},{16,80}... | collective-permute-start | bytes 3145736 | tf_op jit(solution)/shard_map/ppermute | solution.py:14
  236.4 24.0 %copy-start = (f32[64,4096]{0,1:T(8,128)}, f32[64,4096]{0,1:T(8,128)S(1)}, u32[]{:S(2)}) copy-start(f32[64,4096]{0,1:T(8,128)S(1)} %add_select_fusion.1) | copy-start | bytes 3145732
  236.4 5.7 %copy-start.2 = (s32[256,1]{0,1:T(1,128)S(1)}, s32[256,1]{0,1:T(1,128)}, u32[]{:S(2)}) copy-start(s32[256,1]{0,1:T(1,128)} %param.7) | copy-start | bytes 3076
  238.1 22.3 %collective-permute-start.6 = (f32[64,4096]{1,0:T(8,128)}, f32[64,4096]{1,0:T(8,128)S(1)}, u32[]{:S(2)}, u32[]{:S(2)}) collective-permute-start(f32[64,4096]{1,0:T(8,128)} %copy.78), channel_id=1, source_target_pairs={{0,128},{2,130},{4,132},{6,134},{8,136},{10,138},{12,140},{14,142}... | collective-permute-start | bytes 3145736 | tf_op jit(solution)/shard_map/ppermute | solution.py:14
  267.8 28.4 %all-to-all-start = ((f32[128,1,512]{2,1,0:T(1,128)}), f32[128,1,512]{2,1,0:T(1,128)S(1)}, u32[]{:S(2)}, u32[]{:S(2)}) async-start(f32[128,1,512]{2,1,0:T(1,128)} %reshape.55), calls=%async_computation | async-start | bytes 524288 | tf_op jit(solution)/shard_map/all_to_all | solution.py:39
where the time goes:
time: 355 us
  waiting for transfers between devices  204 us (57%)
  other arithmetic  72.7 us (20%)
  starting transfers between devices  36.9 us (10%)
  local copies, waits for them, and re-layouts  32.5 us (9%)
  blocking collectives  7.19 us (2%)
    ppermute x7, waiting for transfers between devices, swapped(): lax.ppermute(value, axis, [(i, i ^ 1 << distance) for i in range(lax.axis...  192 us
    another operation x4, other arithmetic, per_device(): upper = jnp.swapaxes(jnp.linalg.cholesky(safe), -1, -2)  47.2 us
    ppermute x7, starting transfers between devices, swapped(): lax.ppermute(value, axis, [(i, i ^ 1 << distance) for i in range(lax.axis...  21.1 us
    select_n x7, other arithmetic, per_device(): current = jnp.where(bit_value == 1, partner - current, current + partner)  19.1 us
    all_to_all x1, starting transfers between devices, deliver_direct(): lax.all_to_all(outgoing, 'rows', split_axis=0, concat_axis=0, tiled=True)  15.9 us
    ppermute x7, local copies, waits for them, and re-layouts, swapped(): lax.ppermute(value, axis, [(i, i ^ 1 << distance) for i in range(lax.axis...  13.4 us
    select_n x6, local copies, waits for them, and re-layouts, per_device(): current = jnp.where(bit_value == 1, partner - current, current + partner)  12.3 us
    all_to_all x1, waiting for transfers between devices, deliver_direct(): lax.all_to_all(outgoing, 'rows', split_axis=0, concat_axis=0, tiled=True)  11.8 us
  transfers between devices with their start and end apart: 8, of which 8 were waited for; matrix products, arithmetic and copies ran while one was open for 1% of the time, Pallas kernels for 0%

commit v1 on v0

v1 whole, which is shorter than its diff:
```python
import math

import jax
import jax.numpy as jnp
from jax import lax
from jax.sharding import PartitionSpec as P

HB = 128
SKETCH_ROW_COUNT = 256
CAPB = 4


def walsh_sign_matrix(order):
    index_row = jnp.arange(order, dtype=jnp.int32)
    parity = jnp.zeros((order, order), jnp.int32)
    for bit_place in range(order.bit_length() - 1):
        both = jnp.bitwise_and(index_row[:, None], index_row[None, :])
        parity = parity + jnp.bitwise_and(jnp.right_shift(both, bit_place), 1)
    return (1 - 2 * (parity % 2)).astype(jnp.float32)


def per_device(matrix, signs, samples, owners):
    slab_width = matrix.shape[0]
    shard_rows = matrix.shape[1]
    row_devices = lax.axis_size("rows")
    processor_number = lax.axis_index("rows")
    sub_rows = shard_rows // row_devices
    flips = (1 - 2 * signs).astype(jnp.bfloat16)
    flipped = matrix * flips[None, :]
    table = walsh_sign_matrix(HB).astype(jnp.bfloat16)
    scale = 1.0 / math.sqrt(HB * row_devices)
    local_mix = jnp.einsum(
        "huj,cbj->bhuc",
        table.reshape(HB // sub_rows, sub_rows, HB),
        flipped.reshape(slab_width, shard_rows // HB, HB),
        preferred_element_type=jnp.float32,
    )
    outgoing = local_mix.reshape(row_devices, sub_rows, slab_width) * scale
    received = lax.all_to_all(outgoing, "rows", split_axis=0, concat_axis=0, tiled=True)
    across = walsh_sign_matrix(row_devices)
    mixed = jnp.einsum(
        "st,tuc->suc", across, received, precision=lax.Precision.HIGHEST
    ).reshape(row_devices * sub_rows, slab_width)

    block_total = samples.shape[0]
    block_ids = jnp.arange(block_total, dtype=jnp.int32)
    first_q = jnp.mod(processor_number - block_ids, row_devices)
    picks = jnp.stack([first_q, first_q + row_devices], axis=1)
    sample_values = jnp.take_along_axis(samples, picks, axis=1)
    shard_of = picks // (samples.shape[1] // row_devices)
    offsets = sample_values - shard_of * shard_rows - processor_number * sub_rows
    chosen = jnp.take(mixed, shard_of * sub_rows + offsets, axis=0)

    owner_list = owners[:, 0]
    preceding_rows = jnp.logical_and(
        owner_list[None, :] == owner_list[:, None], block_ids[None, :] < block_ids[:, None]
    )
    ranks = jnp.sum(preceding_rows.astype(jnp.int32), axis=1)
    slots = owner_list * CAPB + ranks
    placing = (jnp.arange(row_devices * CAPB, dtype=jnp.int32)[:, None] == slots[None, :]).astype(
        jnp.float32
    )
    bundled = jnp.einsum("kb,bps->kps", placing, chosen, precision=lax.Precision.HIGHEST)
    bundled = bundled.reshape(row_devices, CAPB, 2, slab_width)
    arriving = lax.all_to_all(bundled, "rows", split_axis=0, concat_axis=0, tiled=True)
    received_rows = jnp.transpose(arriving, (1, 0, 2, 3)).reshape(CAPB, row_devices * 2, slab_width)
    whole_rows = lax.all_gather(received_rows, "cols", axis=2, tiled=True)
    window_width = whole_rows.shape[2]
    gram_product = (
        jnp.einsum("sqi,sqk->sik", whole_rows, whole_rows, precision=lax.Precision.HIGHEST)
        / SKETCH_ROW_COUNT
    )
    owned_total = jnp.sum((owner_list == processor_number).astype(jnp.int32))
    live = jnp.arange(CAPB, dtype=jnp.int32) < owned_total
    identity = jnp.eye(window_width, dtype=jnp.float32)
    safe = jnp.where(live[:, None, None], gram_product, identity[None, :, :])
    upper = jnp.swapaxes(jnp.linalg.cholesky(safe), -1, -2)
    upper = jnp.where(live[:, None, None], upper, jnp.zeros_like(upper))
    column_start = lax.axis_index("cols") * slab_width
    return lax.dynamic_slice_in_dim(upper, column_start, slab_width, 1)


def solution(mesh):
    in_specs = (P("cols", "rows"), P("rows"), P(), P())
    out_specs = P("rows", "cols", None)
    return jax.shard_map(
        per_device, mesh=mesh, in_specs=in_specs, out_specs=out_specs, check_vma=False
    )
```

time: 355 us -> 144 us (0.41)
  waiting for transfers between devices: 204 us -> 35.3 us
  other arithmetic: 72.7 us -> 55.9 us
  starting transfers between devices: 36.9 us -> 22.9 us
  local copies, waits for them, and re-layouts: 32.5 us -> 19.4 us
    ppermute x7 -> x0, waiting for transfers between devices: 192 us -> none  [swapped(): lax.ppermute(value, axis, [(i, i ^ 1 << distance) for i in range(lax.axis...]
    all_to_all x1 -> x2, waiting for transfers between devices: 11.8 us -> 35.3 us  [the longest x1 23.5 us: per_device(): lax.all_to_all(outgoing, 'rows', split_axis=0, concat_axis=0, tiled=True)]
    ppermute x7 -> x0, starting transfers between devices: 21.1 us -> none  [swapped(): lax.ppermute(value, axis, [(i, i ^ 1 << distance) for i in range(lax.axis...]
    select_n x8 -> x3, other arithmetic: 20.1 us -> 0.07 us  [the longest x2 0.05 us: per_device(): chosen = jnp.take(mixed, shard_of * sub_rows + offsets, axis=0)]
    ppermute x7 -> x0, local copies, waits for them, and re-layouts: 13.4 us -> none  [swapped(): lax.ppermute(value, axis, [(i, i ^ 1 << distance) for i in range(lax.axis...]
    select_n x6 -> x2, local copies, waits for them, and re-layouts: 12.3 us -> 0.28 us  [per_device(): chosen = jnp.take(mixed, shard_of * sub_rows + offsets, axis=0)]
    all_to_all x1 -> x2, starting transfers between devices: 15.9 us -> 22.9 us  [the longest x1 16.5 us: per_device(): lax.all_to_all(outgoing, 'rows', split_axis=0, concat_axis=0, tiled=True)]
    gather x2 -> x9, local copies, waits for them, and re-layouts: 1.16 us -> 6.39 us  [the longest x7 5.23 us: per_device(): sample_values = jnp.take_along_axis(samples, picks, axis=1)]
  transfers between devices with their start and end apart: 8 -> 2, of which waited for: 8 -> 2; matrix products, arithmetic and copies ran while one was open for 1% -> 5% of each run, Pallas kernels for 0% -> 0%
where the time goes in v1:
time: 144 us
  other arithmetic  55.9 us (39%)
  waiting for transfers between devices  35.3 us (25%)
  starting transfers between devices  22.9 us (16%)
  local copies, waits for them, and re-layouts  19.4 us (13%)
  blocking collectives  5.37 us (4%)
  matrix products  4.87 us (3%)
    another operation x4, other arithmetic, per_device(): upper = jnp.swapaxes(jnp.linalg.cholesky(safe), -1, -2)  47.2 us
    all_to_all x1, waiting for transfers between devices, per_device(): lax.all_to_all(outgoing, 'rows', split_axis=0, concat_axis=0, tiled=True)  23.5 us
    all_to_all x1, starting transfers between devices, per_device(): lax.all_to_all(outgoing, 'rows', split_axis=0, concat_axis=0, tiled=True)  16.5 us
    all_to_all x1, waiting for transfers between devices, per_device(): lax.all_to_all(bundled, 'rows', split_axis=0, concat_axis=0, tiled=True)  11.7 us
    all_to_all x1, starting transfers between devices, per_device(): lax.all_to_all(bundled, 'rows', split_axis=0, concat_axis=0, tiled=True)  6.39 us
    all_gather x1, blocking collectives, per_device(): whole_rows = lax.all_gather(received_rows, 'cols', axis=2, tiled=True)  5.37 us
    gather x7, local copies, waits for them, and re-layouts, per_device(): sample_values = jnp.take_along_axis(samples, picks, axis=1)  5.23 us
    unnamed x9, local copies, waits for them, and re-layouts  4.68 us
  transfers between devices with their start and end apart: 2, of which 2 were waited for; matrix products, arithmetic and copies ran while one was open for 5% of the time, Pallas kernels for 0%

profile of v1, /device:TPU:1, one launch (start us, length us, event | category | flops | bytes accessed | tf_op | source)
XLA Modules:
  0.0 144.1 jit_solution(4396828559685897636)
XLA Ops:
  0.0 0.0 copy-start
  0.0 0.8 subtract_convert_fusion
  0.8 1.1 multiply_bitcast_fusion.1
  1.9 0.1 copy.97
  2.0 2.8 %multiply_bitcast_fusion = f32[32,4,32,64]{2,0,1,3:T(8,128)} fusion(bf16[64,32,128,1]{2,1,0,3:T(8,128)(2,1)S(1)} %bitcast.54, s32[4,32]{1,0:T(4,128)S(1)} %multiply_add_fusion), kind=kOutput, calls=%fused_computation.2 | convolution fusion | flops 67960832 | bytes 1573376 | tf_op jit(solution)/shard_map/huj,cbj->bhuc/dot_general | solution.py:32
  4.7 3.8 %copy.78 = f32[32,4,32,64]{3,2,1,0:T(8,128)S(1)} copy(f32[32,4,32,64]{2,0,1,3:T(8,128)} %multiply_bitcast_fusion) | data formatting | bytes 2097152 | tf_op jit(solution)/shard_map/mul | solution.py:38
  8.5 2.3 %reshape.469 = f32[128,1,2048]{2,1,0:T(1,128)} reshape(f32[128,32,64]{2,1,0:T(8,128)S(1)} %bitcast.50) | data formatting | bytes 2097152
  10.8 16.5 %all-to-all-start = ((f32[128,1,2048]{2,1,0:T(1,128)}), f32[128,1,2048]{2,1,0:T(1,128)S(1)}, u32[]{:S(2)}, u32[]{:S(2)}) async-start(f32[128,1,2048]{2,1,0:T(1,128)} %reshape.469), calls=%async_computation | async-start | bytes 2097152 | tf_op jit(solution)/shard_map/all_to_all | solution.py:39
  27.4 0.1 copy.76
  27.5 0.1 reshape.454
  27.7 0.0 copy-start.1
  27.7 4.5 %gather_fusion.1 = s32[512]{0:T(512)S(1)} fusion(s32[256,256]{1,0:T(8,128)S(1)} %copy-done, s32[512]{0:T(512)S(1)} %reshape.454), kind=kCustom, calls=%fused_computation.1 | custom fusion | bytes 8192 | tf_op jit(solution)/shard_map/jit(take_along_axis)/gather | solution.py:49
  32.2 0.1 gather.11
  32.3 0.1 reshape.457
  32.5 0.1 copy.81
  32.6 0.1 copy.82
  32.7 0.1 reshape.448
  32.9 0.1 copy.77
  33.0 0.2 convert_reduce_fusion
  33.2 0.6 fusion.44
  33.9 23.5 %all-to-all-done = f32[128,1,2048]{2,1,0:T(1,128)S(1)} async-done(((f32[128,1,2048]{2,1,0:T(1,128)}), f32[128,1,2048]{2,1,0:T(1,128)S(1)}, u32[]{:S(2)}, u32[]{:S(2)}) %all-to-all-start) | async-done | bytes 1048608 | tf_op jit(solution)/shard_map/all_to_all | solution.py:39
  57.4 0.6 broadcast.1051
  58.0 3.2 %reduce.6 = f32[128,2048]{1,0:T(8,128)S(1)} reduce(f32[128,1,2048]{2,1,0:T(1,128)S(1)} %all-to-all-done, f32[]{:T(128)} %broadcast.1051), dimensions={1}, to_apply=%all_to_all.6.reduce_sub_computation | reduce | bytes 2097156 | tf_op jit(solution)/shard_map/all_to_all | solution.py:39
  61.1 0.8 reshape.470
  62.0 1.3 copy.79
  63.3 1.1 fusion.13
  64.4 1.7 %copy.80 = f32[128,32,64]{2,1,0:T(8,128)S(1)} copy(f32[128,32,64]{0,2,1:T(8,128)S(1)} %bitcast.53) | data formatting | bytes 2097152 | tf_op jit(solution)/shard_map/st,tuc->suc/dot_general | solution.py:41
  66.0 1.0 gather_fusion
  67.1 0.1 copy.83
  67.2 0.4 fusion.1
  67.7 0.2 copy.84
  67.9 0.1 copy.99
  68.0 1.2 reshape.471
  69.1 6.4 %all-to-all-start.1 = ((f32[128,1,512]{2,1,0:T(1,128)}), f32[128,1,512]{2,1,0:T(1,128)S(1)}, u32[]{:S(2)}, u32[]{:S(2)}) async-start(f32[128,1,512]{2,1,0:T(1,128)} %reshape.471), calls=%async_computation.1 | async-start | bytes 524288 | tf_op jit(solution)/shard_map/all_to_all | solution.py:65
  75.5 0.7 iota_compare_fusion.6
  76.3 11.7 %all-to-all-done.1 = f32[128,1,512]{2,1,0:T(1,128)S(1)} async-done(((f32[128,1,512]{2,1,0:T(1,128)}), f32[128,1,512]{2,1,0:T(1,128)S(1)}, u32[]{:S(2)}, u32[]{:S(2)}) %all-to-all-start.1) | async-done | bytes 262176 | tf_op jit(solution)/shard_map/all_to_all | solution.py:65
  88.0 1.2 reduce.7
  89.3 0.3 reshape.472
  89.6 0.2 copy.87
  89.8 5.4 %all_gather.3 = f32[4,256,128]{1,2,0:T(8,128)S(1)} all-gather(f32[4,256,64]{1,2,0:T(8,128)S(1)} %copy.87), channel_id=1, replica_groups=mesh['rows'=128,'cols'=2] {'cols'}, dimensions={2}, use_global_device_ids=true | all-gather | bytes 786432 | tf_op jit(solution)/shard_map/all_gather | solution.py:67
  95.1 0.6 broadcast_select_fusion
  95.8 0.1 copy.90
  95.9 0.1 fusion.3
  96.0 46.9 %custom-call.4 = f32[4,128,128]{2,1,0:T(8,128)S(1)} custom-call(f32[4,128,128]{2,1,0:T(8,128)S(1)} %fusion.3), custom_call_target="Cholesky" | custom-call | tf_op jit(solution)/shard_map/jit(cholesky)/cholesky | solution.py:77
  142.9 0.1 copy.91
  143.0 0.1 select_reduce_fusion
  143.2 0.1 compare_reduce_fusion
  143.3 0.8 fusion.8
  (15 shorter events, 0.2 us)
Async XLA Ops:
  0.0 27.6 %copy-start = (s32[256,256]{1,0:T(8,128)S(1)}, s32[256,256]{1,0:T(8,128)}, u32[]{:S(2)}) copy-start(s32[256,256]{1,0:T(8,128)} %param.6) | copy-start | bytes 786436
  10.8 46.6 %all-to-all-start = ((f32[128,1,2048]{2,1,0:T(1,128)}), f32[128,1,2048]{2,1,0:T(1,128)S(1)}, u32[]{:S(2)}, u32[]{:S(2)}) async-start(f32[128,1,2048]{2,1,0:T(1,128)} %reshape.469), calls=%async_computation | async-start | bytes 2097152 | tf_op jit(solution)/shard_map/all_to_all | solution.py:39
  27.7 5.4 %copy-start.1 = (s32[256,1]{0,1:T(1,128)S(1)}, s32[256,1]{0,1:T(1,128)}, u32[]{:S(2)}) copy-start(s32[256,1]{0,1:T(1,128)} %param.7) | copy-start | bytes 3076
  69.1 18.9 %all-to-all-start.1 = ((f32[128,1,512]{2,1,0:T(1,128)}), f32[128,1,512]{2,1,0:T(1,128)S(1)}, u32[]{:S(2)}, u32[]{:S(2)}) async-start(f32[128,1,512]{2,1,0:T(1,128)} %reshape.471), calls=%async_computation.1 | async-start | bytes 524288 | tf_op jit(solution)/shard_map/all_to_all | solution.py:65

commit v2 on v1

--- a/solution.py
+++ b/solution.py
@@ -3,11 +3,55 @@
 import jax
 import jax.numpy as jnp
 from jax import lax
+from jax.experimental import pallas as pl
+from jax.experimental.pallas import tpu as pltpu
 from jax.sharding import PartitionSpec as P
 
 HB = 128
 SKETCH_ROW_COUNT = 256
 CAPB = 4
+
+PANEL = 8
+
+
+def cholesky_kernel(gram_ref, out_ref, work_ref):
+    blocks, order, _ = gram_ref.shape
+    work_ref[...] = gram_ref[...]
+    lane = lax.broadcasted_iota(jnp.int32, (blocks, 1, order), 2)
+    lane_panel = lax.broadcasted_iota(jnp.int32, (blocks, PANEL, order), 2)
+    sub_panel = lax.broadcasted_iota(jnp.int32, (blocks, PANEL, order), 1)
+    for p in range(order // PANEL):
+        base = p * PANEL
+        panel = work_ref[:, base:base + PANEL, :]
+        for jj in range(PANEL):
+            j = base + jj
+            row = panel[:, jj:jj + 1, :]
+            pivot = row[:, :, j:j + 1]
+            r = jnp.where(lane >= j, row / jnp.sqrt(pivot), 0.0)
+            spread = jnp.broadcast_to(r, (blocks, PANEL, order))
+            col = jnp.sum(jnp.where(lane_panel == base + sub_panel, spread, 0.0), axis=2, keepdims=True)
+            col = jnp.where(sub_panel[:, :, :1] > jj, col, 0.0)
+            panel = panel - col * spread
+            panel = jnp.where(sub_panel == jj, spread, panel)
+        out_ref[:, base:base + PANEL, :] = panel
+        if p + 1 < order // PANEL:
+            for b in range(blocks):
+                update = lax.dot_general(
+                    panel[b], panel[b], (((0,), (0,)), ((), ())),
+                    precision=lax.Precision.HIGHEST, preferred_element_type=jnp.float32,
+                )
+                work_ref[b, base + PANEL:, :] = work_ref[b, base + PANEL:, :] - update[base + PANEL:, :]
+
+
+def cholesky_upper(gram):
+    blocks, order, _ = gram.shape
+    return pl.pallas_call(
+        cholesky_kernel,
+        out_shape=jax.ShapeDtypeStruct(gram.shape, jnp.float32),
+        in_specs=[pl.BlockSpec(memory_space=pltpu.VMEM)],
+        out_specs=pl.BlockSpec(memory_space=pltpu.VMEM),
+        scratch_shapes=[pltpu.VMEM(gram.shape, jnp.float32)],
+    )(gram)
 
 
 def walsh_sign_matrix(order):
@@ -74,7 +118,7 @@
     live = jnp.arange(CAPB, dtype=jnp.int32) < owned_total
     identity = jnp.eye(window_width, dtype=jnp.float32)
     safe = jnp.where(live[:, None, None], gram_product, identity[None, :, :])
-    upper = jnp.swapaxes(jnp.linalg.cholesky(safe), -1, -2)
+    upper = cholesky_upper(safe)
     upper = jnp.where(live[:, None, None], upper, jnp.zeros_like(upper))
     column_start = lax.axis_index("cols") * slab_width
     return lax.dynamic_slice_in_dim(upper, column_start, slab_width, 1)

time: 144 us -> 126 us (0.88)
  other arithmetic: 55.9 us -> 9.66 us
  Pallas kernels: 0 us -> 27.3 us
    another operation x4 -> x0, other arithmetic: 47.2 us -> none  [per_device(): upper = jnp.swapaxes(jnp.linalg.cholesky(safe), -1, -2)]
    pallas_call x0 -> x1, Pallas kernels: none -> 27.3 us  [cholesky_upper(): pl.pallas_call(cholesky_kernel, out_shape=jax.ShapeDtypeStruct(gram.shape...]
    select_n x0 -> x1, other arithmetic: none -> 1.64 us  [per_device(): upper = jnp.where(live[:, None, None], upper, jnp.zeros_like(upper))]
  transfers between devices with their start and end apart: 2 -> 2, of which waited for: 2 -> 2; matrix products, arithmetic and copies ran while one was open for 5% -> 6% of each run, Pallas kernels for 0% -> 0%
where the time goes in v2:
time: 126 us; the launch traced here: 125 us
  waiting for transfers between devices  35.2 us (28%)
  Pallas kernels  27.3 us (22%)
  starting transfers between devices  22.9 us (18%)
  local copies, waits for them, and re-layouts  19.1 us (15%)
  other arithmetic  9.66 us (8%)
  matrix products  5.58 us (4%)
  blocking collectives  5.37 us (4%)
    pallas_call x1, Pallas kernels, cholesky_upper(): pl.pallas_call(cholesky_kernel, out_shape=jax.ShapeDtypeStruct(gram.shape...  27.3 us
    all_to_all x1, waiting for transfers between devices, per_device(): lax.all_to_all(outgoing, 'rows', split_axis=0, concat_axis=0, tiled=True)  23.5 us
    all_to_all x1, starting transfers between devices, per_device(): lax.all_to_all(outgoing, 'rows', split_axis=0, concat_axis=0, tiled=True)  16.5 us
    all_to_all x1, waiting for transfers between devices, per_device(): lax.all_to_all(bundled, 'rows', split_axis=0, concat_axis=0, tiled=True)  11.8 us
    all_to_all x1, starting transfers between devices, per_device(): lax.all_to_all(bundled, 'rows', split_axis=0, concat_axis=0, tiled=True)  6.39 us
    all_gather x1, blocking collectives, per_device(): whole_rows = lax.all_gather(received_rows, 'cols', axis=2, tiled=True)  5.37 us
    gather x7, local copies, waits for them, and re-layouts, per_device(): sample_values = jnp.take_along_axis(samples, picks, axis=1)  5.23 us
    unnamed x9, local copies, waits for them, and re-layouts  4.68 us
  transfers between devices with their start and end apart: 2, of which 2 were waited for; matrix products, arithmetic and copies ran while one was open for 6% of the time, Pallas kernels for 0%

profile of v2, /device:TPU:1, one launch (start us, length us, event | category | flops | bytes accessed | tf_op | source)
XLA Modules:
  0.0 125.3 jit_solution(10100518928789685982)
XLA Ops:
  0.0 0.0 copy-start
  0.0 0.8 subtract_convert_fusion
  0.8 1.1 multiply_bitcast_fusion.1
  1.9 0.1 copy.71
  2.0 2.8 %multiply_bitcast_fusion = f32[32,4,32,64]{2,0,1,3:T(8,128)} fusion(bf16[64,32,128,1]{2,1,0,3:T(8,128)(2,1)S(1)} %bitcast.46, s32[4,32]{1,0:T(4,128)S(1)} %multiply_add_fusion), kind=kOutput, calls=%fused_computation.2 | convolution fusion | flops 67960832 | bytes 1573376 | tf_op jit(solution)/shard_map/huj,cbj->bhuc/dot_general | solution.py:76
  4.7 3.8 %copy.58 = f32[32,4,32,64]{3,2,1,0:T(8,128)S(1)} copy(f32[32,4,32,64]{2,0,1,3:T(8,128)} %multiply_bitcast_fusion) | data formatting | bytes 2097152 | tf_op jit(solution)/shard_map/mul | solution.py:82
  8.5 2.3 %reshape.464 = f32[128,1,2048]{2,1,0:T(1,128)} reshape(f32[128,32,64]{2,1,0:T(8,128)S(1)} %bitcast.42) | data formatting | bytes 2097152
  10.8 16.5 %all-to-all-start = ((f32[128,1,2048]{2,1,0:T(1,128)}), f32[128,1,2048]{2,1,0:T(1,128)S(1)}, u32[]{:S(2)}, u32[]{:S(2)}) async-start(f32[128,1,2048]{2,1,0:T(1,128)} %reshape.464), calls=%async_computation | async-start | bytes 2097152 | tf_op jit(solution)/shard_map/all_to_all | solution.py:83
  27.4 0.1 copy.56
  27.5 0.1 reshape.449
  27.6 0.0 copy-done
  27.7 0.0 copy-start.1
  27.7 4.5 %gather_fusion.1 = s32[512]{0:T(512)S(1)} fusion(s32[256,256]{1,0:T(8,128)S(1)} %copy-done, s32[512]{0:T(512)S(1)} %reshape.449), kind=kCustom, calls=%fused_computation.1 | custom fusion | bytes 8192 | tf_op jit(solution)/shard_map/jit(take_along_axis)/gather | solution.py:93
  32.2 0.1 gather.11
  32.3 0.1 reshape.452
  32.5 0.1 copy.61
  32.6 0.1 copy.62
  32.7 0.1 reshape.443
  32.9 0.1 copy.57
  33.0 0.0 copy-done.1
  33.0 0.2 convert_reduce_fusion
  33.2 0.7 fusion.39
  33.9 23.5 %all-to-all-done = f32[128,1,2048]{2,1,0:T(1,128)S(1)} async-done(((f32[128,1,2048]{2,1,0:T(1,128)}), f32[128,1,2048]{2,1,0:T(1,128)S(1)}, u32[]{:S(2)}, u32[]{:S(2)}) %all-to-all-start) | async-done | bytes 1048608 | tf_op jit(solution)/shard_map/all_to_all | solution.py:83
  57.4 0.5 broadcast.1008
  57.9 3.2 %reduce = f32[128,2048]{1,0:T(8,128)S(1)} reduce(f32[128,1,2048]{2,1,0:T(1,128)S(1)} %all-to-all-done, f32[]{:T(128)} %broadcast.1008), dimensions={1}, to_apply=%all_to_all.6.reduce_sub_computation | reduce | bytes 2097156 | tf_op jit(solution)/shard_map/all_to_all | solution.py:83
  61.1 0.8 reshape.465
  62.0 1.3 %copy.59 = f32[128,32,64]{0,2,1:T(8,128)S(1)} copy(f32[128,32,64]{2,1,0:T(8,128)S(1)} %reshape.465) | data formatting | bytes 2097152 | tf_op jit(solution)/shard_map/all_to_all | solution.py:83
  63.2 1.1 fusion.9
  64.3 1.7 %copy.60 = f32[128,32,64]{2,1,0:T(8,128)S(1)} copy(f32[128,32,64]{0,2,1:T(8,128)S(1)} %bitcast.45) | data formatting | bytes 2097152 | tf_op jit(solution)/shard_map/st,tuc->suc/dot_general | solution.py:85
  66.0 1.0 gather_fusion
  67.0 0.1 copy.63
  67.2 0.4 fusion.2
  67.6 0.2 copy.64
  67.8 0.1 copy.73
  67.9 1.2 reshape.466
  69.1 6.4 %all-to-all-start.1 = ((f32[128,1,512]{2,1,0:T(1,128)}), f32[128,1,512]{2,1,0:T(1,128)S(1)}, u32[]{:S(2)}, u32[]{:S(2)}) async-start(f32[128,1,512]{2,1,0:T(1,128)} %reshape.466), calls=%async_computation.1 | async-start | bytes 524288 | tf_op jit(solution)/shard_map/all_to_all | solution.py:109
  75.5 0.7 iota_compare_fusion.4
  76.2 11.8 %all-to-all-done.1 = f32[128,1,512]{2,1,0:T(1,128)S(1)} async-done(((f32[128,1,512]{2,1,0:T(1,128)}), f32[128,1,512]{2,1,0:T(1,128)S(1)}, u32[]{:S(2)}, u32[]{:S(2)}) %all-to-all-start.1) | async-done | bytes 262176 | tf_op jit(solution)/shard_map/all_to_all | solution.py:109
  88.0 1.3 %reduce.1 = f32[128,512]{1,0:T(8,128)S(1)} reduce(f32[128,1,512]{2,1,0:T(1,128)S(1)} %all-to-all-done.1, f32[]{:T(128)} %broadcast.1008), dimensions={1}, to_apply=%all_to_all.7.reduce_sub_computation | reduce | bytes 524292 | tf_op jit(solution)/shard_map/all_to_all | solution.py:109
  89.3 0.3 reshape.467
  89.5 0.2 copy.67
  89.8 5.4 %all_gather.3 = f32[4,256,128]{1,2,0:T(8,128)S(1)} all-gather(f32[4,256,64]{1,2,0:T(8,128)S(1)} %copy.67), channel_id=1, replica_groups=mesh['rows'=128,'cols'=2] {'cols'}, dimensions={2}, use_global_device_ids=true | all-gather | bytes 786432 | tf_op jit(solution)/shard_map/all_gather | solution.py:111
  95.1 1.3 %fusion.gram_ref = f32[4,128,128]{2,1,0:T(8,128)} fusion(f32[4,256,128]{1,2,0:T(8,128)S(1)} %all_gather.3, f32[128,128]{1,0:T(8,128)S(1)} %fusion.16, pred[4]{0:T(512)(128)(4,1)S(1)} %iota_compare_fusion.4), kind=kOutput, calls=%fused_computation.4 | convolution fusion | flops 201457664 | bytes 851972 | tf_op jit(solution)/shard_map/sqi,sqk->sik/dot_general | solution.py:114
  96.4 27.3 %shard_map.46 = f32[4,128,128]{2,1,0:T(8,128)} custom-call(f32[4,128,128]{2,1,0:T(8,128)} %fusion.gram_ref), custom_call_target="tpu_custom_call" | custom-call | tf_op jit(solution)/shard_map/pallas_call | solution.py:48
  123.7 1.6 %dynamic-slice_select_fusion = f32[4,64,128]{2,1,0:T(8,128)} fusion(f32[4,128,128]{2,1,0:T(8,128)} %shard_map.46, s32[]{:T(128)S(6)} %select_n.180, pred[4]{0:T(512)(128)(4,1)S(1)} %iota_compare_fusion.4), kind=kLoop, calls=%fused_computation.13 | loop fusion | flops 32768 | bytes 262152 | tf_op jit(solution)/shard_map/jit(_where)/select_n | solution.py:122
  (9 shorter events, 0.1 us)
Async XLA Ops:
  0.0 27.6 %copy-start = (s32[256,256]{1,0:T(8,128)S(1)}, s32[256,256]{1,0:T(8,128)}, u32[]{:S(2)}) copy-start(s32[256,256]{1,0:T(8,128)} %param.6) | copy-start | bytes 786436
  10.8 46.6 %all-to-all-start = ((f32[128,1,2048]{2,1,0:T(1,128)}), f32[128,1,2048]{2,1,0:T(1,128)S(1)}, u32[]{:S(2)}, u32[]{:S(2)}) async-start(f32[128,1,2048]{2,1,0:T(1,128)} %reshape.464), calls=%async_computation | async-start | bytes 2097152 | tf_op jit(solution)/shard_map/all_to_all | solution.py:83
  27.7 5.4 %copy-start.1 = (s32[256,1]{0,1:T(1,128)S(1)}, s32[256,1]{0,1:T(1,128)}, u32[]{:S(2)}) copy-start(s32[256,1]{0,1:T(1,128)} %param.7) | copy-start | bytes 3076
  69.1 18.9 %all-to-all-start.1 = ((f32[128,1,512]{2,1,0:T(1,128)}), f32[128,1,512]{2,1,0:T(1,128)S(1)}, u32[]{:S(2)}, u32[]{:S(2)}) async-start(f32[128,1,512]{2,1,0:T(1,128)} %reshape.466), calls=%async_computation.1 | async-start | bytes 524288 | tf_op jit(solution)/shard_map/all_to_all | solution.py:109

commit v3 on v2

--- a/solution.py
+++ b/solution.py
@@ -11,28 +11,27 @@
 SKETCH_ROW_COUNT = 256
 CAPB = 4
 
-PANEL = 8
+PANEL = 32
 
 
 def cholesky_kernel(gram_ref, out_ref, work_ref):
     blocks, order, _ = gram_ref.shape
     work_ref[...] = gram_ref[...]
     lane = lax.broadcasted_iota(jnp.int32, (blocks, 1, order), 2)
-    lane_panel = lax.broadcasted_iota(jnp.int32, (blocks, PANEL, order), 2)
     sub_panel = lax.broadcasted_iota(jnp.int32, (blocks, PANEL, order), 1)
+    sub_col = lax.broadcasted_iota(jnp.int32, (blocks, PANEL, 1), 1)
     for p in range(order // PANEL):
         base = p * PANEL
         panel = work_ref[:, base:base + PANEL, :]
         for jj in range(PANEL):
             j = base + jj
             row = panel[:, jj:jj + 1, :]
-            pivot = row[:, :, j:j + 1]
-            r = jnp.where(lane >= j, row / jnp.sqrt(pivot), 0.0)
-            spread = jnp.broadcast_to(r, (blocks, PANEL, order))
-            col = jnp.sum(jnp.where(lane_panel == base + sub_panel, spread, 0.0), axis=2, keepdims=True)
-            col = jnp.where(sub_panel[:, :, :1] > jj, col, 0.0)
-            panel = panel - col * spread
-            panel = jnp.where(sub_panel == jj, spread, panel)
+            column = panel[:, :, j:j + 1]
+            inverse_root = lax.rsqrt(column[:, jj:jj + 1, :])
+            factor_row = jnp.where(lane >= j, row * inverse_root, 0.0)
+            factor_column = jnp.where(sub_col > jj, column * inverse_root, 0.0)
+            panel = panel - factor_column * factor_row
+            panel = jnp.where(sub_panel == jj, factor_row, panel)
         out_ref[:, base:base + PANEL, :] = panel
         if p + 1 < order // PANEL:
             for b in range(blocks):
@@ -79,8 +78,9 @@
         flipped.reshape(slab_width, shard_rows // HB, HB),
         preferred_element_type=jnp.float32,
     )
-    outgoing = local_mix.reshape(row_devices, sub_rows, slab_width) * scale
+    outgoing = local_mix.reshape(row_devices, sub_rows * slab_width // 128, 128) * scale
     received = lax.all_to_all(outgoing, "rows", split_axis=0, concat_axis=0, tiled=True)
+    received = received.reshape(row_devices, sub_rows, slab_width)
     across = walsh_sign_matrix(row_devices)
     mixed = jnp.einsum(
         "st,tuc->suc", across, received, precision=lax.Precision.HIGHEST

time: 126 us -> 106 us (0.84)
  Pallas kernels: 27.3 us -> 13.8 us
  other arithmetic: 9.66 us -> 6.36 us
  local copies, waits for them, and re-layouts: 19.1 us -> 16.4 us
    pallas_call x1, Pallas kernels: 27.3 us -> 13.8 us  [cholesky_upper(): pl.pallas_call(cholesky_kernel, out_shape=jax.ShapeDtypeStruct(gram.shape...]
    all_to_all x1 -> x0, other arithmetic: 3.18 us -> none  [per_device(): lax.all_to_all(outgoing, 'rows', split_axis=0, concat_axis=0, tiled=True)]
    unnamed x9 -> x7, local copies, waits for them, and re-layouts: 4.68 us -> 1.56 us
    all_to_all x2 -> x1, local copies, waits for them, and re-layouts: 1.79 us -> 0.42 us  [per_device(): lax.all_to_all(outgoing, 'rows', split_axis=0, concat_axis=0, tiled=True)]
    mul x1 -> x2, local copies, waits for them, and re-layouts: 3.79 us -> 5.13 us  [per_device(): local_mix.reshape(row_devices, sub_rows * slab_width // 128, 128) * scale]
  transfers between devices with their start and end apart: 2 -> 2, of which waited for: 2 -> 2; matrix products, arithmetic and copies ran while one was open for 6% -> 7% of each run, Pallas kernels for 0% -> 0%
where the time goes in v3:
time: 106 us
  waiting for transfers between devices  35.6 us (34%)
  starting transfers between devices  22.7 us (21%)
  local copies, waits for them, and re-layouts  16.4 us (15%)
  Pallas kernels  13.8 us (13%)
  other arithmetic  6.36 us (6%)
  matrix products  5.56 us (5%)
  blocking collectives  5.37 us (5%)
    all_to_all x1, waiting for transfers between devices, per_device(): lax.all_to_all(outgoing, 'rows', split_axis=0, concat_axis=0, tiled=True)  23.7 us
    all_to_all x1, starting transfers between devices, per_device(): lax.all_to_all(outgoing, 'rows', split_axis=0, concat_axis=0, tiled=True)  16.3 us
    pallas_call x1, Pallas kernels, cholesky_upper(): pl.pallas_call(cholesky_kernel, out_shape=jax.ShapeDtypeStruct(gram.shape...  13.8 us
    all_to_all x1, waiting for transfers between devices, per_device(): lax.all_to_all(bundled, 'rows', split_axis=0, concat_axis=0, tiled=True)  11.8 us
    all_to_all x1, starting transfers between devices, per_device(): lax.all_to_all(bundled, 'rows', split_axis=0, concat_axis=0, tiled=True)  6.34 us
    all_gather x1, blocking collectives, per_device(): whole_rows = lax.all_gather(received_rows, 'cols', axis=2, tiled=True)  5.37 us
    gather x7, local copies, waits for them, and re-layouts, per_device(): sample_values = jnp.take_along_axis(samples, picks, axis=1)  5.23 us
    mul x2, local copies, waits for them, and re-layouts, per_device(): local_mix.reshape(row_devices, sub_rows * slab_width // 128, 128) * scale  5.13 us
  transfers between devices with their start and end apart: 2, of which 2 were waited for; matrix products, arithmetic and copies ran while one was open for 7% of the time, Pallas kernels for 0%

profile of v3, /device:TPU:1, one launch (start us, length us, event | category | flops | bytes accessed | tf_op | source)
XLA Modules:
  0.0 106.0 jit_solution(13187961110653008905)
XLA Ops:
  0.0 0.0 copy-start
  0.0 0.8 subtract_convert_fusion
  0.8 1.1 %multiply_bitcast_fusion.1 = bf16[8,8,32,128]{3,1,2,0:T(8,128)(2,1)S(1)} fusion(bf16[64,4096]{1,0:T(8,128)(2,1)} %param.4, bf16[4096]{0:T(1024)(128)(2,1)S(1)} %subtract_convert_fusion), kind=kLoop, calls=%fused_computation.6 | loop fusion | flops 262144 | bytes 1056768
  1.9 0.1 copy.71
  2.0 2.8 %multiply_bitcast_fusion = f32[32,4,32,64]{2,0,1,3:T(8,128)} fusion(bf16[64,32,128,1]{2,1,0,3:T(8,128)(2,1)S(1)} %bitcast.48, s32[4,32]{1,0:T(4,128)S(1)} %multiply_add_fusion), kind=kOutput, calls=%fused_computation.2 | convolution fusion | flops 67960832 | bytes 1573376 | tf_op jit(solution)/shard_map/huj,cbj->bhuc/dot_general | solution.py:75
  4.7 3.8 %copy.58 = f32[32,4,32,64]{3,2,1,0:T(8,128)S(1)} copy(f32[32,4,32,64]{2,0,1,3:T(8,128)} %multiply_bitcast_fusion) | data formatting | bytes 2097152 | tf_op jit(solution)/shard_map/mul | solution.py:81
  8.5 1.3 %mul.116 = f32[128,16,128]{2,1,0:T(8,128)} reshape(f32[32,4,32,64]{3,2,1,0:T(8,128)S(1)} %copy.58) | data formatting | bytes 2097152 | tf_op jit(solution)/shard_map/mul | solution.py:81
  9.9 16.3 %all-to-all-start = ((f32[128,16,128]{2,1,0:T(8,128)}), f32[128,16,128]{2,1,0:T(8,128)S(1)}, u32[]{:S(2)}, u32[]{:S(2)}) async-start(f32[128,16,128]{2,1,0:T(8,128)} %mul.116), calls=%async_computation | async-start | bytes 2097152 | tf_op jit(solution)/shard_map/all_to_all | solution.py:82
  26.2 0.1 copy.56
  26.4 0.1 reshape.453
  26.5 0.0 copy-done
  26.5 0.0 copy-start.1
  26.5 4.5 %gather_fusion.1 = s32[512]{0:T(512)S(1)} fusion(s32[256,256]{1,0:T(8,128)S(1)} %copy-done, s32[512]{0:T(512)S(1)} %reshape.453), kind=kCustom, calls=%fused_computation.1 | custom fusion | bytes 8192 | tf_op jit(solution)/shard_map/jit(take_along_axis)/gather | solution.py:93
  31.1 0.1 gather.11
  31.2 0.1 reshape.456
  31.4 0.1 copy.61
  31.5 0.1 copy.62
  31.6 0.1 reshape.447
  31.8 0.1 copy.57
  31.9 0.0 copy-done.1
  31.9 0.2 convert_reduce_fusion
  32.1 0.6 fusion.39
  32.7 23.7 %all-to-all-done = f32[128,16,128]{2,1,0:T(8,128)S(1)} async-done(((f32[128,16,128]{2,1,0:T(8,128)}), f32[128,16,128]{2,1,0:T(8,128)S(1)}, u32[]{:S(2)}, u32[]{:S(2)}) %all-to-all-start) | async-done | bytes 1048608 | tf_op jit(solution)/shard_map/all_to_all | solution.py:82
  56.5 0.4 copy.59
  56.9 1.1 fusion.9
  58.0 1.7 %copy.60 = f32[128,32,64]{2,1,0:T(8,128)S(1)} copy(f32[128,32,64]{0,2,1:T(8,128)S(1)} %bitcast.46) | data formatting | bytes 2097152 | tf_op jit(solution)/shard_map/st,tuc->suc/dot_general | solution.py:85
  59.6 1.0 gather_fusion
  60.7 0.1 copy.63
  60.8 0.4 fusion.2
  61.3 0.2 copy.64
  61.5 0.1 copy.73
  61.6 1.2 %reshape.468 = f32[128,1,512]{2,1,0:T(1,128)} reshape(f32[128,2,4,64]{3,2,1,0:T(4,128)S(1)} %bitcast.51) | data formatting | bytes 524288
  62.7 6.3 %all-to-all-start.1 = ((f32[128,1,512]{2,1,0:T(1,128)}), f32[128,1,512]{2,1,0:T(1,128)S(1)}, u32[]{:S(2)}, u32[]{:S(2)}) async-start(f32[128,1,512]{2,1,0:T(1,128)} %reshape.468), calls=%async_computation.1 | async-start | bytes 524288 | tf_op jit(solution)/shard_map/all_to_all | solution.py:109
  69.1 0.7 iota_compare_fusion.4
  69.8 11.8 %all-to-all-done.1 = f32[128,1,512]{2,1,0:T(1,128)S(1)} async-done(((f32[128,1,512]{2,1,0:T(1,128)}), f32[128,1,512]{2,1,0:T(1,128)S(1)}, u32[]{:S(2)}, u32[]{:S(2)}) %all-to-all-start.1) | async-done | bytes 262176 | tf_op jit(solution)/shard_map/all_to_all | solution.py:109
  81.6 0.5 broadcast.1008
  82.1 1.3 %reduce = f32[128,512]{1,0:T(8,128)S(1)} reduce(f32[128,1,512]{2,1,0:T(1,128)S(1)} %all-to-all-done.1, f32[]{:T(128)} %broadcast.1008), dimensions={1}, to_apply=%all_to_all.7.reduce_sub_computation | reduce | bytes 524292 | tf_op jit(solution)/shard_map/all_to_all | solution.py:109
  83.4 0.3 reshape.469
  83.7 0.2 copy.67
  83.9 5.4 %all_gather.3 = f32[4,256,128]{1,2,0:T(8,128)S(1)} all-gather(f32[4,256,64]{1,2,0:T(8,128)S(1)} %copy.67), channel_id=1, replica_groups=mesh['rows'=128,'cols'=2] {'cols'}, dimensions={2}, use_global_device_ids=true | all-gather | bytes 786432 | tf_op jit(solution)/shard_map/all_gather | solution.py:111
  89.3 1.3 %fusion.gram_ref = f32[4,128,128]{2,1,0:T(8,128)} fusion(f32[4,256,128]{1,2,0:T(8,128)S(1)} %all_gather.3, f32[128,128]{1,0:T(8,128)S(1)} %fusion.16, pred[4]{0:T(512)(128)(4,1)S(1)} %iota_compare_fusion.4), kind=kOutput, calls=%fused_computation.4 | convolution fusion | flops 201457664 | bytes 851972 | tf_op jit(solution)/shard_map/sqi,sqk->sik/dot_general | solution.py:114
  90.6 13.8 %shard_map.46 = f32[4,128,128]{2,1,0:T(8,128)} custom-call(f32[4,128,128]{2,1,0:T(8,128)} %fusion.gram_ref), custom_call_target="tpu_custom_call" | custom-call | tf_op jit(solution)/shard_map/pallas_call | solution.py:47
  104.4 1.6 %dynamic-slice_select_fusion = f32[4,64,128]{2,1,0:T(8,128)} fusion(f32[4,128,128]{2,1,0:T(8,128)} %shard_map.46, s32[]{:T(128)S(6)} %select_n.180, pred[4]{0:T(512)(128)(4,1)S(1)} %iota_compare_fusion.4), kind=kLoop, calls=%fused_computation.13 | loop fusion | flops 32768 | bytes 262152 | tf_op jit(solution)/shard_map/jit(_where)/select_n | solution.py:122
  (9 shorter events, 0.1 us)
Async XLA Ops:
  0.0 26.5 %copy-start = (s32[256,256]{1,0:T(8,128)S(1)}, s32[256,256]{1,0:T(8,128)}, u32[]{:S(2)}) copy-start(s32[256,256]{1,0:T(8,128)} %param.6) | copy-start | bytes 786436
  9.9 46.6 %all-to-all-start = ((f32[128,16,128]{2,1,0:T(8,128)}), f32[128,16,128]{2,1,0:T(8,128)S(1)}, u32[]{:S(2)}, u32[]{:S(2)}) async-start(f32[128,16,128]{2,1,0:T(8,128)} %mul.116), calls=%async_computation | async-start | bytes 2097152 | tf_op jit(solution)/shard_map/all_to_all | solution.py:82
  26.5 5.4 %copy-start.1 = (s32[256,1]{0,1:T(1,128)S(1)}, s32[256,1]{0,1:T(1,128)}, u32[]{:S(2)}) copy-start(s32[256,1]{0,1:T(1,128)} %param.7) | copy-start | bytes 3076
  62.7 18.9 %all-to-all-start.1 = ((f32[128,1,512]{2,1,0:T(1,128)}), f32[128,1,512]{2,1,0:T(1,128)S(1)}, u32[]{:S(2)}, u32[]{:S(2)}) async-start(f32[128,1,512]{2,1,0:T(1,128)} %reshape.468), calls=%async_computation.1 | async-start | bytes 524288 | tf_op jit(solution)/shard_map/all_to_all | solution.py:109

commit v4 on v3

--- a/solution.py
+++ b/solution.py
@@ -53,6 +53,39 @@
     )(gram)
 
 
+def local_mix_kernel(matrix_ref, flips_ref, table_ref, out_ref):
+    slab_width = matrix_ref.shape[0]
+    groups = table_ref.shape[1] // out_ref.shape[1]
+
+    def body(blk, carry):
+        start = pl.multiple_of(blk * HB, HB)
+        flipped = matrix_ref[:, pl.ds(start, HB)] * flips_ref[:, pl.ds(start, HB)]
+        for parity in range(2):
+            mixed = lax.dot_general(
+                table_ref[parity], flipped, (((1,), (1,)), ((), ())),
+                preferred_element_type=jnp.float32,
+            )
+            for h in range(groups):
+                rows = out_ref.shape[1]
+                out_ref[blk * groups + h, :, parity * slab_width:(parity + 1) * slab_width] = (
+                    mixed[h * rows:(h + 1) * rows, :]
+                )
+        return carry
+
+    lax.fori_loop(0, matrix_ref.shape[1] // HB, body, 0)
+
+
+def local_mix(matrix, flips, table, row_devices):
+    slab_width, shard_rows = matrix.shape
+    sub_rows = shard_rows // row_devices
+    return pl.pallas_call(
+        local_mix_kernel,
+        out_shape=jax.ShapeDtypeStruct((row_devices, sub_rows // 2, 2 * slab_width), jnp.float32),
+        in_specs=[pl.BlockSpec(memory_space=pltpu.VMEM)] * 3,
+        out_specs=pl.BlockSpec(memory_space=pltpu.VMEM),
+    )(matrix, flips, table)
+
+
 def walsh_sign_matrix(order):
     index_row = jnp.arange(order, dtype=jnp.int32)
     parity = jnp.zeros((order, order), jnp.int32)
@@ -68,23 +101,16 @@
     row_devices = lax.axis_size("rows")
     processor_number = lax.axis_index("rows")
     sub_rows = shard_rows // row_devices
-    flips = (1 - 2 * signs).astype(jnp.bfloat16)
-    flipped = matrix * flips[None, :]
-    table = walsh_sign_matrix(HB).astype(jnp.bfloat16)
+    flips = (1 - 2 * signs).astype(jnp.bfloat16).reshape(1, shard_rows)
     scale = 1.0 / math.sqrt(HB * row_devices)
-    local_mix = jnp.einsum(
-        "huj,cbj->bhuc",
-        table.reshape(HB // sub_rows, sub_rows, HB),
-        flipped.reshape(slab_width, shard_rows // HB, HB),
-        preferred_element_type=jnp.float32,
-    )
-    outgoing = local_mix.reshape(row_devices, sub_rows * slab_width // 128, 128) * scale
+    table = (walsh_sign_matrix(HB) * scale).astype(jnp.bfloat16)
+    table = table.reshape(HB // 2, 2, HB).transpose(1, 0, 2)
+    outgoing = local_mix(matrix, flips, table, row_devices)
     received = lax.all_to_all(outgoing, "rows", split_axis=0, concat_axis=0, tiled=True)
-    received = received.reshape(row_devices, sub_rows, slab_width)
     across = walsh_sign_matrix(row_devices)
     mixed = jnp.einsum(
-        "st,tuc->suc", across, received, precision=lax.Precision.HIGHEST
-    ).reshape(row_devices * sub_rows, slab_width)
+        "st,tvl->svl", across, received, precision=lax.Precision.HIGHEST
+    ).reshape(row_devices * sub_rows // 2, 2 * slab_width)
 
     block_total = samples.shape[0]
     block_ids = jnp.arange(block_total, dtype=jnp.int32)
@@ -93,7 +119,10 @@
     sample_values = jnp.take_along_axis(samples, picks, axis=1)
     shard_of = picks // (samples.shape[1] // row_devices)
     offsets = sample_values - shard_of * shard_rows - processor_number * sub_rows
-    chosen = jnp.take(mixed, shard_of * sub_rows + offsets, axis=0)
+    both_halves = jnp.take(mixed, shard_of * (sub_rows // 2) + offsets // 2, axis=0)
+    chosen = jnp.where(
+        (offsets % 2 == 1)[:, :, None], both_halves[:, :, slab_width:], both_halves[:, :, :slab_width]
+    )
 
     owner_list = owners[:, 0]
     preceding_rows = jnp.logical_and(

time: 106 us -> 107 us (level)
  Pallas kernels: 13.8 us -> 22.6 us
  local copies, waits for them, and re-layouts: 16.4 us -> 11 us
  matrix products: 5.56 us -> 3.02 us
    pallas_call x0 -> x1, Pallas kernels: none -> 8.86 us  [local_mix(): pl.pallas_call(local_mix_kernel, out_shape=jax.ShapeDtypeStruct((row_devi...]
    mul x2 -> x0, local copies, waits for them, and re-layouts: 5.13 us -> none  [per_device(): local_mix.reshape(row_devices, sub_rows * slab_width // 128, 128) * scale]
    dot_general x1, matrix products: 2.77 us -> 1.29 us  [per_device(): jnp.einsum('st,tvl->svl', across, received, precision=lax.Precision.HIGHEST)]
    unnamed x1 -> x0, other arithmetic: 1.08 us -> none
where the time goes in v4:
time: 107 us; the launch traced here: 106 us
  waiting for transfers between devices  35.1 us (33%)
  Pallas kernels  22.6 us (21%)
  starting transfers between devices  22.5 us (21%)
  local copies, waits for them, and re-layouts  11 us (10%)
  other arithmetic  6.1 us (6%)
  blocking collectives  5.55 us (5%)
  matrix products  3.02 us (3%)
    all_to_all x1, waiting for transfers between devices, per_device(): lax.all_to_all(outgoing, 'rows', split_axis=0, concat_axis=0, tiled=True)  23.1 us
    all_to_all x1, starting transfers between devices, per_device(): lax.all_to_all(outgoing, 'rows', split_axis=0, concat_axis=0, tiled=True)  16.3 us
    pallas_call x1, Pallas kernels, cholesky_upper(): pl.pallas_call(cholesky_kernel, out_shape=jax.ShapeDtypeStruct(gram.shape...  13.8 us
    all_to_all x1, waiting for transfers between devices, per_device(): lax.all_to_all(bundled, 'rows', split_axis=0, concat_axis=0, tiled=True)  12 us
    pallas_call x1, Pallas kernels, local_mix(): pl.pallas_call(local_mix_kernel, out_shape=jax.ShapeDtypeStruct((row_devi...  8.86 us
    all_to_all x1, starting transfers between devices, per_device(): lax.all_to_all(bundled, 'rows', split_axis=0, concat_axis=0, tiled=True)  6.14 us
    all_gather x1, blocking collectives, per_device(): whole_rows = lax.all_gather(received_rows, 'cols', axis=2, tiled=True)  5.55 us
    gather x7, local copies, waits for them, and re-layouts, per_device(): sample_values = jnp.take_along_axis(samples, picks, axis=1)  5.23 us
  transfers between devices with their start and end apart: 2, of which 2 were waited for; matrix products, arithmetic and copies ran while one was open for 7% of the time, Pallas kernels for 0%

profile of v4, /device:TPU:1, one launch (start us, length us, event | category | flops | bytes accessed | tf_op | source)
XLA Modules:
  0.0 106.1 jit_solution(11705839899096275898)
XLA Ops:
  0.0 0.0 copy-start
  0.0 0.8 subtract_convert_fusion
  0.8 0.6 reshape.413.flips_ref
  1.4 0.8 fusion.17.table_ref
  2.2 8.9 %shard_map.46 = f32[128,16,128]{2,1,0:T(8,128)} custom-call(bf16[64,4096]{1,0:T(8,128)(2,1)} %matrix_ref.1, bf16[1,4096]{1,0:T(2,128)(2,1)} %reshape.413.flips_ref, bf16[2,64,128]{2,1,0:T(8,128)(2,1)} %fusion.17.table_ref), custom_call_target="tpu_custom_call" | custom-call | tf_op jit(solution)/shard_map/pallas_call | solution.py:81
  11.0 16.3 %all-to-all-start = ((f32[128,16,128]{2,1,0:T(8,128)}), f32[128,16,128]{2,1,0:T(8,128)S(1)}, u32[]{:S(2)}, u32[]{:S(2)}) async-start(f32[128,16,128]{2,1,0:T(8,128)} %shard_map.46), calls=%async_computation | async-start | bytes 2097152 | tf_op jit(solution)/shard_map/all_to_all | solution.py:109
  27.4 0.1 copy.57
  27.5 0.1 reshape.425
  27.7 0.0 copy-done
  27.7 4.5 %gather_fusion.1 = s32[512]{0:T(512)S(1)} fusion(s32[256,256]{1,0:T(8,128)S(1)} %copy-done, s32[512]{0:T(512)S(1)} %reshape.425), kind=kCustom, calls=%fused_computation.1 | custom fusion | bytes 8192 | tf_op jit(solution)/shard_map/jit(take_along_axis)/gather | solution.py:119
  32.2 0.1 gather.11
  32.4 0.1 reshape.428
  32.5 0.1 copy.61
  32.6 0.1 copy.62
  32.8 0.1 reshape.419
  32.9 0.1 copy.58
  33.1 0.0 copy-start.1
  33.1 0.7 copy-done.1
  33.7 0.2 convert_reduce_fusion
  33.9 0.6 fusion.34
  34.6 23.1 %all-to-all-done = f32[128,16,128]{2,1,0:T(8,128)S(1)} async-done(((f32[128,16,128]{2,1,0:T(8,128)}), f32[128,16,128]{2,1,0:T(8,128)S(1)}, u32[]{:S(2)}, u32[]{:S(2)}) %all-to-all-start) | async-done | bytes 1048608 | tf_op jit(solution)/shard_map/all_to_all | solution.py:109
  57.7 1.3 %fusion.1 = f32[128,16,128]{2,0,1:T(8,128)S(1)} fusion(f32[128,16,128]{2,1,0:T(8,128)S(1)} %all-to-all-done), kind=kOutput, calls=%fused_computation.4 | convolution fusion | flops 403226624 | bytes 2097152 | tf_op jit(solution)/shard_map/st,tvl->svl/dot_general | solution.py:111
  59.0 0.6 copy.60
  59.6 1.0 gather_fusion
  60.6 0.1 copy.63
  60.8 0.4 fusion.3
  61.2 0.2 copy.64
  61.4 0.1 copy.73
  61.5 1.2 %reshape.436 = f32[128,1,512]{2,1,0:T(1,128)} reshape(f32[128,2,4,64]{3,2,1,0:T(4,128)S(1)} %bitcast.30) | data formatting | bytes 524288
  62.7 6.1 %all-to-all-start.1 = ((f32[128,1,512]{2,1,0:T(1,128)}), f32[128,1,512]{2,1,0:T(1,128)S(1)}, u32[]{:S(2)}, u32[]{:S(2)}) async-start(f32[128,1,512]{2,1,0:T(1,128)} %reshape.436), calls=%async_computation.1 | async-start | bytes 524288 | tf_op jit(solution)/shard_map/all_to_all | solution.py:138
  68.9 0.7 iota_compare_fusion.4
  69.6 12.0 %all-to-all-done.1 = f32[128,1,512]{2,1,0:T(1,128)S(1)} async-done(((f32[128,1,512]{2,1,0:T(1,128)}), f32[128,1,512]{2,1,0:T(1,128)S(1)}, u32[]{:S(2)}, u32[]{:S(2)}) %all-to-all-start.1) | async-done | bytes 262176 | tf_op jit(solution)/shard_map/all_to_all | solution.py:138
  81.6 0.5 broadcast.834
  82.1 1.3 %reduce = f32[128,512]{1,0:T(8,128)S(1)} reduce(f32[128,1,512]{2,1,0:T(1,128)S(1)} %all-to-all-done.1, f32[]{:T(128)} %broadcast.834), dimensions={1}, to_apply=%all_to_all.7.reduce_sub_computation | reduce | bytes 524292 | tf_op jit(solution)/shard_map/all_to_all | solution.py:138
  83.4 0.3 reshape.437
  83.6 0.2 copy.67
  83.8 5.5 %all_gather.3 = f32[4,256,128]{1,2,0:T(8,128)S(1)} all-gather(f32[4,256,64]{1,2,0:T(8,128)S(1)} %copy.67), channel_id=1, replica_groups=mesh['rows'=128,'cols'=2] {'cols'}, dimensions={2}, use_global_device_ids=true | all-gather | bytes 786432 | tf_op jit(solution)/shard_map/all_gather | solution.py:140
  89.4 1.3 %fusion.gram_ref = f32[4,128,128]{2,1,0:T(8,128)} fusion(f32[4,256,128]{1,2,0:T(8,128)S(1)} %all_gather.3, f32[128,128]{1,0:T(8,128)S(1)} %fusion.18, pred[4]{0:T(512)(128)(4,1)S(1)} %iota_compare_fusion.4), kind=kOutput, calls=%fused_computation.3 | convolution fusion | flops 201457664 | bytes 851972 | tf_op jit(solution)/shard_map/sqi,sqk->sik/dot_general | solution.py:143
  90.7 13.8 %shard_map.47 = f32[4,128,128]{2,1,0:T(8,128)} custom-call(f32[4,128,128]{2,1,0:T(8,128)} %fusion.gram_ref), custom_call_target="tpu_custom_call" | custom-call | tf_op jit(solution)/shard_map/pallas_call | solution.py:47
  104.5 1.6 %dynamic-slice_select_fusion = f32[4,64,128]{2,1,0:T(8,128)} fusion(f32[4,128,128]{2,1,0:T(8,128)} %shard_map.47, s32[]{:T(128)S(6)} %select_n.209, pred[4]{0:T(512)(128)(4,1)S(1)} %iota_compare_fusion.4), kind=kLoop, calls=%fused_computation.12 | loop fusion | flops 32768 | bytes 262152 | tf_op jit(solution)/shard_map/jit(_where)/select_n | solution.py:151
  (11 shorter events, 0.2 us)
Async XLA Ops:
  0.0 27.7 %copy-start = (s32[256,256]{1,0:T(8,128)S(1)}, s32[256,256]{1,0:T(8,128)}, u32[]{:S(2)}) copy-start(s32[256,256]{1,0:T(8,128)} %param.6) | copy-start | bytes 786436
  11.0 46.6 %all-to-all-start = ((f32[128,16,128]{2,1,0:T(8,128)}), f32[128,16,128]{2,1,0:T(8,128)S(1)}, u32[]{:S(2)}, u32[]{:S(2)}) async-start(f32[128,16,128]{2,1,0:T(8,128)} %shard_map.46), calls=%async_computation | async-start | bytes 2097152 | tf_op jit(solution)/shard_map/all_to_all | solution.py:109
  33.1 0.7 copy-start.1
  62.7 18.8 %all-to-all-start.1 = ((f32[128,1,512]{2,1,0:T(1,128)}), f32[128,1,512]{2,1,0:T(1,128)S(1)}, u32[]{:S(2)}, u32[]{:S(2)}) async-start(f32[128,1,512]{2,1,0:T(1,128)} %reshape.436), calls=%async_computation.1 | async-start | bytes 524288 | tf_op jit(solution)/shard_map/all_to_all | solution.py:138

commit v5 on v4

--- a/solution.py
+++ b/solution.py
@@ -1,6 +1,7 @@
 import math
 
 import jax
+import numpy as np
 import jax.numpy as jnp
 from jax import lax
 from jax.experimental import pallas as pl
@@ -53,29 +54,30 @@
     )(gram)
 
 
-def local_mix_kernel(matrix_ref, flips_ref, table_ref, out_ref):
+def local_mix_kernel(matrix_ref, signs_ref, table_ref, out_ref):
     slab_width = matrix_ref.shape[0]
-    groups = table_ref.shape[1] // out_ref.shape[1]
+    rows = out_ref.shape[1]
+    groups = table_ref.shape[1] // rows
 
     def body(blk, carry):
         start = pl.multiple_of(blk * HB, HB)
-        flipped = matrix_ref[:, pl.ds(start, HB)] * flips_ref[:, pl.ds(start, HB)]
+        flips = (1 - 2 * signs_ref[:, pl.ds(start, HB)]).astype(jnp.float32)
+        flipped = (matrix_ref[:, pl.ds(start, HB)].astype(jnp.float32) * flips).astype(jnp.bfloat16)
         for parity in range(2):
             mixed = lax.dot_general(
                 table_ref[parity], flipped, (((1,), (1,)), ((), ())),
                 preferred_element_type=jnp.float32,
             )
             for h in range(groups):
-                rows = out_ref.shape[1]
                 out_ref[blk * groups + h, :, parity * slab_width:(parity + 1) * slab_width] = (
                     mixed[h * rows:(h + 1) * rows, :]
                 )
         return carry
 
-    lax.fori_loop(0, matrix_ref.shape[1] // HB, body, 0)
+    lax.fori_loop(0, matrix_ref.shape[1] // HB, body, 0, unroll=True)
 
 
-def local_mix(matrix, flips, table, row_devices):
+def local_mix(matrix, signs, table, row_devices):
     slab_width, shard_rows = matrix.shape
     sub_rows = shard_rows // row_devices
     return pl.pallas_call(
@@ -83,16 +85,16 @@
         out_shape=jax.ShapeDtypeStruct((row_devices, sub_rows // 2, 2 * slab_width), jnp.float32),
         in_specs=[pl.BlockSpec(memory_space=pltpu.VMEM)] * 3,
         out_specs=pl.BlockSpec(memory_space=pltpu.VMEM),
-    )(matrix, flips, table)
+    )(matrix, signs, table)
 
 
 def walsh_sign_matrix(order):
-    index_row = jnp.arange(order, dtype=jnp.int32)
-    parity = jnp.zeros((order, order), jnp.int32)
+    index_row = np.arange(order)
+    parity = np.zeros((order, order), np.int64)
     for bit_place in range(order.bit_length() - 1):
-        both = jnp.bitwise_and(index_row[:, None], index_row[None, :])
-        parity = parity + jnp.bitwise_and(jnp.right_shift(both, bit_place), 1)
-    return (1 - 2 * (parity % 2)).astype(jnp.float32)
+        both = np.bitwise_and(index_row[:, None], index_row[None, :])
+        parity = parity + np.bitwise_and(np.right_shift(both, bit_place), 1)
+    return (1 - 2 * (parity % 2)).astype(np.float32)
 
 
 def per_device(matrix, signs, samples, owners):
@@ -101,13 +103,11 @@
     row_devices = lax.axis_size("rows")
     processor_number = lax.axis_index("rows")
     sub_rows = shard_rows // row_devices
-    flips = (1 - 2 * signs).astype(jnp.bfloat16).reshape(1, shard_rows)
     scale = 1.0 / math.sqrt(HB * row_devices)
-    table = (walsh_sign_matrix(HB) * scale).astype(jnp.bfloat16)
-    table = table.reshape(HB // 2, 2, HB).transpose(1, 0, 2)
-    outgoing = local_mix(matrix, flips, table, row_devices)
+    table = (walsh_sign_matrix(HB) * scale).reshape(HB // 2, 2, HB).transpose(1, 0, 2)
+    outgoing = local_mix(matrix, signs.reshape(1, shard_rows), jnp.asarray(table, jnp.bfloat16), row_devices)
     received = lax.all_to_all(outgoing, "rows", split_axis=0, concat_axis=0, tiled=True)
-    across = walsh_sign_matrix(row_devices)
+    across = jnp.asarray(walsh_sign_matrix(row_devices))
     mixed = jnp.einsum(
         "st,tvl->svl", across, received, precision=lax.Precision.HIGHEST
     ).reshape(row_devices * sub_rows // 2, 2 * slab_width)

time: 107 us -> 98.3 us (0.919)
  Pallas kernels: 22.6 us -> 16.6 us
  other arithmetic: 6.1 us -> 4.56 us
    pallas_call x1, Pallas kernels: 8.86 us -> 2.83 us  [local_mix(): pl.pallas_call(local_mix_kernel, out_shape=jax.ShapeDtypeStruct((row_devi...]
    convert_element_type x2 -> x0, other arithmetic: 1.54 us -> none  [the longest x1 0.77 us: per_device(): table = (walsh_sign_matrix(HB) * scale).astype(jnp.bfloat16)]
where the time goes in v5:
time: 98.3 us; the launch traced here: 98 us
  waiting for transfers between devices  35 us (36%)
  starting transfers between devices  22.5 us (23%)
  Pallas kernels  16.6 us (17%)
  local copies, waits for them, and re-layouts  10.4 us (11%)
  blocking collectives  5.55 us (6%)
  other arithmetic  4.56 us (5%)
  matrix products  3.02 us (3%)
    all_to_all x1, waiting for transfers between devices, per_device(): lax.all_to_all(outgoing, 'rows', split_axis=0, concat_axis=0, tiled=True)  23 us
    all_to_all x1, starting transfers between devices, per_device(): lax.all_to_all(outgoing, 'rows', split_axis=0, concat_axis=0, tiled=True)  16.3 us
    pallas_call x1, Pallas kernels, cholesky_upper(): pl.pallas_call(cholesky_kernel, out_shape=jax.ShapeDtypeStruct(gram.shape...  13.8 us
    all_to_all x1, waiting for transfers between devices, per_device(): lax.all_to_all(bundled, 'rows', split_axis=0, concat_axis=0, tiled=True)  12 us
    all_to_all x1, starting transfers between devices, per_device(): lax.all_to_all(bundled, 'rows', split_axis=0, concat_axis=0, tiled=True)  6.16 us
    all_gather x1, blocking collectives, per_device(): whole_rows = lax.all_gather(received_rows, 'cols', axis=2, tiled=True)  5.55 us
    gather x7, local copies, waits for them, and re-layouts, per_device(): sample_values = jnp.take_along_axis(samples, picks, axis=1)  5.22 us
    pallas_call x1, Pallas kernels, local_mix(): pl.pallas_call(local_mix_kernel, out_shape=jax.ShapeDtypeStruct((row_devi...  2.83 us
  transfers between devices with their start and end apart: 2, of which 2 were waited for; matrix products, arithmetic and copies ran while one was open for 7% of the time, Pallas kernels for 0%

profile of v5, /device:TPU:1, one launch (start us, length us, event | category | flops | bytes accessed | tf_op | source)
XLA Modules:
  0.0 98.0 jit_solution(10309864855855951339)
XLA Ops:
  0.0 0.0 copy-start
  0.0 2.8 %shard_map.64 = f32[128,16,128]{2,1,0:T(8,128)} custom-call(bf16[64,4096]{1,0:T(8,128)(2,1)} %matrix_ref.1, s32[1,4096]{1,0:T(1,128)} %bitcast.34, bf16[2,64,128]{2,1,0:T(8,128)(2,1)} %constant.107.clone.table_ref), custom_call_target="tpu_custom_call" | custom-call | tf_op jit(solution)/shard_map/pallas_call | solution.py:83
  2.8 16.3 %all-to-all-start = ((f32[128,16,128]{2,1,0:T(8,128)}), f32[128,16,128]{2,1,0:T(8,128)S(1)}, u32[]{:S(2)}, u32[]{:S(2)}) async-start(f32[128,16,128]{2,1,0:T(8,128)} %shard_map.64), calls=%async_computation | async-start | bytes 2097152 | tf_op jit(solution)/shard_map/all_to_all | solution.py:109
  19.2 0.1 copy.59
  19.4 0.1 reshape.412
  19.5 0.0 copy-done
  19.5 4.5 %gather_fusion.1 = s32[512]{0:T(512)S(1)} fusion(s32[256,256]{1,0:T(8,128)S(1)} %copy-done, s32[512]{0:T(512)S(1)} %reshape.412), kind=kCustom, calls=%fused_computation.1 | custom fusion | bytes 8192 | tf_op jit(solution)/shard_map/jit(take_along_axis)/gather | solution.py:119
  24.0 0.1 gather.11
  24.2 0.1 reshape.415
  24.3 0.1 copy.63
  24.5 0.1 copy.64
  24.6 0.1 reshape.406
  24.7 0.0 copy-start.1
  24.8 0.1 copy.60
  24.9 0.0 copy-start.2
  24.9 0.7 copy-done.2
  25.6 0.2 convert_reduce_fusion
  25.7 0.6 fusion.12
  26.4 23.0 %all-to-all-done = f32[128,16,128]{2,1,0:T(8,128)S(1)} async-done(((f32[128,16,128]{2,1,0:T(8,128)}), f32[128,16,128]{2,1,0:T(8,128)S(1)}, u32[]{:S(2)}, u32[]{:S(2)}) %all-to-all-start) | async-done | bytes 1048608 | tf_op jit(solution)/shard_map/all_to_all | solution.py:109
  49.5 0.0 copy-done.1
  49.5 1.3 %fusion.1 = f32[128,16,128]{2,0,1:T(8,128)S(1)} fusion(f32[128,128,1]{1,0,2:T(8,128)S(1)} %copy-done.1, f32[128,16,128]{2,1,0:T(8,128)S(1)} %all-to-all-done), kind=kOutput, calls=%fused_computation.4 | convolution fusion | flops 402653184 | bytes 2162688 | tf_op jit(solution)/shard_map/st,tvl->svl/dot_general | solution.py:111
  50.8 0.6 copy.62
  51.4 1.0 %gather_fusion = f32[512,128]{1,0:T(8,128)S(1)} fusion(f32[2048,128]{1,0:T(8,128)S(1)} %bitcast.27, s32[1024]{0:T(1024)S(1)} %pad_clamp_fusion), kind=kCustom, calls=%fused_computation | custom fusion | bytes 526336 | tf_op jit(solution)/shard_map/jit(_take)/gather | solution.py:122
  52.4 0.1 copy.65
  52.6 0.4 fusion.3
  53.1 0.2 copy.66
  53.3 0.1 copy.75
  53.4 1.2 %reshape.423 = f32[128,1,512]{2,1,0:T(1,128)} reshape(f32[128,2,4,64]{3,2,1,0:T(4,128)S(1)} %bitcast.30) | data formatting | bytes 524288
  54.5 6.2 %all-to-all-start.1 = ((f32[128,1,512]{2,1,0:T(1,128)}), f32[128,1,512]{2,1,0:T(1,128)S(1)}, u32[]{:S(2)}, u32[]{:S(2)}) async-start(f32[128,1,512]{2,1,0:T(1,128)} %reshape.423), calls=%async_computation.1 | async-start | bytes 524288 | tf_op jit(solution)/shard_map/all_to_all | solution.py:138
  60.7 0.7 iota_compare_fusion.4
  61.4 12.0 %all-to-all-done.1 = f32[128,1,512]{2,1,0:T(1,128)S(1)} async-done(((f32[128,1,512]{2,1,0:T(1,128)}), f32[128,1,512]{2,1,0:T(1,128)S(1)}, u32[]{:S(2)}, u32[]{:S(2)}) %all-to-all-start.1) | async-done | bytes 262176 | tf_op jit(solution)/shard_map/all_to_all | solution.py:138
  73.4 0.5 broadcast.701
  73.9 1.3 %reduce = f32[128,512]{1,0:T(8,128)S(1)} reduce(f32[128,1,512]{2,1,0:T(1,128)S(1)} %all-to-all-done.1, f32[]{:T(128)} %broadcast.701), dimensions={1}, to_apply=%all_to_all.7.reduce_sub_computation | reduce | bytes 524292 | tf_op jit(solution)/shard_map/all_to_all | solution.py:138
  75.2 0.3 reshape.424
  75.5 0.2 copy.69
  75.7 5.5 %all_gather.3 = f32[4,256,128]{1,2,0:T(8,128)S(1)} all-gather(f32[4,256,64]{1,2,0:T(8,128)S(1)} %copy.69), channel_id=1, replica_groups=mesh['rows'=128,'cols'=2] {'cols'}, dimensions={2}, use_global_device_ids=true | all-gather | bytes 786432 | tf_op jit(solution)/shard_map/all_gather | solution.py:140
  81.2 1.3 %fusion.gram_ref = f32[4,128,128]{2,1,0:T(8,128)} fusion(f32[4,256,128]{1,2,0:T(8,128)S(1)} %all_gather.3, f32[128,128]{1,0:T(8,128)S(1)} %fusion.6, pred[4]{0:T(512)(128)(4,1)S(1)} %iota_compare_fusion.4), kind=kOutput, calls=%fused_computation.3 | convolution fusion | flops 201457664 | bytes 851972 | tf_op jit(solution)/shard_map/sqi,sqk->sik/dot_general | solution.py:143
  82.5 13.8 %shard_map.65 = f32[4,128,128]{2,1,0:T(8,128)} custom-call(f32[4,128,128]{2,1,0:T(8,128)} %fusion.gram_ref), custom_call_target="tpu_custom_call" | custom-call | tf_op jit(solution)/shard_map/pallas_call | solution.py:48
  96.3 1.6 %dynamic-slice_select_fusion = f32[4,64,128]{2,1,0:T(8,128)} fusion(f32[4,128,128]{2,1,0:T(8,128)} %shard_map.65, s32[]{:T(128)S(6)} %select_n.195, pred[4]{0:T(512)(128)(4,1)S(1)} %iota_compare_fusion.4), kind=kLoop, calls=%fused_computation.12 | loop fusion | flops 32768 | bytes 262152 | tf_op jit(solution)/shard_map/jit(_where)/select_n | solution.py:151
  (10 shorter events, 0.2 us)
Async XLA Ops:
  0.0 19.5 %copy-start = (s32[256,256]{1,0:T(8,128)S(1)}, s32[256,256]{1,0:T(8,128)}, u32[]{:S(2)}) copy-start(s32[256,256]{1,0:T(8,128)} %param.8) | copy-start | bytes 786436
  2.8 46.6 %all-to-all-start = ((f32[128,16,128]{2,1,0:T(8,128)}), f32[128,16,128]{2,1,0:T(8,128)S(1)}, u32[]{:S(2)}, u32[]{:S(2)}) async-start(f32[128,16,128]{2,1,0:T(8,128)} %shard_map.64), calls=%async_computation | async-start | bytes 2097152 | tf_op jit(solution)/shard_map/all_to_all | solution.py:109
  24.7 24.7 %copy-start.1 = (f32[128,128,1]{1,0,2:T(8,128)S(1)}, f32[128,128,1]{1,0,2:T(8,128)}, u32[]{:S(2)}) copy-start(f32[128,128,1]{1,0,2:T(8,128)} %constant.122) | copy-start | bytes 196612
  24.9 0.7 copy-start.2
  54.5 18.9 %all-to-all-start.1 = ((f32[128,1,512]{2,1,0:T(1,128)}), f32[128,1,512]{2,1,0:T(1,128)S(1)}, u32[]{:S(2)}, u32[]{:S(2)}) async-start(f32[128,1,512]{2,1,0:T(1,128)} %reshape.423), calls=%async_computation.1 | async-start | bytes 524288 | tf_op jit(solution)/shard_map/all_to_all | solution.py:138

commit v6 on v5

--- a/solution.py
+++ b/solution.py
@@ -15,9 +15,19 @@
 PANEL = 32
 
 
-def cholesky_kernel(gram_ref, out_ref, work_ref):
-    blocks, order, _ = gram_ref.shape
-    work_ref[...] = gram_ref[...]
+def cholesky_kernel(column_ref, rows_ref, live_ref, out_ref, work_ref):
+    blocks, samples, order = rows_ref.shape
+    for b in range(blocks):
+        gram = lax.dot_general(
+            rows_ref[b], rows_ref[b], (((0,), (0,)), ((), ())),
+            precision=lax.Precision.HIGHEST, preferred_element_type=jnp.float32,
+        ) / samples
+        diagonal = (
+            lax.broadcasted_iota(jnp.int32, (order, order), 0)
+            == lax.broadcasted_iota(jnp.int32, (order, order), 1)
+        )
+        identity = jnp.where(diagonal, 1.0, 0.0)
+        work_ref[b] = jnp.where(live_ref[b] > 0.0, gram, identity)
     lane = lax.broadcasted_iota(jnp.int32, (blocks, 1, order), 2)
     sub_panel = lax.broadcasted_iota(jnp.int32, (blocks, PANEL, order), 1)
     sub_col = lax.broadcasted_iota(jnp.int32, (blocks, PANEL, 1), 1)
@@ -33,7 +43,6 @@
             factor_column = jnp.where(sub_col > jj, column * inverse_root, 0.0)
             panel = panel - factor_column * factor_row
             panel = jnp.where(sub_panel == jj, factor_row, panel)
-        out_ref[:, base:base + PANEL, :] = panel
         if p + 1 < order // PANEL:
             for b in range(blocks):
                 update = lax.dot_general(
@@ -41,17 +50,24 @@
                     precision=lax.Precision.HIGHEST, preferred_element_type=jnp.float32,
                 )
                 work_ref[b, base + PANEL:, :] = work_ref[b, base + PANEL:, :] - update[base + PANEL:, :]
+        work_ref[:, base:base + PANEL, :] = panel * live_ref[...]
+    start = pl.multiple_of(column_ref[0] * out_ref.shape[1], out_ref.shape[1])
+    out_ref[...] = work_ref[:, pl.ds(start, out_ref.shape[1]), :]
 
 
-def cholesky_upper(gram):
-    blocks, order, _ = gram.shape
+def cholesky_upper(column_index, whole_rows, live, slab_width):
+    blocks, samples, order = whole_rows.shape
     return pl.pallas_call(
         cholesky_kernel,
-        out_shape=jax.ShapeDtypeStruct(gram.shape, jnp.float32),
-        in_specs=[pl.BlockSpec(memory_space=pltpu.VMEM)],
-        out_specs=pl.BlockSpec(memory_space=pltpu.VMEM),
-        scratch_shapes=[pltpu.VMEM(gram.shape, jnp.float32)],
-    )(gram)
+        out_shape=jax.ShapeDtypeStruct((blocks, slab_width, order), jnp.float32),
+        grid_spec=pltpu.PrefetchScalarGridSpec(
+            num_scalar_prefetch=1,
+            grid=(1,),
+            in_specs=[pl.BlockSpec(memory_space=pltpu.VMEM)] * 2,
+            out_specs=pl.BlockSpec(memory_space=pltpu.VMEM),
+            scratch_shapes=[pltpu.VMEM((blocks, order, order), jnp.float32)],
+        ),
+    )(column_index, whole_rows, live)
 
 
 def local_mix_kernel(matrix_ref, signs_ref, table_ref, out_ref):
@@ -134,23 +150,15 @@
         jnp.float32
     )
     bundled = jnp.einsum("kb,bps->kps", placing, chosen, precision=lax.Precision.HIGHEST)
-    bundled = bundled.reshape(row_devices, CAPB, 2, slab_width)
+    bundled = bundled.reshape(row_devices, CAPB, 2 * slab_width)
     arriving = lax.all_to_all(bundled, "rows", split_axis=0, concat_axis=0, tiled=True)
-    received_rows = jnp.transpose(arriving, (1, 0, 2, 3)).reshape(CAPB, row_devices * 2, slab_width)
+    received_rows = jnp.transpose(arriving, (1, 0, 2)).reshape(CAPB, row_devices * 2, slab_width)
     whole_rows = lax.all_gather(received_rows, "cols", axis=2, tiled=True)
-    window_width = whole_rows.shape[2]
-    gram_product = (
-        jnp.einsum("sqi,sqk->sik", whole_rows, whole_rows, precision=lax.Precision.HIGHEST)
-        / SKETCH_ROW_COUNT
-    )
     owned_total = jnp.sum((owner_list == processor_number).astype(jnp.int32))
-    live = jnp.arange(CAPB, dtype=jnp.int32) < owned_total
-    identity = jnp.eye(window_width, dtype=jnp.float32)
-    safe = jnp.where(live[:, None, None], gram_product, identity[None, :, :])
-    upper = cholesky_upper(safe)
-    upper = jnp.where(live[:, None, None], upper, jnp.zeros_like(upper))
-    column_start = lax.axis_index("cols") * slab_width
-    return lax.dynamic_slice_in_dim(upper, column_start, slab_width, 1)
+    live = (jnp.arange(CAPB, dtype=jnp.int32) < owned_total).astype(jnp.float32)
+    live = jnp.broadcast_to(live[:, None, None], (CAPB, 1, whole_rows.shape[2]))
+    column_index = lax.axis_index("cols").astype(jnp.int32).reshape(1)
+    return cholesky_upper(column_index, whole_rows, live, slab_width)
 
 
 def solution(mesh):

time: 98.3 us -> 95 us (0.966)
  other arithmetic: 4.56 us -> 1.65 us
    select_n x1 -> x0, other arithmetic: 1.64 us -> none  [per_device(): upper = jnp.where(live[:, None, None], upper, jnp.zeros_like(upper))]
    unnamed x8 -> x6, local copies, waits for them, and re-layouts: 2.14 us -> 0.69 us
    dot_general x1 -> x0, matrix products: 1.32 us -> none  [per_device(): jnp.einsum('sqi,sqk->sik', whole_rows, whole_rows, precision=lax.Precisio...]
    all_to_all x1 -> x0, other arithmetic: 1.26 us -> none  [per_device(): lax.all_to_all(bundled, 'rows', split_axis=0, concat_axis=0, tiled=True)]
    all_gather x0 -> x1, local copies, waits for them, and re-layouts: none -> 1.02 us  [per_device(): whole_rows = lax.all_gather(received_rows, 'cols', axis=2, tiled=True)]
  transfers between devices with their start and end apart: 2 -> 2, of which waited for: 2 -> 2; matrix products, arithmetic and copies ran while one was open for 7% -> 8% of each run, Pallas kernels for 0% -> 0%
where the time goes in v6:
time: 95 us; the launch traced here: 94.7 us
  waiting for transfers between devices  35.1 us (37%)
  starting transfers between devices  22.5 us (24%)
  Pallas kernels  17.3 us (18%)
  local copies, waits for them, and re-layouts  10 us (11%)
  blocking collectives  5.55 us (6%)
  matrix products  2.37 us (2%)
  other arithmetic  1.65 us (2%)
    all_to_all x1, waiting for transfers between devices, per_device(): lax.all_to_all(outgoing, 'rows', split_axis=0, concat_axis=0, tiled=True)  23 us
    all_to_all x1, starting transfers between devices, per_device(): lax.all_to_all(outgoing, 'rows', split_axis=0, concat_axis=0, tiled=True)  16.3 us
    pallas_call x1, Pallas kernels, cholesky_upper(): pl.pallas_call(cholesky_kernel, out_shape=jax.ShapeDtypeStruct((blocks, s...  14.5 us
    all_to_all x1, waiting for transfers between devices, per_device(): lax.all_to_all(bundled, 'rows', split_axis=0, concat_axis=0, tiled=True)  12 us
    all_to_all x1, starting transfers between devices, per_device(): lax.all_to_all(bundled, 'rows', split_axis=0, concat_axis=0, tiled=True)  6.17 us
    all_gather x1, blocking collectives, per_device(): whole_rows = lax.all_gather(received_rows, 'cols', axis=2, tiled=True)  5.55 us
    gather x7, local copies, waits for them, and re-layouts, per_device(): sample_values = jnp.take_along_axis(samples, picks, axis=1)  5.22 us
    pallas_call x1, Pallas kernels, local_mix(): pl.pallas_call(local_mix_kernel, out_shape=jax.ShapeDtypeStruct((row_devi...  2.84 us
  transfers between devices with their start and end apart: 2, of which 2 were waited for; matrix products, arithmetic and copies ran while one was open for 8% of the time, Pallas kernels for 0%

profile of v6, /device:TPU:1, one launch (start us, length us, event | category | flops | bytes accessed | tf_op | source)
XLA Modules:
  0.0 94.7 jit_solution(14931529737176031917)
XLA Ops:
  0.0 0.0 copy-start
  0.0 2.8 %shard_map.64 = f32[128,16,128]{2,1,0:T(8,128)} custom-call(bf16[64,4096]{1,0:T(8,128)(2,1)} %matrix_ref.1, s32[1,4096]{1,0:T(1,128)} %bitcast.24, bf16[2,64,128]{2,1,0:T(8,128)(2,1)} %constant.100.clone.table_ref), custom_call_target="tpu_custom_call" | custom-call | tf_op jit(solution)/shard_map/pallas_call | solution.py:99
  2.8 16.3 %all-to-all-start = ((f32[128,16,128]{2,1,0:T(8,128)}), f32[128,16,128]{2,1,0:T(8,128)S(1)}, u32[]{:S(2)}, u32[]{:S(2)}) async-start(f32[128,16,128]{2,1,0:T(8,128)} %shard_map.64), calls=%async_computation | async-start | bytes 2097152 | tf_op jit(solution)/shard_map/all_to_all | solution.py:125
  19.2 0.1 copy.58
  19.4 0.1 reshape.411
  19.5 0.0 copy-done
  19.5 4.5 %gather_fusion.1 = s32[512]{0:T(512)S(1)} fusion(s32[256,256]{1,0:T(8,128)S(1)} %copy-done, s32[512]{0:T(512)S(1)} %reshape.411), kind=kCustom, calls=%fused_computation.1 | custom fusion | bytes 8192 | tf_op jit(solution)/shard_map/jit(take_along_axis)/gather | solution.py:135
  24.0 0.1 gather.11
  24.2 0.1 reshape.414
  24.3 0.1 copy.62
  24.5 0.1 copy.63
  24.6 0.1 reshape.405
  24.8 0.0 copy-start.1
  24.8 0.1 copy.59
  24.9 0.0 copy-start.2
  24.9 0.7 copy-done.2
  25.6 0.2 convert_reduce_fusion
  25.7 0.6 fusion.10
  26.4 23.0 %all-to-all-done = f32[128,16,128]{2,1,0:T(8,128)S(1)} async-done(((f32[128,16,128]{2,1,0:T(8,128)}), f32[128,16,128]{2,1,0:T(8,128)S(1)}, u32[]{:S(2)}, u32[]{:S(2)}) %all-to-all-start) | async-done | bytes 1048608 | tf_op jit(solution)/shard_map/all_to_all | solution.py:125
  49.5 0.0 copy-done.1
  49.5 1.3 %fusion = f32[128,16,128]{2,0,1:T(8,128)S(1)} fusion(f32[128,128,1]{1,0,2:T(8,128)S(1)} %copy-done.1, f32[128,16,128]{2,1,0:T(8,128)S(1)} %all-to-all-done), kind=kOutput, calls=%fused_computation.2 | convolution fusion | flops 402653184 | bytes 2162688 | tf_op jit(solution)/shard_map/st,tvl->svl/dot_general | solution.py:127
  50.8 0.6 copy.61
  51.4 1.0 %gather_fusion = f32[512,128]{1,0:T(8,128)S(1)} fusion(f32[2048,128]{1,0:T(8,128)S(1)} %bitcast.20, s32[1024]{0:T(1024)S(1)} %pad_clamp_fusion), kind=kCustom, calls=%fused_computation | custom fusion | bytes 526336 | tf_op jit(solution)/shard_map/jit(_take)/gather | solution.py:138
  52.4 0.1 copy.64
  52.6 1.1 %fusion.2 = f32[512,128]{1,0:T(8,128)} fusion(f32[256,128]{0,1:T(8,128)S(1)} %bitcast.23, s32[256]{0:T(256)S(1)} %get-tuple-element.9), kind=kOutput, calls=%fused_computation.5 | convolution fusion | flops 201457664 | bytes 394240
  53.7 6.2 %all-to-all-start.1 = ((f32[128,4,128]{2,1,0:T(4,128)}), f32[128,4,128]{2,1,0:T(4,128)S(1)}, u32[]{:S(2)}, u32[]{:S(2)}) async-start(f32[128,4,128]{2,1,0:T(4,128)} %bitcast.11), calls=%async_computation.1 | async-start | bytes 524288 | tf_op jit(solution)/shard_map/all_to_all | solution.py:154
  59.9 0.7 compare_convert_fusion
  60.6 12.0 %all-to-all-done.1 = f32[128,4,128]{2,1,0:T(4,128)S(1)} async-done(((f32[128,4,128]{2,1,0:T(4,128)}), f32[128,4,128]{2,1,0:T(4,128)S(1)}, u32[]{:S(2)}, u32[]{:S(2)}) %all-to-all-start.1) | async-done | bytes 262176 | tf_op jit(solution)/shard_map/all_to_all | solution.py:154
  72.6 0.1 reshape.402
  72.8 0.2 copy.67
  73.0 5.5 %all_gather.3 = f32[4,256,128]{1,0,2:T(4,128)S(1)} all-gather(f32[4,256,64]{1,0,2:T(4,128)S(1)} %copy.67), channel_id=1, replica_groups=mesh['rows'=128,'cols'=2] {'cols'}, dimensions={2}, use_global_device_ids=true | all-gather | bytes 786432 | tf_op jit(solution)/shard_map/all_gather | solution.py:156
  78.5 1.0 %copy.68.rows_ref = f32[4,256,128]{2,1,0:T(8,128)} copy(f32[4,256,128]{1,0,2:T(4,128)S(1)} %all_gather.3) | data formatting | bytes 1048576 | tf_op jit(solution)/shard_map/all_gather | solution.py:156
  79.5 0.6 broadcast_in_dim.40.live_ref
  80.2 14.5 %shard_map.65 = f32[4,64,128]{2,1,0:T(8,128)} custom-call(s32[1]{0:T(128)} %bitcast.column_ref, f32[4,256,128]{2,1,0:T(8,128)} %copy.68.rows_ref, f32[4,1,128]{2,1,0:T(1,128)} %broadcast_in_dim.40.live_ref), custom_call_target="tpu_custom_call" | custom-call | tf_op jit(solution)/shard_map/pallas_call | solution.py:60
  (10 shorter events, 0.2 us)
Async XLA Ops:
  0.0 19.5 %copy-start = (s32[256,256]{1,0:T(8,128)S(1)}, s32[256,256]{1,0:T(8,128)}, u32[]{:S(2)}) copy-start(s32[256,256]{1,0:T(8,128)} %param.8) | copy-start | bytes 786436
  2.8 46.6 %all-to-all-start = ((f32[128,16,128]{2,1,0:T(8,128)}), f32[128,16,128]{2,1,0:T(8,128)S(1)}, u32[]{:S(2)}, u32[]{:S(2)}) async-start(f32[128,16,128]{2,1,0:T(8,128)} %shard_map.64), calls=%async_computation | async-start | bytes 2097152 | tf_op jit(solution)/shard_map/all_to_all | solution.py:125
  24.8 24.7 %copy-start.1 = (f32[128,128,1]{1,0,2:T(8,128)S(1)}, f32[128,128,1]{1,0,2:T(8,128)}, u32[]{:S(2)}) copy-start(f32[128,128,1]{1,0,2:T(8,128)} %constant.115) | copy-start | bytes 196612
  24.9 0.7 copy-start.2
  53.7 18.9 %all-to-all-start.1 = ((f32[128,4,128]{2,1,0:T(4,128)}), f32[128,4,128]{2,1,0:T(4,128)S(1)}, u32[]{:S(2)}, u32[]{:S(2)}) async-start(f32[128,4,128]{2,1,0:T(4,128)} %bitcast.11), calls=%async_computation.1 | async-start | bytes 524288 | tf_op jit(solution)/shard_map/all_to_all | solution.py:154

commit v7 on v6

--- a/solution.py
+++ b/solution.py
@@ -13,6 +13,7 @@
 CAPB = 4
 
 PANEL = 32
+STEP = 8
 
 
 def cholesky_kernel(column_ref, rows_ref, live_ref, out_ref, work_ref):
@@ -30,19 +31,30 @@
         work_ref[b] = jnp.where(live_ref[b] > 0.0, gram, identity)
     lane = lax.broadcasted_iota(jnp.int32, (blocks, 1, order), 2)
     sub_panel = lax.broadcasted_iota(jnp.int32, (blocks, PANEL, order), 1)
-    sub_col = lax.broadcasted_iota(jnp.int32, (blocks, PANEL, 1), 1)
     for p in range(order // PANEL):
         base = p * PANEL
         panel = work_ref[:, base:base + PANEL, :]
-        for jj in range(PANEL):
-            j = base + jj
-            row = panel[:, jj:jj + 1, :]
-            column = panel[:, :, j:j + 1]
-            inverse_root = lax.rsqrt(column[:, jj:jj + 1, :])
-            factor_row = jnp.where(lane >= j, row * inverse_root, 0.0)
-            factor_column = jnp.where(sub_col > jj, column * inverse_root, 0.0)
-            panel = panel - factor_column * factor_row
-            panel = jnp.where(sub_panel == jj, factor_row, panel)
+        for first in range(0, PANEL, STEP):
+            columns = [
+                jnp.broadcast_to(panel[:, :, base + first + m:base + first + m + 1], panel.shape)
+                for m in range(STEP)
+            ]
+            factor_rows, factor_columns = [], []
+            for m in range(STEP):
+                jj = first + m
+                column = columns[m]
+                row = panel[:, jj:jj + 1, :]
+                for earlier in range(m):
+                    coupling = factor_columns[earlier][:, jj:jj + 1, :]
+                    column = column - factor_columns[earlier] * coupling
+                    row = row - coupling * factor_rows[earlier]
+                inverse_root = lax.rsqrt(column[:, jj:jj + 1, :])
+                factor_rows.append(jnp.where(lane >= base + jj, row * inverse_root, 0.0))
+                factor_columns.append(jnp.where(sub_panel > jj, column * inverse_root, 0.0))
+            for m in range(STEP):
+                panel = panel - factor_columns[m] * factor_rows[m]
+            for m in range(STEP):
+                panel = jnp.where(sub_panel == first + m, factor_rows[m], panel)
         if p + 1 < order // PANEL:
             for b in range(blocks):
                 update = lax.dot_general(

time: 95 us -> 88.1 us (0.927)
  Pallas kernels: 17.3 us -> 10.4 us
    pallas_call x1, Pallas kernels: 14.5 us -> 7.57 us  [cholesky_upper(): pl.pallas_call(cholesky_kernel, out_shape=jax.ShapeDtypeStruct((blocks, s...]
where the time goes in v7:
time: 88.1 us; the launch traced here: 87.8 us
  waiting for transfers between devices  35.1 us (40%)
  starting transfers between devices  22.5 us (26%)
  Pallas kernels  10.4 us (12%)
  local copies, waits for them, and re-layouts  10 us (11%)
  blocking collectives  5.55 us (6%)
  matrix products  2.37 us (3%)
  other arithmetic  1.65 us (2%)
    all_to_all x1, waiting for transfers between devices, per_device(): lax.all_to_all(outgoing, 'rows', split_axis=0, concat_axis=0, tiled=True)  23 us
    all_to_all x1, starting transfers between devices, per_device(): lax.all_to_all(outgoing, 'rows', split_axis=0, concat_axis=0, tiled=True)  16.3 us
    all_to_all x1, waiting for transfers between devices, per_device(): lax.all_to_all(bundled, 'rows', split_axis=0, concat_axis=0, tiled=True)  12 us
    pallas_call x1, Pallas kernels, cholesky_upper(): pl.pallas_call(cholesky_kernel, out_shape=jax.ShapeDtypeStruct((blocks, s...  7.57 us
    all_to_all x1, starting transfers between devices, per_device(): lax.all_to_all(bundled, 'rows', split_axis=0, concat_axis=0, tiled=True)  6.17 us
    all_gather x1, blocking collectives, per_device(): whole_rows = lax.all_gather(received_rows, 'cols', axis=2, tiled=True)  5.55 us
    gather x7, local copies, waits for them, and re-layouts, per_device(): sample_values = jnp.take_along_axis(samples, picks, axis=1)  5.22 us
    pallas_call x1, Pallas kernels, local_mix(): pl.pallas_call(local_mix_kernel, out_shape=jax.ShapeDtypeStruct((row_devi...  2.84 us
  transfers between devices with their start and end apart: 2, of which 2 were waited for; matrix products, arithmetic and copies ran while one was open for 8% of the time, Pallas kernels for 0%

profile of v7, /device:TPU:1, one launch (start us, length us, event | category | flops | bytes accessed | tf_op | source)
XLA Modules:
  0.0 87.8 jit_solution(865897287616088102)
XLA Ops:
  0.0 0.0 copy-start
  0.0 2.8 %shard_map.64 = f32[128,16,128]{2,1,0:T(8,128)} custom-call(bf16[64,4096]{1,0:T(8,128)(2,1)} %matrix_ref.1, s32[1,4096]{1,0:T(1,128)} %bitcast.24, bf16[2,64,128]{2,1,0:T(8,128)(2,1)} %constant.100.clone.table_ref), custom_call_target="tpu_custom_call" | custom-call | tf_op jit(solution)/shard_map/pallas_call | solution.py:111
  2.8 16.3 %all-to-all-start = ((f32[128,16,128]{2,1,0:T(8,128)}), f32[128,16,128]{2,1,0:T(8,128)S(1)}, u32[]{:S(2)}, u32[]{:S(2)}) async-start(f32[128,16,128]{2,1,0:T(8,128)} %shard_map.64), calls=%async_computation | async-start | bytes 2097152 | tf_op jit(solution)/shard_map/all_to_all | solution.py:137
  19.2 0.1 copy.58
  19.4 0.1 reshape.411
  19.5 0.0 copy-done
  19.5 4.5 %gather_fusion.1 = s32[512]{0:T(512)S(1)} fusion(s32[256,256]{1,0:T(8,128)S(1)} %copy-done, s32[512]{0:T(512)S(1)} %reshape.411), kind=kCustom, calls=%fused_computation.1 | custom fusion | bytes 8192 | tf_op jit(solution)/shard_map/jit(take_along_axis)/gather | solution.py:147
  24.0 0.1 gather.11
  24.2 0.1 reshape.414
  24.3 0.1 copy.62
  24.5 0.1 copy.63
  24.6 0.1 reshape.405
  24.8 0.0 copy-start.1
  24.8 0.1 copy.59
  24.9 0.0 copy-start.2
  24.9 0.7 copy-done.2
  25.6 0.2 convert_reduce_fusion
  25.7 0.6 fusion.10
  26.4 23.0 %all-to-all-done = f32[128,16,128]{2,1,0:T(8,128)S(1)} async-done(((f32[128,16,128]{2,1,0:T(8,128)}), f32[128,16,128]{2,1,0:T(8,128)S(1)}, u32[]{:S(2)}, u32[]{:S(2)}) %all-to-all-start) | async-done | bytes 1048608 | tf_op jit(solution)/shard_map/all_to_all | solution.py:137
  49.5 0.0 copy-done.1
  49.5 1.3 %fusion = f32[128,16,128]{2,0,1:T(8,128)S(1)} fusion(f32[128,128,1]{1,0,2:T(8,128)S(1)} %copy-done.1, f32[128,16,128]{2,1,0:T(8,128)S(1)} %all-to-all-done), kind=kOutput, calls=%fused_computation.2 | convolution fusion | flops 402653184 | bytes 2162688 | tf_op jit(solution)/shard_map/st,tvl->svl/dot_general | solution.py:139
  50.8 0.6 copy.61
  51.4 1.0 %gather_fusion = f32[512,128]{1,0:T(8,128)S(1)} fusion(f32[2048,128]{1,0:T(8,128)S(1)} %bitcast.20, s32[1024]{0:T(1024)S(1)} %pad_clamp_fusion), kind=kCustom, calls=%fused_computation | custom fusion | bytes 526336 | tf_op jit(solution)/shard_map/jit(_take)/gather | solution.py:150
  52.4 0.1 copy.64
  52.6 1.1 %fusion.2 = f32[512,128]{1,0:T(8,128)} fusion(f32[256,128]{0,1:T(8,128)S(1)} %bitcast.23, s32[256]{0:T(256)S(1)} %get-tuple-element.9), kind=kOutput, calls=%fused_computation.5 | convolution fusion | flops 201457664 | bytes 394240
  53.7 6.2 %all-to-all-start.1 = ((f32[128,4,128]{2,1,0:T(4,128)}), f32[128,4,128]{2,1,0:T(4,128)S(1)}, u32[]{:S(2)}, u32[]{:S(2)}) async-start(f32[128,4,128]{2,1,0:T(4,128)} %bitcast.11), calls=%async_computation.1 | async-start | bytes 524288 | tf_op jit(solution)/shard_map/all_to_all | solution.py:166
  59.9 0.7 compare_convert_fusion
  60.6 12.0 %all-to-all-done.1 = f32[128,4,128]{2,1,0:T(4,128)S(1)} async-done(((f32[128,4,128]{2,1,0:T(4,128)}), f32[128,4,128]{2,1,0:T(4,128)S(1)}, u32[]{:S(2)}, u32[]{:S(2)}) %all-to-all-start.1) | async-done | bytes 262176 | tf_op jit(solution)/shard_map/all_to_all | solution.py:166
  72.6 0.1 reshape.402
  72.8 0.2 copy.67
  73.0 5.5 %all_gather.3 = f32[4,256,128]{1,0,2:T(4,128)S(1)} all-gather(f32[4,256,64]{1,0,2:T(4,128)S(1)} %copy.67), channel_id=1, replica_groups=mesh['rows'=128,'cols'=2] {'cols'}, dimensions={2}, use_global_device_ids=true | all-gather | bytes 786432 | tf_op jit(solution)/shard_map/all_gather | solution.py:168
  78.5 1.0 %copy.68.rows_ref = f32[4,256,128]{2,1,0:T(8,128)} copy(f32[4,256,128]{1,0,2:T(4,128)S(1)} %all_gather.3) | data formatting | bytes 1048576 | tf_op jit(solution)/shard_map/all_gather | solution.py:168
  79.6 0.6 broadcast_in_dim.40.live_ref
  80.2 7.6 %shard_map.65 = f32[4,64,128]{2,1,0:T(8,128)} custom-call(s32[1]{0:T(128)} %bitcast.column_ref, f32[4,256,128]{2,1,0:T(8,128)} %copy.68.rows_ref, f32[4,1,128]{2,1,0:T(1,128)} %broadcast_in_dim.40.live_ref), custom_call_target="tpu_custom_call" | custom-call | tf_op jit(solution)/shard_map/pallas_call | solution.py:72
  (10 shorter events, 0.2 us)
Async XLA Ops:
  0.0 19.5 %copy-start = (s32[256,256]{1,0:T(8,128)S(1)}, s32[256,256]{1,0:T(8,128)}, u32[]{:S(2)}) copy-start(s32[256,256]{1,0:T(8,128)} %param.8) | copy-start | bytes 786436
  2.8 46.6 %all-to-all-start = ((f32[128,16,128]{2,1,0:T(8,128)}), f32[128,16,128]{2,1,0:T(8,128)S(1)}, u32[]{:S(2)}, u32[]{:S(2)}) async-start(f32[128,16,128]{2,1,0:T(8,128)} %shard_map.64), calls=%async_computation | async-start | bytes 2097152 | tf_op jit(solution)/shard_map/all_to_all | solution.py:137
  24.8 24.7 %copy-start.1 = (f32[128,128,1]{1,0,2:T(8,128)S(1)}, f32[128,128,1]{1,0,2:T(8,128)}, u32[]{:S(2)}) copy-start(f32[128,128,1]{1,0,2:T(8,128)} %constant.115) | copy-start | bytes 196612
  24.9 0.7 copy-start.2
  53.7 18.9 %all-to-all-start.1 = ((f32[128,4,128]{2,1,0:T(4,128)}), f32[128,4,128]{2,1,0:T(4,128)S(1)}, u32[]{:S(2)}, u32[]{:S(2)}) async-start(f32[128,4,128]{2,1,0:T(4,128)} %bitcast.11), calls=%async_computation.1 | async-start | bytes 524288 | tf_op jit(solution)/shard_map/all_to_all | solution.py:166

commit v8 on v7

--- a/solution.py
+++ b/solution.py
@@ -16,7 +16,7 @@
 STEP = 8
 
 
-def cholesky_kernel(column_ref, rows_ref, live_ref, out_ref, work_ref):
+def cholesky_kernel(scalar_ref, rows_ref, out_ref, work_ref):
     blocks, samples, order = rows_ref.shape
     for b in range(blocks):
         gram = lax.dot_general(
@@ -28,7 +28,7 @@
             == lax.broadcasted_iota(jnp.int32, (order, order), 1)
         )
         identity = jnp.where(diagonal, 1.0, 0.0)
-        work_ref[b] = jnp.where(live_ref[b] > 0.0, gram, identity)
+        work_ref[b] = jnp.where(b < scalar_ref[1], gram, identity)
     lane = lax.broadcasted_iota(jnp.int32, (blocks, 1, order), 2)
     sub_panel = lax.broadcasted_iota(jnp.int32, (blocks, PANEL, order), 1)
     for p in range(order // PANEL):
@@ -62,12 +62,13 @@
                     precision=lax.Precision.HIGHEST, preferred_element_type=jnp.float32,
                 )
                 work_ref[b, base + PANEL:, :] = work_ref[b, base + PANEL:, :] - update[base + PANEL:, :]
-        work_ref[:, base:base + PANEL, :] = panel * live_ref[...]
-    start = pl.multiple_of(column_ref[0] * out_ref.shape[1], out_ref.shape[1])
-    out_ref[...] = work_ref[:, pl.ds(start, out_ref.shape[1]), :]
+        work_ref[:, base:base + PANEL, :] = panel
+    start = pl.multiple_of(scalar_ref[0] * out_ref.shape[1], out_ref.shape[1])
+    for b in range(blocks):
+        out_ref[b] = jnp.where(b < scalar_ref[1], work_ref[b, pl.ds(start, out_ref.shape[1]), :], 0.0)
 
 
-def cholesky_upper(column_index, whole_rows, live, slab_width):
+def cholesky_upper(scalars, whole_rows, slab_width):
     blocks, samples, order = whole_rows.shape
     return pl.pallas_call(
         cholesky_kernel,
@@ -75,11 +76,11 @@
         grid_spec=pltpu.PrefetchScalarGridSpec(
             num_scalar_prefetch=1,
             grid=(1,),
-            in_specs=[pl.BlockSpec(memory_space=pltpu.VMEM)] * 2,
+            in_specs=[pl.BlockSpec(memory_space=pltpu.VMEM)],
             out_specs=pl.BlockSpec(memory_space=pltpu.VMEM),
             scratch_shapes=[pltpu.VMEM((blocks, order, order), jnp.float32)],
         ),
-    )(column_index, whole_rows, live)
+    )(scalars, whole_rows)
 
 
 def local_mix_kernel(matrix_ref, signs_ref, table_ref, out_ref):
@@ -167,10 +168,8 @@
     received_rows = jnp.transpose(arriving, (1, 0, 2)).reshape(CAPB, row_devices * 2, slab_width)
     whole_rows = lax.all_gather(received_rows, "cols", axis=2, tiled=True)
     owned_total = jnp.sum((owner_list == processor_number).astype(jnp.int32))
-    live = (jnp.arange(CAPB, dtype=jnp.int32) < owned_total).astype(jnp.float32)
-    live = jnp.broadcast_to(live[:, None, None], (CAPB, 1, whole_rows.shape[2]))
-    column_index = lax.axis_index("cols").astype(jnp.int32).reshape(1)
-    return cholesky_upper(column_index, whole_rows, live, slab_width)
+    scalars = jnp.stack([lax.axis_index("cols").astype(jnp.int32), owned_total.astype(jnp.int32)])
+    return cholesky_upper(scalars, whole_rows, slab_width)
 
 
 def solution(mesh):

time: 88.1 us -> 88.1 us (level)
    another operation x0 -> x1, other arithmetic: none -> 1.3 us  [per_device(): jnp.stack([lax.axis_index('cols').astype(jnp.int32), owned_total.astype(j...]
  transfers between devices with their start and end apart: 2 -> 2, of which waited for: 2 -> 2; matrix products, arithmetic and copies ran while one was open for 8% -> 9% of each run, Pallas kernels for 0% -> 0%
where the time goes in v8:
time: 88.1 us; the launch traced here: 87.7 us
  waiting for transfers between devices  34.4 us (39%)
  starting transfers between devices  22.5 us (26%)
  Pallas kernels  11 us (12%)
  local copies, waits for them, and re-layouts  9.37 us (11%)
  blocking collectives  5.55 us (6%)
  matrix products  2.37 us (3%)
  other arithmetic  2.3 us (3%)
    all_to_all x1, waiting for transfers between devices, per_device(): lax.all_to_all(outgoing, 'rows', split_axis=0, concat_axis=0, tiled=True)  23 us
    all_to_all x1, starting transfers between devices, per_device(): lax.all_to_all(outgoing, 'rows', split_axis=0, concat_axis=0, tiled=True)  16.3 us
    all_to_all x1, waiting for transfers between devices, per_device(): lax.all_to_all(bundled, 'rows', split_axis=0, concat_axis=0, tiled=True)  11.4 us
    pallas_call x1, Pallas kernels, cholesky_upper(): pl.pallas_call(cholesky_kernel, out_shape=jax.ShapeDtypeStruct((blocks, s...  8.19 us
    all_to_all x1, starting transfers between devices, per_device(): lax.all_to_all(bundled, 'rows', split_axis=0, concat_axis=0, tiled=True)  6.18 us
    all_gather x1, blocking collectives, per_device(): whole_rows = lax.all_gather(received_rows, 'cols', axis=2, tiled=True)  5.55 us
    gather x7, local copies, waits for them, and re-layouts, per_device(): sample_values = jnp.take_along_axis(samples, picks, axis=1)  5.22 us
    pallas_call x1, Pallas kernels, local_mix(): pl.pallas_call(local_mix_kernel, out_shape=jax.ShapeDtypeStruct((row_devi...  2.84 us
  transfers between devices with their start and end apart: 2, of which 2 were waited for; matrix products, arithmetic and copies ran while one was open for 9% of the time, Pallas kernels for 0%

profile of v8, /device:TPU:1, one launch (start us, length us, event | category | flops | bytes accessed | tf_op | source)
XLA Modules:
  0.0 87.7 jit_solution(9218866771252568204)
XLA Ops:
  0.0 0.0 copy-start
  0.0 2.8 %shard_map.64 = f32[128,16,128]{2,1,0:T(8,128)} custom-call(bf16[64,4096]{1,0:T(8,128)(2,1)} %matrix_ref.1, s32[1,4096]{1,0:T(1,128)} %bitcast.25, bf16[2,64,128]{2,1,0:T(8,128)(2,1)} %constant.100.clone.table_ref), custom_call_target="tpu_custom_call" | custom-call | tf_op jit(solution)/shard_map/pallas_call | solution.py:112
  2.8 16.3 %all-to-all-start = ((f32[128,16,128]{2,1,0:T(8,128)}), f32[128,16,128]{2,1,0:T(8,128)S(1)}, u32[]{:S(2)}, u32[]{:S(2)}) async-start(f32[128,16,128]{2,1,0:T(8,128)} %shard_map.64), calls=%async_computation | async-start | bytes 2097152 | tf_op jit(solution)/shard_map/all_to_all | solution.py:138
  19.2 0.1 copy.58
  19.4 0.1 reshape.400
  19.5 0.0 copy-done
  19.5 4.5 %gather_fusion.1 = s32[512]{0:T(512)S(1)} fusion(s32[256,256]{1,0:T(8,128)S(1)} %copy-done, s32[512]{0:T(512)S(1)} %reshape.400), kind=kCustom, calls=%fused_computation.1 | custom fusion | bytes 8192 | tf_op jit(solution)/shard_map/jit(take_along_axis)/gather | solution.py:148
  24.0 0.1 gather.11
  24.2 0.1 reshape.403
  24.3 0.1 copy.62
  24.5 0.1 copy.63
  24.6 0.1 reshape.394
  24.8 0.0 copy-start.1
  24.8 0.1 copy.59
  24.9 0.0 copy-start.2
  24.9 0.7 copy-done.2
  25.6 0.2 convert_reduce_fusion
  25.7 0.6 multiply_add_fusion
  26.4 23.0 %all-to-all-done = f32[128,16,128]{2,1,0:T(8,128)S(1)} async-done(((f32[128,16,128]{2,1,0:T(8,128)}), f32[128,16,128]{2,1,0:T(8,128)S(1)}, u32[]{:S(2)}, u32[]{:S(2)}) %all-to-all-start) | async-done | bytes 1048608 | tf_op jit(solution)/shard_map/all_to_all | solution.py:138
  49.5 0.0 copy-done.1
  49.5 1.3 %fusion = f32[128,16,128]{2,0,1:T(8,128)S(1)} fusion(f32[128,128,1]{1,0,2:T(8,128)S(1)} %copy-done.1, f32[128,16,128]{2,1,0:T(8,128)S(1)} %all-to-all-done), kind=kOutput, calls=%fused_computation.2 | convolution fusion | flops 402653184 | bytes 2162688 | tf_op jit(solution)/shard_map/st,tvl->svl/dot_general | solution.py:140
  50.8 0.6 copy.61
  51.4 1.0 %gather_fusion = f32[512,128]{1,0:T(8,128)S(1)} fusion(f32[2048,128]{1,0:T(8,128)S(1)} %bitcast.21, s32[1024]{0:T(1024)S(1)} %pad_clamp_fusion), kind=kCustom, calls=%fused_computation | custom fusion | bytes 526336 | tf_op jit(solution)/shard_map/jit(_take)/gather | solution.py:151
  52.4 0.1 copy.64
  52.6 1.1 %fusion.2 = f32[512,128]{1,0:T(8,128)} fusion(f32[256,128]{0,1:T(8,128)S(1)} %bitcast.24, s32[256]{0:T(256)S(1)} %get-tuple-element.8), kind=kOutput, calls=%fused_computation.5 | convolution fusion | flops 201457664 | bytes 394240
  53.7 6.2 %all-to-all-start.1 = ((f32[128,4,128]{2,1,0:T(4,128)}), f32[128,4,128]{2,1,0:T(4,128)S(1)}, u32[]{:S(2)}, u32[]{:S(2)}) async-start(f32[128,4,128]{2,1,0:T(4,128)} %bitcast.12), calls=%async_computation.1 | async-start | bytes 524288 | tf_op jit(solution)/shard_map/all_to_all | solution.py:167
  59.9 1.3 %pad_add_fusion.2.scalar_ref = s32[2]{0:T(128)} fusion(s32[1]{0:T(128)} %bitcast.2, s32[1]{0:T(128)} %bitcast), kind=kLoop, calls=%fused_computation.54 | loop fusion | flops 2 | bytes 16 | tf_op jit(solution)/shard_map/stack | solution.py:171
  61.2 11.4 %all-to-all-done.1 = f32[128,4,128]{2,1,0:T(4,128)S(1)} async-done(((f32[128,4,128]{2,1,0:T(4,128)}), f32[128,4,128]{2,1,0:T(4,128)S(1)}, u32[]{:S(2)}, u32[]{:S(2)}) %all-to-all-start.1) | async-done | bytes 262176 | tf_op jit(solution)/shard_map/all_to_all | solution.py:167
  72.6 0.1 reshape.391
  72.8 0.2 copy.67
  73.0 5.5 %all_gather.3 = f32[4,256,128]{1,0,2:T(4,128)S(1)} all-gather(f32[4,256,64]{1,0,2:T(4,128)S(1)} %copy.67), channel_id=1, replica_groups=mesh['rows'=128,'cols'=2] {'cols'}, dimensions={2}, use_global_device_ids=true | all-gather | bytes 786432 | tf_op jit(solution)/shard_map/all_gather | solution.py:169
  78.5 1.0 %copy.68.rows_ref = f32[4,256,128]{2,1,0:T(8,128)} copy(f32[4,256,128]{1,0,2:T(4,128)S(1)} %all_gather.3) | data formatting | bytes 1048576 | tf_op jit(solution)/shard_map/all_gather | solution.py:169
  79.6 8.2 %shard_map.65 = f32[4,64,128]{2,1,0:T(8,128)} custom-call(s32[2]{0:T(128)} %pad_add_fusion.2.scalar_ref, f32[4,256,128]{2,1,0:T(8,128)} %copy.68.rows_ref), custom_call_target="tpu_custom_call" | custom-call | tf_op jit(solution)/shard_map/pallas_call | solution.py:73
  (10 shorter events, 0.2 us)
Async XLA Ops:
  0.0 19.5 %copy-start = (s32[256,256]{1,0:T(8,128)S(1)}, s32[256,256]{1,0:T(8,128)}, u32[]{:S(2)}) copy-start(s32[256,256]{1,0:T(8,128)} %param.8) | copy-start | bytes 786436
  2.8 46.6 %all-to-all-start = ((f32[128,16,128]{2,1,0:T(8,128)}), f32[128,16,128]{2,1,0:T(8,128)S(1)}, u32[]{:S(2)}, u32[]{:S(2)}) async-start(f32[128,16,128]{2,1,0:T(8,128)} %shard_map.64), calls=%async_computation | async-start | bytes 2097152 | tf_op jit(solution)/shard_map/all_to_all | solution.py:138
  24.8 24.7 %copy-start.1 = (f32[128,128,1]{1,0,2:T(8,128)S(1)}, f32[128,128,1]{1,0,2:T(8,128)}, u32[]{:S(2)}) copy-start(f32[128,128,1]{1,0,2:T(8,128)} %constant.115) | copy-start | bytes 196612
  24.9 0.7 copy-start.2
  53.7 18.9 %all-to-all-start.1 = ((f32[128,4,128]{2,1,0:T(4,128)}), f32[128,4,128]{2,1,0:T(4,128)S(1)}, u32[]{:S(2)}, u32[]{:S(2)}) async-start(f32[128,4,128]{2,1,0:T(4,128)} %bitcast.12), calls=%async_computation.1 | async-start | bytes 524288 | tf_op jit(solution)/shard_map/all_to_all | solution.py:167

commit v9 on v8

--- a/solution.py
+++ b/solution.py
@@ -136,34 +136,43 @@
     table = (walsh_sign_matrix(HB) * scale).reshape(HB // 2, 2, HB).transpose(1, 0, 2)
     outgoing = local_mix(matrix, signs.reshape(1, shard_rows), jnp.asarray(table, jnp.bfloat16), row_devices)
     received = lax.all_to_all(outgoing, "rows", split_axis=0, concat_axis=0, tiled=True)
-    across = jnp.asarray(walsh_sign_matrix(row_devices))
-    mixed = jnp.einsum(
-        "st,tvl->svl", across, received, precision=lax.Precision.HIGHEST
-    ).reshape(row_devices * sub_rows // 2, 2 * slab_width)
-
     block_total = samples.shape[0]
     block_ids = jnp.arange(block_total, dtype=jnp.int32)
-    first_q = jnp.mod(processor_number - block_ids, row_devices)
-    picks = jnp.stack([first_q, first_q + row_devices], axis=1)
-    sample_values = jnp.take_along_axis(samples, picks, axis=1)
-    shard_of = picks // (samples.shape[1] // row_devices)
-    offsets = sample_values - shard_of * shard_rows - processor_number * sub_rows
-    both_halves = jnp.take(mixed, shard_of * (sub_rows // 2) + offsets // 2, axis=0)
-    chosen = jnp.where(
-        (offsets % 2 == 1)[:, :, None], both_halves[:, :, slab_width:], both_halves[:, :, :slab_width]
-    )
-
     owner_list = owners[:, 0]
     preceding_rows = jnp.logical_and(
         owner_list[None, :] == owner_list[:, None], block_ids[None, :] < block_ids[:, None]
     )
     ranks = jnp.sum(preceding_rows.astype(jnp.int32), axis=1)
     slots = owner_list * CAPB + ranks
-    placing = (jnp.arange(row_devices * CAPB, dtype=jnp.int32)[:, None] == slots[None, :]).astype(
-        jnp.float32
+    slot_ids = jnp.arange(row_devices * CAPB, dtype=jnp.int32)
+    match = slots[None, :] == slot_ids[:, None]
+    filled = jnp.any(match, axis=1)
+
+    first_q = jnp.mod(processor_number - block_ids, row_devices)
+    sample_pos = jnp.arange(samples.shape[1], dtype=jnp.int32)
+    per_shard = samples.shape[1] // row_devices
+    row_parts, parity_parts = [], []
+    for half in range(per_shard):
+        q = first_q + half * row_devices
+        value = jnp.sum(jnp.where(sample_pos[None, :] == q[:, None], samples, 0), axis=1)
+        shard = q // per_shard
+        offset = value - shard * shard_rows - processor_number * sub_rows
+        row = jnp.sum(jnp.where(match, (shard * (sub_rows // 2) + offset // 2)[None, :], 0), axis=1)
+        parity = jnp.sum(jnp.where(match, (offset % 2)[None, :], 0), axis=1)
+        row_parts.append(row)
+        parity_parts.append(parity)
+    slot_rows = jnp.stack(row_parts, axis=1)
+    slot_parity = jnp.stack(parity_parts, axis=1)
+
+    across = jnp.asarray(walsh_sign_matrix(row_devices))
+    mixed = jnp.einsum(
+        "st,tvl->svl", across, received, precision=lax.Precision.HIGHEST
+    ).reshape(row_devices * sub_rows // 2, 2 * slab_width)
+    both_halves = jnp.take(mixed, slot_rows, axis=0)
+    chosen = jnp.where(
+        (slot_parity == 1)[:, :, None], both_halves[:, :, slab_width:], both_halves[:, :, :slab_width]
     )
-    bundled = jnp.einsum("kb,bps->kps", placing, chosen, precision=lax.Precision.HIGHEST)
-    bundled = bundled.reshape(row_devices, CAPB, 2 * slab_width)
+    bundled = jnp.where(filled[:, None, None], chosen, 0.0).reshape(row_devices, CAPB, per_shard * slab_width)
     arriving = lax.all_to_all(bundled, "rows", split_axis=0, concat_axis=0, tiled=True)
     received_rows = jnp.transpose(arriving, (1, 0, 2)).reshape(CAPB, row_devices * 2, slab_width)
     whole_rows = lax.all_gather(received_rows, "cols", axis=2, tiled=True)

time: 88.1 us -> 93.3 us (1.059)
  other arithmetic: 2.3 us -> 6.64 us
  waiting for transfers between devices: 34.4 us -> 38.5 us
  local copies, waits for them, and re-layouts: 9.37 us -> 7.28 us
  matrix products: 2.37 us -> 1.28 us
    all_to_all x1, waiting for transfers between devices: 23 us -> 27.1 us  [per_device(): lax.all_to_all(outgoing, 'rows', split_axis=0, concat_axis=0, tiled=True)]
    gather x9 -> x1, local copies, waits for them, and re-layouts: 6.4 us -> 2.81 us  [per_device(): both_halves = jnp.take(mixed, slot_rows, axis=0)]
    select_n x3 -> x4, other arithmetic: 0.09 us -> 3.63 us  [the longest x1 1.97 us: per_device(): jnp.where(filled[:, None, None], chosen, 0.0)]
    unnamed x1 -> x0, matrix products: 1.09 us -> none
    reshape x0 -> x1, local copies, waits for them, and re-layouts: none -> 1.08 us  [per_device(): jnp.where(filled[:, None, None], chosen, 0.0)]
  transfers between devices with their start and end apart: 2 -> 2, of which waited for: 2 -> 2; matrix products, arithmetic and copies ran while one was open for 9% -> 4% of each run, Pallas kernels for 0% -> 0%
where the time goes in v9:
time: 93.3 us; the launch traced here: 93 us
  waiting for transfers between devices  38.5 us (41%)
  starting transfers between devices  22.6 us (24%)
  Pallas kernels  11 us (12%)
  local copies, waits for them, and re-layouts  7.28 us (8%)
  other arithmetic  6.64 us (7%)
  blocking collectives  5.55 us (6%)
  matrix products  1.28 us (1%)
    all_to_all x1, waiting for transfers between devices, per_device(): lax.all_to_all(outgoing, 'rows', split_axis=0, concat_axis=0, tiled=True)  27.1 us
    all_to_all x1, starting transfers between devices, per_device(): lax.all_to_all(outgoing, 'rows', split_axis=0, concat_axis=0, tiled=True)  16.5 us
    all_to_all x1, waiting for transfers between devices, per_device(): lax.all_to_all(bundled, 'rows', split_axis=0, concat_axis=0, tiled=True)  11.4 us
    pallas_call x1, Pallas kernels, cholesky_upper(): pl.pallas_call(cholesky_kernel, out_shape=jax.ShapeDtypeStruct((blocks, s...  8.19 us
    all_to_all x1, starting transfers between devices, per_device(): lax.all_to_all(bundled, 'rows', split_axis=0, concat_axis=0, tiled=True)  6.17 us
    all_gather x1, blocking collectives, per_device(): whole_rows = lax.all_gather(received_rows, 'cols', axis=2, tiled=True)  5.55 us
    gather x1, local copies, waits for them, and re-layouts, per_device(): both_halves = jnp.take(mixed, slot_rows, axis=0)  2.81 us
    pallas_call x1, Pallas kernels, local_mix(): pl.pallas_call(local_mix_kernel, out_shape=jax.ShapeDtypeStruct((row_devi...  2.81 us
  transfers between devices with their start and end apart: 2, of which 2 were waited for; matrix products, arithmetic and copies ran while one was open for 4% of the time, Pallas kernels for 0%

profile of v9, /device:TPU:1, one launch (start us, length us, event | category | flops | bytes accessed | tf_op | source)
XLA Modules:
  0.0 93.0 jit_solution(5125812984218115176)
XLA Ops:
  0.0 2.8 %shard_map.64 = f32[128,16,128]{2,1,0:T(8,128)} custom-call(bf16[64,4096]{1,0:T(8,128)(2,1)} %matrix_ref.1, s32[1,4096]{1,0:T(1,128)} %bitcast.24, bf16[2,64,128]{2,1,0:T(8,128)(2,1)} %constant.107.clone.table_ref), custom_call_target="tpu_custom_call" | custom-call | tf_op jit(solution)/shard_map/pallas_call | solution.py:112
  2.8 0.0 copy-start
  2.8 16.5 %all-to-all-start = ((f32[128,16,128]{2,1,0:T(8,128)}), f32[128,16,128]{2,1,0:T(8,128)S(1)}, u32[]{:S(2)}, u32[]{:S(2)}) async-start(f32[128,16,128]{2,1,0:T(8,128)} %shard_map.64), calls=%async_computation | async-start | bytes 2097152 | tf_op jit(solution)/shard_map/all_to_all | solution.py:138
  19.3 0.0 copy-start.2
  19.3 0.7 copy-done.2
  20.0 0.2 convert_reduce_fusion
  20.2 0.0 copy-done
  20.2 0.3 select_reduce_fusion.5
  20.4 0.6 multiply_add_fusion
  21.1 0.4 select_reduce_fusion.3
  21.5 0.1 copy.26
  21.7 0.2 reshape.282
  21.9 0.0 copy-start.1
  21.9 0.2 copy.23
  22.1 0.2 copy.22
  22.3 0.2 fusion.3
  22.5 27.1 %all-to-all-done = f32[128,16,128]{2,1,0:T(8,128)S(1)} async-done(((f32[128,16,128]{2,1,0:T(8,128)}), f32[128,16,128]{2,1,0:T(8,128)S(1)}, u32[]{:S(2)}, u32[]{:S(2)}) %all-to-all-start) | async-done | bytes 1048608 | tf_op jit(solution)/shard_map/all_to_all | solution.py:138
  49.6 0.0 copy-done.1
  49.6 1.3 %fusion = f32[128,16,128]{2,0,1:T(8,128)S(1)} fusion(f32[128,128,1]{1,0,2:T(8,128)S(1)} %copy-done.1, f32[128,16,128]{2,1,0:T(8,128)S(1)} %all-to-all-done), kind=kOutput, calls=%fused_computation.1 | convolution fusion | flops 402653184 | bytes 2162688 | tf_op jit(solution)/shard_map/st,tvl->svl/dot_general | solution.py:168
  50.9 0.6 copy.25
  51.5 2.8 %gather_fusion = f32[1024,128]{1,0:T(8,128)S(1)} fusion(f32[2048,128]{1,0:T(8,128)S(1)} %bitcast.17, s32[1024]{0:T(1024)S(1)} %broadcast_clamp_fusion), kind=kCustom, calls=%fused_computation | custom fusion | bytes 1052672 | tf_op jit(solution)/shard_map/jit(_take)/gather | solution.py:171
  54.3 1.6 %broadcast_select_fusion = f32[512,2,128]{2,1,0:T(2,128)S(1)} fusion(f32[512,2,128]{2,1,0:T(2,128)S(1)} %bitcast.18, pred[512,2]{1,0:T(8,128)(4,1)S(1)} %copy.23), kind=kLoop, calls=%fused_computation.11 | loop fusion | flops 131072 | bytes 1049600 | tf_op jit(solution)/shard_map/jit(_take)/select_n | solution.py:171
  55.9 2.0 %fusion.2 = f32[512,2,64]{2,1,0:T(2,128)S(1)} fusion(f32[512,2,128]{2,1,0:T(2,128)S(1)} %broadcast_select_fusion, pred[512]{0:T(512)(128)(4,1)S(1)} %fusion.3, pred[512,2]{1,0:T(8,128)(4,1)S(1)} %copy.22), kind=kLoop, calls=%fused_computation.4 | loop fusion | flops 131072 | bytes 787968 | tf_op jit(solution)/shard_map/jit(_where)/select_n | solution.py:175
  57.9 1.1 %reshape.278 = f32[128,4,128]{2,1,0:T(4,128)} reshape(f32[512,2,64]{2,1,0:T(2,128)S(1)} %fusion.2) | data formatting | bytes 524288 | tf_op jit(solution)/shard_map/reshape | solution.py:175
  59.0 6.2 %all-to-all-start.1 = ((f32[128,4,128]{2,1,0:T(4,128)}), f32[128,4,128]{2,1,0:T(4,128)S(1)}, u32[]{:S(2)}, u32[]{:S(2)}) async-start(f32[128,4,128]{2,1,0:T(4,128)} %reshape.278), calls=%async_computation.1 | async-start | bytes 524288 | tf_op jit(solution)/shard_map/all_to_all | solution.py:176
  65.2 1.3 %pad_add_fusion.scalar_ref = s32[2]{0:T(128)} fusion(s32[1]{0:T(128)} %bitcast.2, s32[1]{0:T(128)} %bitcast), kind=kLoop, calls=%fused_computation.53 | loop fusion | flops 2 | bytes 16 | tf_op jit(solution)/shard_map/stack | solution.py:180
  66.5 11.4 %all-to-all-done.1 = f32[128,4,128]{2,1,0:T(4,128)S(1)} async-done(((f32[128,4,128]{2,1,0:T(4,128)}), f32[128,4,128]{2,1,0:T(4,128)S(1)}, u32[]{:S(2)}, u32[]{:S(2)}) %all-to-all-start.1) | async-done | bytes 262176 | tf_op jit(solution)/shard_map/all_to_all | solution.py:176
  77.9 0.1 reshape.279
  78.0 0.2 copy.28
  78.3 5.5 %all_gather.3 = f32[4,256,128]{1,0,2:T(4,128)S(1)} all-gather(f32[4,256,64]{1,0,2:T(4,128)S(1)} %copy.28), channel_id=1, replica_groups=mesh['rows'=128,'cols'=2] {'cols'}, dimensions={2}, use_global_device_ids=true | all-gather | bytes 786432 | tf_op jit(solution)/shard_map/all_gather | solution.py:178
  83.8 1.0 %copy.29.rows_ref = f32[4,256,128]{2,1,0:T(8,128)} copy(f32[4,256,128]{1,0,2:T(4,128)S(1)} %all_gather.3) | data formatting | bytes 1048576 | tf_op jit(solution)/shard_map/all_gather | solution.py:178
  84.8 8.2 %shard_map.65 = f32[4,64,128]{2,1,0:T(8,128)} custom-call(s32[2]{0:T(128)} %pad_add_fusion.scalar_ref, f32[4,256,128]{2,1,0:T(8,128)} %copy.29.rows_ref), custom_call_target="tpu_custom_call" | custom-call | tf_op jit(solution)/shard_map/pallas_call | solution.py:73
  (8 shorter events, 0.1 us)
Async XLA Ops:
  2.8 17.4 %copy-start = (s32[256,256]{1,0:T(8,128)S(1)}, s32[256,256]{1,0:T(8,128)}, u32[]{:S(2)}) copy-start(s32[256,256]{1,0:T(8,128)} %param.8) | copy-start | bytes 786436
  2.8 46.8 %all-to-all-start = ((f32[128,16,128]{2,1,0:T(8,128)}), f32[128,16,128]{2,1,0:T(8,128)S(1)}, u32[]{:S(2)}, u32[]{:S(2)}) async-start(f32[128,16,128]{2,1,0:T(8,128)} %shard_map.64), calls=%async_computation | async-start | bytes 2097152 | tf_op jit(solution)/shard_map/all_to_all | solution.py:138
  19.3 0.7 copy-start.2
  21.9 27.7 %copy-start.1 = (f32[128,128,1]{1,0,2:T(8,128)S(1)}, f32[128,128,1]{1,0,2:T(8,128)}, u32[]{:S(2)}) copy-start(f32[128,128,1]{1,0,2:T(8,128)} %constant.109) | copy-start | bytes 196612
  59.0 18.9 %all-to-all-start.1 = ((f32[128,4,128]{2,1,0:T(4,128)}), f32[128,4,128]{2,1,0:T(4,128)S(1)}, u32[]{:S(2)}, u32[]{:S(2)}) async-start(f32[128,4,128]{2,1,0:T(4,128)} %reshape.278), calls=%async_computation.1 | async-start | bytes 524288 | tf_op jit(solution)/shard_map/all_to_all | solution.py:176

commit v10 on v8

--- a/solution.py
+++ b/solution.py
@@ -13,22 +13,35 @@
 CAPB = 4
 
 PANEL = 32
+SAMPLES_PER_SHARD = 2
 STEP = 8
 
 
 def cholesky_kernel(scalar_ref, rows_ref, out_ref, work_ref):
-    blocks, samples, order = rows_ref.shape
+    cores, blocks, sources, lanes = rows_ref.shape
+    width = lanes // SAMPLES_PER_SHARD
+    order = cores * width
+    samples = sources * SAMPLES_PER_SHARD
+    diagonal = (
+        lax.broadcasted_iota(jnp.int32, (width, width), 0)
+        == lax.broadcasted_iota(jnp.int32, (width, width), 1)
+    )
     for b in range(blocks):
-        gram = lax.dot_general(
-            rows_ref[b], rows_ref[b], (((0,), (0,)), ((), ())),
-            precision=lax.Precision.HIGHEST, preferred_element_type=jnp.float32,
-        ) / samples
-        diagonal = (
-            lax.broadcasted_iota(jnp.int32, (order, order), 0)
-            == lax.broadcasted_iota(jnp.int32, (order, order), 1)
-        )
-        identity = jnp.where(diagonal, 1.0, 0.0)
-        work_ref[b] = jnp.where(b < scalar_ref[1], gram, identity)
+        for left in range(cores):
+            for right in range(cores):
+                product = None
+                for j in range(SAMPLES_PER_SHARD):
+                    term = lax.dot_general(
+                        rows_ref[left, b, :, j * width:(j + 1) * width],
+                        rows_ref[right, b, :, j * width:(j + 1) * width],
+                        (((0,), (0,)), ((), ())),
+                        precision=lax.Precision.HIGHEST, preferred_element_type=jnp.float32,
+                    )
+                    product = term if product is None else product + term
+                fill = jnp.where(diagonal, 1.0, 0.0) if left == right else jnp.zeros((width, width), jnp.float32)
+                work_ref[b, left * width:(left + 1) * width, right * width:(right + 1) * width] = jnp.where(
+                    b < scalar_ref[1], product / samples, fill
+                )
     lane = lax.broadcasted_iota(jnp.int32, (blocks, 1, order), 2)
     sub_panel = lax.broadcasted_iota(jnp.int32, (blocks, PANEL, order), 1)
     for p in range(order // PANEL):
@@ -69,7 +82,8 @@
 
 
 def cholesky_upper(scalars, whole_rows, slab_width):
-    blocks, samples, order = whole_rows.shape
+    cores, blocks, _, lanes = whole_rows.shape
+    order = cores * slab_width
     return pl.pallas_call(
         cholesky_kernel,
         out_shape=jax.ShapeDtypeStruct((blocks, slab_width, order), jnp.float32),
@@ -163,10 +177,9 @@
         jnp.float32
     )
     bundled = jnp.einsum("kb,bps->kps", placing, chosen, precision=lax.Precision.HIGHEST)
-    bundled = bundled.reshape(row_devices, CAPB, 2 * slab_width)
-    arriving = lax.all_to_all(bundled, "rows", split_axis=0, concat_axis=0, tiled=True)
-    received_rows = jnp.transpose(arriving, (1, 0, 2)).reshape(CAPB, row_devices * 2, slab_width)
-    whole_rows = lax.all_gather(received_rows, "cols", axis=2, tiled=True)
+    bundled = bundled.reshape(row_devices, CAPB, 2 * slab_width).transpose(1, 0, 2)
+    arriving = lax.all_to_all(bundled, "rows", split_axis=1, concat_axis=1, tiled=True)
+    whole_rows = lax.all_gather(arriving, "cols", axis=0, tiled=False)
     owned_total = jnp.sum((owner_list == processor_number).astype(jnp.int32))
     scalars = jnp.stack([lax.axis_index("cols").astype(jnp.int32), owned_total.astype(jnp.int32)])
     return cholesky_upper(scalars, whole_rows, slab_width)

time: 88.1 us -> 88.6 us (level)
  Pallas kernels: 11 us -> 12.8 us
  local copies, waits for them, and re-layouts: 9.37 us -> 8 us
    pallas_call x1, Pallas kernels: 8.19 us -> 9.95 us  [cholesky_upper(): pl.pallas_call(cholesky_kernel, out_shape=jax.ShapeDtypeStruct((blocks, s...]
    all_gather x1 -> x0, local copies, waits for them, and re-layouts: 1.02 us -> none  [per_device(): whole_rows = lax.all_gather(received_rows, 'cols', axis=2, tiled=True)]
where the time goes in v10:
time: 88.6 us; the launch traced here: 88.2 us
  waiting for transfers between devices  34.4 us (39%)
  starting transfers between devices  22.5 us (25%)
  Pallas kernels  12.8 us (14%)
  local copies, waits for them, and re-layouts  8 us (9%)
  blocking collectives  5.68 us (6%)
  matrix products  2.37 us (3%)
  other arithmetic  2.3 us (3%)
    all_to_all x1, waiting for transfers between devices, per_device(): lax.all_to_all(outgoing, 'rows', split_axis=0, concat_axis=0, tiled=True)  23 us
    all_to_all x1, starting transfers between devices, per_device(): lax.all_to_all(outgoing, 'rows', split_axis=0, concat_axis=0, tiled=True)  16.3 us
    all_to_all x1, waiting for transfers between devices, per_device(): lax.all_to_all(bundled, 'rows', split_axis=1, concat_axis=1, tiled=True)  11.4 us
    pallas_call x1, Pallas kernels, cholesky_upper(): pl.pallas_call(cholesky_kernel, out_shape=jax.ShapeDtypeStruct((blocks, s...  9.95 us
    all_to_all x1, starting transfers between devices, per_device(): lax.all_to_all(bundled, 'rows', split_axis=1, concat_axis=1, tiled=True)  6.18 us
    all_gather x1, blocking collectives, per_device(): whole_rows = lax.all_gather(arriving, 'cols', axis=0, tiled=False)  5.68 us
    gather x7, local copies, waits for them, and re-layouts, per_device(): sample_values = jnp.take_along_axis(samples, picks, axis=1)  5.22 us
    pallas_call x1, Pallas kernels, local_mix(): pl.pallas_call(local_mix_kernel, out_shape=jax.ShapeDtypeStruct((row_devi...  2.84 us
  transfers between devices with their start and end apart: 2, of which 2 were waited for; matrix products, arithmetic and copies ran while one was open for 9% of the time, Pallas kernels for 0%

profile of v10, /device:TPU:1, one launch (start us, length us, event | category | flops | bytes accessed | tf_op | source)
XLA Modules:
  0.0 88.2 jit_solution(622451428236733254)
XLA Ops:
  0.0 0.0 copy-start
  0.0 2.8 %shard_map.64 = f32[128,16,128]{2,1,0:T(8,128)} custom-call(bf16[64,4096]{1,0:T(8,128)(2,1)} %matrix_ref.1, s32[1,4096]{1,0:T(1,128)} %bitcast.27, bf16[2,64,128]{2,1,0:T(8,128)(2,1)} %constant.100.clone.table_ref), custom_call_target="tpu_custom_call" | custom-call | tf_op jit(solution)/shard_map/pallas_call | solution.py:126
  2.8 16.3 %all-to-all-start = ((f32[128,16,128]{2,1,0:T(8,128)}), f32[128,16,128]{2,1,0:T(8,128)S(1)}, u32[]{:S(2)}, u32[]{:S(2)}) async-start(f32[128,16,128]{2,1,0:T(8,128)} %shard_map.64), calls=%async_computation | async-start | bytes 2097152 | tf_op jit(solution)/shard_map/all_to_all | solution.py:152
  19.2 0.1 copy.54
  19.4 0.1 reshape.396
  19.5 0.0 copy-done
  19.5 4.5 %gather_fusion.1 = s32[512]{0:T(512)S(1)} fusion(s32[256,256]{1,0:T(8,128)S(1)} %copy-done, s32[512]{0:T(512)S(1)} %reshape.396), kind=kCustom, calls=%fused_computation.1 | custom fusion | bytes 8192 | tf_op jit(solution)/shard_map/jit(take_along_axis)/gather | solution.py:162
  24.0 0.1 gather.11
  24.2 0.1 reshape.399
  24.3 0.1 copy.58
  24.5 0.1 copy.59
  24.6 0.1 reshape.390
  24.8 0.0 copy-start.1
  24.8 0.1 copy.55
  24.9 0.0 copy-start.2
  24.9 0.7 copy-done.2
  25.6 0.2 convert_reduce_fusion
  25.7 0.6 multiply_add_fusion
  26.4 23.0 %all-to-all-done = f32[128,16,128]{2,1,0:T(8,128)S(1)} async-done(((f32[128,16,128]{2,1,0:T(8,128)}), f32[128,16,128]{2,1,0:T(8,128)S(1)}, u32[]{:S(2)}, u32[]{:S(2)}) %all-to-all-start) | async-done | bytes 1048608 | tf_op jit(solution)/shard_map/all_to_all | solution.py:152
  49.5 0.0 copy-done.1
  49.5 1.3 %fusion = f32[128,16,128]{2,0,1:T(8,128)S(1)} fusion(f32[128,128,1]{1,0,2:T(8,128)S(1)} %copy-done.1, f32[128,16,128]{2,1,0:T(8,128)S(1)} %all-to-all-done), kind=kOutput, calls=%fused_computation.2 | convolution fusion | flops 402653184 | bytes 2162688 | tf_op jit(solution)/shard_map/st,tvl->svl/dot_general | solution.py:154
  50.8 0.6 copy.57
  51.4 1.0 %gather_fusion = f32[512,128]{1,0:T(8,128)S(1)} fusion(f32[2048,128]{1,0:T(8,128)S(1)} %bitcast.23, s32[1024]{0:T(1024)S(1)} %pad_clamp_fusion), kind=kCustom, calls=%fused_computation | custom fusion | bytes 526336 | tf_op jit(solution)/shard_map/jit(_take)/gather | solution.py:165
  52.4 0.1 copy.60
  52.6 1.1 %fusion.2 = f32[512,128]{1,0:T(8,128)} fusion(f32[256,128]{0,1:T(8,128)S(1)} %bitcast.26, s32[256]{0:T(256)S(1)} %get-tuple-element.8), kind=kOutput, calls=%fused_computation.5 | convolution fusion | flops 201457664 | bytes 394240
  53.7 6.2 %all-to-all-start.1 = ((f32[4,128,128]{2,0,1:T(4,128)}), f32[4,128,128]{2,0,1:T(4,128)S(1)}, u32[]{:S(2)}, u32[]{:S(2)}) async-start(f32[4,128,128]{2,0,1:T(4,128)} %bitcast.11), calls=%async_computation.1 | async-start | bytes 524288 | tf_op jit(solution)/shard_map/all_to_all | solution.py:181
  59.9 1.3 %pad_add_fusion.2.scalar_ref = s32[2]{0:T(128)} fusion(s32[1]{0:T(128)} %bitcast.2, s32[1]{0:T(128)} %bitcast), kind=kLoop, calls=%fused_computation.54 | loop fusion | flops 2 | bytes 16 | tf_op jit(solution)/shard_map/stack | solution.py:184
  61.2 11.4 %all-to-all-done.1 = f32[4,128,128]{2,0,1:T(4,128)S(1)} async-done(((f32[4,128,128]{2,0,1:T(4,128)}), f32[4,128,128]{2,0,1:T(4,128)S(1)}, u32[]{:S(2)}, u32[]{:S(2)}) %all-to-all-start.1) | async-done | bytes 262176 | tf_op jit(solution)/shard_map/all_to_all | solution.py:181
  72.6 5.7 %all-gather = f32[8,128,128]{2,1,0:T(8,128)} all-gather(f32[4,128,128]{2,1,0:T(8,128)S(1)} %copy.62), channel_id=2, replica_groups=mesh['rows'=128,'cols'=2] {'cols'}, dimensions={0}, use_global_device_ids=true | all-gather | bytes 786432 | tf_op jit(solution)/shard_map/all_gather | solution.py:182
  78.3 9.9 %shard_map.65 = f32[4,64,128]{2,1,0:T(8,128)} custom-call(s32[2]{0:T(128)} %pad_add_fusion.2.scalar_ref, f32[2,4,128,128]{3,2,1,0:T(8,128)} %bitcast.24), custom_call_target="tpu_custom_call" | custom-call | tf_op jit(solution)/shard_map/pallas_call | solution.py:87
  (10 shorter events, 0.2 us)
Async XLA Ops:
  0.0 19.5 %copy-start = (s32[256,256]{1,0:T(8,128)S(1)}, s32[256,256]{1,0:T(8,128)}, u32[]{:S(2)}) copy-start(s32[256,256]{1,0:T(8,128)} %param.8) | copy-start | bytes 786436
  2.8 46.6 %all-to-all-start = ((f32[128,16,128]{2,1,0:T(8,128)}), f32[128,16,128]{2,1,0:T(8,128)S(1)}, u32[]{:S(2)}, u32[]{:S(2)}) async-start(f32[128,16,128]{2,1,0:T(8,128)} %shard_map.64), calls=%async_computation | async-start | bytes 2097152 | tf_op jit(solution)/shard_map/all_to_all | solution.py:152
  24.8 24.7 %copy-start.1 = (f32[128,128,1]{1,0,2:T(8,128)S(1)}, f32[128,128,1]{1,0,2:T(8,128)}, u32[]{:S(2)}) copy-start(f32[128,128,1]{1,0,2:T(8,128)} %constant.115) | copy-start | bytes 196612
  24.9 0.7 copy-start.2
  53.7 18.9 %all-to-all-start.1 = ((f32[4,128,128]{2,0,1:T(4,128)}), f32[4,128,128]{2,0,1:T(4,128)S(1)}, u32[]{:S(2)}, u32[]{:S(2)}) async-start(f32[4,128,128]{2,0,1:T(4,128)} %bitcast.11), calls=%async_computation.1 | async-start | bytes 524288 | tf_op jit(solution)/shard_map/all_to_all | solution.py:181

commit v11 on v8

--- a/solution.py
+++ b/solution.py
@@ -106,14 +106,20 @@
     lax.fori_loop(0, matrix_ref.shape[1] // HB, body, 0, unroll=True)
 
 
-def local_mix(matrix, signs, table, row_devices):
+def local_mix(matrix, signs, table, row_devices, steps=4):
     slab_width, shard_rows = matrix.shape
     sub_rows = shard_rows // row_devices
+    span = shard_rows // steps
     return pl.pallas_call(
         local_mix_kernel,
         out_shape=jax.ShapeDtypeStruct((row_devices, sub_rows // 2, 2 * slab_width), jnp.float32),
-        in_specs=[pl.BlockSpec(memory_space=pltpu.VMEM)] * 3,
-        out_specs=pl.BlockSpec(memory_space=pltpu.VMEM),
+        grid=(steps,),
+        in_specs=[
+            pl.BlockSpec((slab_width, span), lambda i: (0, i)),
+            pl.BlockSpec((1, span), lambda i: (0, i)),
+            pl.BlockSpec(table.shape, lambda i: (0, 0, 0)),
+        ],
+        out_specs=pl.BlockSpec((row_devices // steps, sub_rows // 2, 2 * slab_width), lambda i: (i, 0, 0)),
     )(matrix, signs, table)
 
 

time: 88.1 us -> 89.3 us (1.014)
  Pallas kernels: 11 us -> 12.2 us
    pallas_call x1, Pallas kernels: 2.84 us -> 3.97 us  [local_mix(): pl.pallas_call(local_mix_kernel, out_shape=jax.ShapeDtypeStruct((row_devi...]
where the time goes in v11:
time: 89.3 us; the launch traced here: 88.9 us
  waiting for transfers between devices  34.4 us (39%)
  starting transfers between devices  22.5 us (25%)
  Pallas kernels  12.2 us (14%)
  local copies, waits for them, and re-layouts  9.37 us (10%)
  blocking collectives  5.55 us (6%)
  matrix products  2.37 us (3%)
  other arithmetic  2.3 us (3%)
    all_to_all x1, waiting for transfers between devices, per_device(): lax.all_to_all(outgoing, 'rows', split_axis=0, concat_axis=0, tiled=True)  23 us
    all_to_all x1, starting transfers between devices, per_device(): lax.all_to_all(outgoing, 'rows', split_axis=0, concat_axis=0, tiled=True)  16.3 us
    all_to_all x1, waiting for transfers between devices, per_device(): lax.all_to_all(bundled, 'rows', split_axis=0, concat_axis=0, tiled=True)  11.4 us
    pallas_call x1, Pallas kernels, cholesky_upper(): pl.pallas_call(cholesky_kernel, out_shape=jax.ShapeDtypeStruct((blocks, s...  8.19 us
    all_to_all x1, starting transfers between devices, per_device(): lax.all_to_all(bundled, 'rows', split_axis=0, concat_axis=0, tiled=True)  6.18 us
    all_gather x1, blocking collectives, per_device(): whole_rows = lax.all_gather(received_rows, 'cols', axis=2, tiled=True)  5.55 us
    gather x7, local copies, waits for them, and re-layouts, per_device(): sample_values = jnp.take_along_axis(samples, picks, axis=1)  5.22 us
    pallas_call x1, Pallas kernels, local_mix(): pl.pallas_call(local_mix_kernel, out_shape=jax.ShapeDtypeStruct((row_devi...  3.97 us
  transfers between devices with their start and end apart: 2, of which 2 were waited for; matrix products, arithmetic and copies ran while one was open for 9% of the time, Pallas kernels for 0%

profile of v11, /device:TPU:1, one launch (start us, length us, event | category | flops | bytes accessed | tf_op | source)
XLA Modules:
  0.0 88.9 jit_solution(10421180626287143343)
XLA Ops:
  0.0 0.0 copy-start
  0.0 4.0 %shard_map.64 = f32[128,16,128]{2,1,0:T(8,128)} custom-call(bf16[64,4096]{1,0:T(8,128)(2,1)} %matrix_ref.1, s32[1,4096]{1,0:T(1,128)} %bitcast.25, bf16[2,64,128]{2,1,0:T(8,128)(2,1)} %constant.100.clone.table_ref), custom_call_target="tpu_custom_call" | custom-call | tf_op jit(solution)/shard_map/pallas_call | solution.py:113
  4.0 16.3 %all-to-all-start = ((f32[128,16,128]{2,1,0:T(8,128)}), f32[128,16,128]{2,1,0:T(8,128)S(1)}, u32[]{:S(2)}, u32[]{:S(2)}) async-start(f32[128,16,128]{2,1,0:T(8,128)} %shard_map.64), calls=%async_computation | async-start | bytes 2097152 | tf_op jit(solution)/shard_map/all_to_all | solution.py:144
  20.4 0.1 copy.58
  20.5 0.1 reshape.400
  20.6 0.0 copy-done
  20.7 4.5 %gather_fusion.1 = s32[512]{0:T(512)S(1)} fusion(s32[256,256]{1,0:T(8,128)S(1)} %copy-done, s32[512]{0:T(512)S(1)} %reshape.400), kind=kCustom, calls=%fused_computation.1 | custom fusion | bytes 8192 | tf_op jit(solution)/shard_map/jit(take_along_axis)/gather | solution.py:154
  25.2 0.1 gather.11
  25.3 0.1 reshape.403
  25.5 0.1 copy.62
  25.6 0.1 copy.63
  25.7 0.1 reshape.394
  25.9 0.0 copy-start.1
  25.9 0.1 copy.59
  26.0 0.0 copy-start.2
  26.0 0.7 copy-done.2
  26.7 0.2 convert_reduce_fusion
  26.9 0.6 multiply_add_fusion
  27.6 23.0 %all-to-all-done = f32[128,16,128]{2,1,0:T(8,128)S(1)} async-done(((f32[128,16,128]{2,1,0:T(8,128)}), f32[128,16,128]{2,1,0:T(8,128)S(1)}, u32[]{:S(2)}, u32[]{:S(2)}) %all-to-all-start) | async-done | bytes 1048608 | tf_op jit(solution)/shard_map/all_to_all | solution.py:144
  50.6 0.0 copy-done.1
  50.6 1.3 %fusion = f32[128,16,128]{2,0,1:T(8,128)S(1)} fusion(f32[128,128,1]{1,0,2:T(8,128)S(1)} %copy-done.1, f32[128,16,128]{2,1,0:T(8,128)S(1)} %all-to-all-done), kind=kOutput, calls=%fused_computation.2 | convolution fusion | flops 402653184 | bytes 2162688 | tf_op jit(solution)/shard_map/st,tvl->svl/dot_general | solution.py:146
  51.9 0.6 copy.61
  52.5 1.0 %gather_fusion = f32[512,128]{1,0:T(8,128)S(1)} fusion(f32[2048,128]{1,0:T(8,128)S(1)} %bitcast.21, s32[1024]{0:T(1024)S(1)} %pad_clamp_fusion), kind=kCustom, calls=%fused_computation | custom fusion | bytes 526336 | tf_op jit(solution)/shard_map/jit(_take)/gather | solution.py:157
  53.6 0.1 copy.64
  53.8 1.1 %fusion.2 = f32[512,128]{1,0:T(8,128)} fusion(f32[256,128]{0,1:T(8,128)S(1)} %bitcast.24, s32[256]{0:T(256)S(1)} %get-tuple-element.8), kind=kOutput, calls=%fused_computation.5 | convolution fusion | flops 201457664 | bytes 394240
  54.9 6.2 %all-to-all-start.1 = ((f32[128,4,128]{2,1,0:T(4,128)}), f32[128,4,128]{2,1,0:T(4,128)S(1)}, u32[]{:S(2)}, u32[]{:S(2)}) async-start(f32[128,4,128]{2,1,0:T(4,128)} %bitcast.12), calls=%async_computation.1 | async-start | bytes 524288 | tf_op jit(solution)/shard_map/all_to_all | solution.py:173
  61.1 1.3 %pad_add_fusion.2.scalar_ref = s32[2]{0:T(128)} fusion(s32[1]{0:T(128)} %bitcast.2, s32[1]{0:T(128)} %bitcast), kind=kLoop, calls=%fused_computation.54 | loop fusion | flops 2 | bytes 16 | tf_op jit(solution)/shard_map/stack | solution.py:177
  62.4 11.4 %all-to-all-done.1 = f32[128,4,128]{2,1,0:T(4,128)S(1)} async-done(((f32[128,4,128]{2,1,0:T(4,128)}), f32[128,4,128]{2,1,0:T(4,128)S(1)}, u32[]{:S(2)}, u32[]{:S(2)}) %all-to-all-start.1) | async-done | bytes 262176 | tf_op jit(solution)/shard_map/all_to_all | solution.py:173
  73.8 0.1 reshape.391
  73.9 0.2 copy.67
  74.1 5.5 %all_gather.3 = f32[4,256,128]{1,0,2:T(4,128)S(1)} all-gather(f32[4,256,64]{1,0,2:T(4,128)S(1)} %copy.67), channel_id=1, replica_groups=mesh['rows'=128,'cols'=2] {'cols'}, dimensions={2}, use_global_device_ids=true | all-gather | bytes 786432 | tf_op jit(solution)/shard_map/all_gather | solution.py:175
  79.7 1.0 %copy.68.rows_ref = f32[4,256,128]{2,1,0:T(8,128)} copy(f32[4,256,128]{1,0,2:T(4,128)S(1)} %all_gather.3) | data formatting | bytes 1048576 | tf_op jit(solution)/shard_map/all_gather | solution.py:175
  80.7 8.2 %shard_map.65 = f32[4,64,128]{2,1,0:T(8,128)} custom-call(s32[2]{0:T(128)} %pad_add_fusion.2.scalar_ref, f32[4,256,128]{2,1,0:T(8,128)} %copy.68.rows_ref), custom_call_target="tpu_custom_call" | custom-call | tf_op jit(solution)/shard_map/pallas_call | solution.py:73
  (10 shorter events, 0.2 us)
Async XLA Ops:
  0.0 20.6 %copy-start = (s32[256,256]{1,0:T(8,128)S(1)}, s32[256,256]{1,0:T(8,128)}, u32[]{:S(2)}) copy-start(s32[256,256]{1,0:T(8,128)} %param.8) | copy-start | bytes 786436
  4.0 46.6 %all-to-all-start = ((f32[128,16,128]{2,1,0:T(8,128)}), f32[128,16,128]{2,1,0:T(8,128)S(1)}, u32[]{:S(2)}, u32[]{:S(2)}) async-start(f32[128,16,128]{2,1,0:T(8,128)} %shard_map.64), calls=%async_computation | async-start | bytes 2097152 | tf_op jit(solution)/shard_map/all_to_all | solution.py:144
  25.9 24.7 %copy-start.1 = (f32[128,128,1]{1,0,2:T(8,128)S(1)}, f32[128,128,1]{1,0,2:T(8,128)}, u32[]{:S(2)}) copy-start(f32[128,128,1]{1,0,2:T(8,128)} %constant.115) | copy-start | bytes 196612
  26.0 0.7 copy-start.2
  54.9 18.9 %all-to-all-start.1 = ((f32[128,4,128]{2,1,0:T(4,128)}), f32[128,4,128]{2,1,0:T(4,128)S(1)}, u32[]{:S(2)}, u32[]{:S(2)}) async-start(f32[128,4,128]{2,1,0:T(4,128)} %bitcast.12), calls=%async_computation.1 | async-start | bytes 524288 | tf_op jit(solution)/shard_map/all_to_all | solution.py:173

commit v12 on v8

--- a/solution.py
+++ b/solution.py
@@ -138,7 +138,7 @@
     received = lax.all_to_all(outgoing, "rows", split_axis=0, concat_axis=0, tiled=True)
     across = jnp.asarray(walsh_sign_matrix(row_devices))
     mixed = jnp.einsum(
-        "st,tvl->svl", across, received, precision=lax.Precision.HIGHEST
+        "st,tvl->vsl", across, received, precision=lax.Precision.HIGHEST
     ).reshape(row_devices * sub_rows // 2, 2 * slab_width)
 
     block_total = samples.shape[0]
@@ -148,7 +148,7 @@
     sample_values = jnp.take_along_axis(samples, picks, axis=1)
     shard_of = picks // (samples.shape[1] // row_devices)
     offsets = sample_values - shard_of * shard_rows - processor_number * sub_rows
-    both_halves = jnp.take(mixed, shard_of * (sub_rows // 2) + offsets // 2, axis=0)
+    both_halves = jnp.take(mixed, (offsets // 2) * row_devices + shard_of, axis=0)
     chosen = jnp.where(
         (offsets % 2 == 1)[:, :, None], both_halves[:, :, slab_width:], both_halves[:, :, :slab_width]
     )

time: 88.1 us -> 87.6 us (level)
  no operation moved by 1% of the time
where the time goes in v12:
time: 87.6 us; the launch traced here: 87.2 us
  waiting for transfers between devices  34.4 us (39%)
  starting transfers between devices  22.5 us (26%)
  Pallas kernels  11 us (13%)
  local copies, waits for them, and re-layouts  8.75 us (10%)
  blocking collectives  5.55 us (6%)
  matrix products  2.45 us (3%)
  other arithmetic  2.3 us (3%)
    all_to_all x1, waiting for transfers between devices, per_device(): lax.all_to_all(outgoing, 'rows', split_axis=0, concat_axis=0, tiled=True)  23 us
    all_to_all x1, starting transfers between devices, per_device(): lax.all_to_all(outgoing, 'rows', split_axis=0, concat_axis=0, tiled=True)  16.3 us
    all_to_all x1, waiting for transfers between devices, per_device(): lax.all_to_all(bundled, 'rows', split_axis=0, concat_axis=0, tiled=True)  11.4 us
    pallas_call x1, Pallas kernels, cholesky_upper(): pl.pallas_call(cholesky_kernel, out_shape=jax.ShapeDtypeStruct((blocks, s...  8.19 us
    all_to_all x1, starting transfers between devices, per_device(): lax.all_to_all(bundled, 'rows', split_axis=0, concat_axis=0, tiled=True)  6.18 us
    all_gather x1, blocking collectives, per_device(): whole_rows = lax.all_gather(received_rows, 'cols', axis=2, tiled=True)  5.55 us
    gather x7, local copies, waits for them, and re-layouts, per_device(): sample_values = jnp.take_along_axis(samples, picks, axis=1)  5.22 us
    pallas_call x1, Pallas kernels, local_mix(): pl.pallas_call(local_mix_kernel, out_shape=jax.ShapeDtypeStruct((row_devi...  2.84 us
  transfers between devices with their start and end apart: 2, of which 2 were waited for; matrix products, arithmetic and copies ran while one was open for 9% of the time, Pallas kernels for 0%

profile of v12, /device:TPU:1, one launch (start us, length us, event | category | flops | bytes accessed | tf_op | source)
XLA Modules:
  0.0 87.2 jit_solution(4040586349202315510)
XLA Ops:
  0.0 0.0 copy-start
  0.0 2.8 %shard_map.64 = f32[128,16,128]{2,1,0:T(8,128)} custom-call(bf16[64,4096]{1,0:T(8,128)(2,1)} %matrix_ref.1, s32[1,4096]{1,0:T(1,128)} %bitcast.27, bf16[2,64,128]{2,1,0:T(8,128)(2,1)} %constant.99.clone.table_ref), custom_call_target="tpu_custom_call" | custom-call | tf_op jit(solution)/shard_map/pallas_call | solution.py:112
  2.8 16.3 %all-to-all-start = ((f32[128,16,128]{2,1,0:T(8,128)}), f32[128,16,128]{2,1,0:T(8,128)S(1)}, u32[]{:S(2)}, u32[]{:S(2)}) async-start(f32[128,16,128]{2,1,0:T(8,128)} %shard_map.64), calls=%async_computation | async-start | bytes 2097152 | tf_op jit(solution)/shard_map/all_to_all | solution.py:138
  19.2 0.1 copy.55
  19.4 0.1 reshape.400
  19.5 0.0 copy-done
  19.5 4.5 %gather_fusion.1 = s32[512]{0:T(512)S(1)} fusion(s32[256,256]{1,0:T(8,128)S(1)} %copy-done, s32[512]{0:T(512)S(1)} %reshape.400), kind=kCustom, calls=%fused_computation.1 | custom fusion | bytes 8192 | tf_op jit(solution)/shard_map/jit(take_along_axis)/gather | solution.py:148
  24.0 0.1 gather.11
  24.2 0.1 reshape.403
  24.3 0.1 copy.58
  24.5 0.1 copy.59
  24.6 0.1 reshape.394
  24.8 0.0 copy-start.1
  24.8 0.1 copy.56
  24.9 0.0 copy-start.2
  24.9 0.7 copy-done.2
  25.6 0.2 convert_reduce_fusion
  25.7 0.6 multiply_add_fusion
  26.4 23.0 %all-to-all-done = f32[128,16,128]{2,1,0:T(8,128)S(1)} async-done(((f32[128,16,128]{2,1,0:T(8,128)}), f32[128,16,128]{2,1,0:T(8,128)S(1)}, u32[]{:S(2)}, u32[]{:S(2)}) %all-to-all-start) | async-done | bytes 1048608 | tf_op jit(solution)/shard_map/all_to_all | solution.py:138
  49.5 0.0 copy-done.1
  49.5 1.4 %fusion = f32[16,128,128]{1,2,0:T(8,128)S(1)} fusion(f32[128,128,1]{1,0,2:T(8,128)S(1)} %copy-done.1, f32[128,16,128]{2,1,0:T(8,128)S(1)} %all-to-all-done), kind=kOutput, calls=%fused_computation.2 | convolution fusion | flops 402653184 | bytes 2162688 | tf_op jit(solution)/shard_map/st,tvl->vsl/dot_general | solution.py:140
  50.8 1.0 %gather_fusion = f32[512,128]{1,0:T(8,128)S(1)} fusion(f32[2048,128]{1,0:T(8,128)S(1)} %bitcast.23, s32[1024]{0:T(1024)S(1)} %pad_clamp_fusion), kind=kCustom, calls=%fused_computation | custom fusion | bytes 526336 | tf_op jit(solution)/shard_map/jit(_take)/gather | solution.py:151
  51.9 0.1 copy.60
  52.1 1.1 %fusion.2 = f32[512,128]{1,0:T(8,128)} fusion(f32[256,128]{0,1:T(8,128)S(1)} %bitcast.26, s32[256]{0:T(256)S(1)} %get-tuple-element.8), kind=kOutput, calls=%fused_computation.5 | convolution fusion | flops 201457664 | bytes 394240
  53.2 6.2 %all-to-all-start.1 = ((f32[128,4,128]{2,1,0:T(4,128)}), f32[128,4,128]{2,1,0:T(4,128)S(1)}, u32[]{:S(2)}, u32[]{:S(2)}) async-start(f32[128,4,128]{2,1,0:T(4,128)} %bitcast.14), calls=%async_computation.1 | async-start | bytes 524288 | tf_op jit(solution)/shard_map/all_to_all | solution.py:167
  59.4 1.3 %pad_add_fusion.2.scalar_ref = s32[2]{0:T(128)} fusion(s32[1]{0:T(128)} %bitcast.2, s32[1]{0:T(128)} %bitcast), kind=kLoop, calls=%fused_computation.53 | loop fusion | flops 2 | bytes 16 | tf_op jit(solution)/shard_map/stack | solution.py:171
  60.7 11.4 %all-to-all-done.1 = f32[128,4,128]{2,1,0:T(4,128)S(1)} async-done(((f32[128,4,128]{2,1,0:T(4,128)}), f32[128,4,128]{2,1,0:T(4,128)S(1)}, u32[]{:S(2)}, u32[]{:S(2)}) %all-to-all-start.1) | async-done | bytes 262176 | tf_op jit(solution)/shard_map/all_to_all | solution.py:167
  72.1 0.1 reshape.391
  72.2 0.2 copy.63
  72.4 5.5 %all_gather.3 = f32[4,256,128]{1,0,2:T(4,128)S(1)} all-gather(f32[4,256,64]{1,0,2:T(4,128)S(1)} %copy.63), channel_id=1, replica_groups=mesh['rows'=128,'cols'=2] {'cols'}, dimensions={2}, use_global_device_ids=true | all-gather | bytes 786432 | tf_op jit(solution)/shard_map/all_gather | solution.py:169
  78.0 1.0 %copy.64.rows_ref = f32[4,256,128]{2,1,0:T(8,128)} copy(f32[4,256,128]{1,0,2:T(4,128)S(1)} %all_gather.3) | data formatting | bytes 1048576 | tf_op jit(solution)/shard_map/all_gather | solution.py:169
  79.0 8.2 %shard_map.65 = f32[4,64,128]{2,1,0:T(8,128)} custom-call(s32[2]{0:T(128)} %pad_add_fusion.2.scalar_ref, f32[4,256,128]{2,1,0:T(8,128)} %copy.64.rows_ref), custom_call_target="tpu_custom_call" | custom-call | tf_op jit(solution)/shard_map/pallas_call | solution.py:73
  (10 shorter events, 0.2 us)
Async XLA Ops:
  0.0 19.5 %copy-start = (s32[256,256]{1,0:T(8,128)S(1)}, s32[256,256]{1,0:T(8,128)}, u32[]{:S(2)}) copy-start(s32[256,256]{1,0:T(8,128)} %param.8) | copy-start | bytes 786436
  2.8 46.6 %all-to-all-start = ((f32[128,16,128]{2,1,0:T(8,128)}), f32[128,16,128]{2,1,0:T(8,128)S(1)}, u32[]{:S(2)}, u32[]{:S(2)}) async-start(f32[128,16,128]{2,1,0:T(8,128)} %shard_map.64), calls=%async_computation | async-start | bytes 2097152 | tf_op jit(solution)/shard_map/all_to_all | solution.py:138
  24.8 24.7 %copy-start.1 = (f32[128,128,1]{1,0,2:T(8,128)S(1)}, f32[128,128,1]{1,0,2:T(8,128)}, u32[]{:S(2)}) copy-start(f32[128,128,1]{1,0,2:T(8,128)} %constant.114) | copy-start | bytes 196612
  24.9 0.7 copy-start.2
  53.2 18.9 %all-to-all-start.1 = ((f32[128,4,128]{2,1,0:T(4,128)}), f32[128,4,128]{2,1,0:T(4,128)S(1)}, u32[]{:S(2)}, u32[]{:S(2)}) async-start(f32[128,4,128]{2,1,0:T(4,128)} %bitcast.14), calls=%async_computation.1 | async-start | bytes 524288 | tf_op jit(solution)/shard_map/all_to_all | solution.py:167

commit v13 on v12

--- a/solution.py
+++ b/solution.py
@@ -17,10 +17,12 @@
 
 
 def cholesky_kernel(scalar_ref, rows_ref, out_ref, work_ref):
-    blocks, samples, order = rows_ref.shape
+    cores, blocks, width, samples = rows_ref.shape
+    order = cores * width
     for b in range(blocks):
+        columns = jnp.concatenate([rows_ref[core, b] for core in range(cores)], axis=0)
         gram = lax.dot_general(
-            rows_ref[b], rows_ref[b], (((0,), (0,)), ((), ())),
+            columns, columns, (((1,), (1,)), ((), ())),
             precision=lax.Precision.HIGHEST, preferred_element_type=jnp.float32,
         ) / samples
         diagonal = (
@@ -69,7 +71,8 @@
 
 
 def cholesky_upper(scalars, whole_rows, slab_width):
-    blocks, samples, order = whole_rows.shape
+    cores, blocks, width, samples = whole_rows.shape
+    order = cores * width
     return pl.pallas_call(
         cholesky_kernel,
         out_shape=jax.ShapeDtypeStruct((blocks, slab_width, order), jnp.float32),
@@ -165,8 +168,9 @@
     bundled = jnp.einsum("kb,bps->kps", placing, chosen, precision=lax.Precision.HIGHEST)
     bundled = bundled.reshape(row_devices, CAPB, 2 * slab_width)
     arriving = lax.all_to_all(bundled, "rows", split_axis=0, concat_axis=0, tiled=True)
-    received_rows = jnp.transpose(arriving, (1, 0, 2)).reshape(CAPB, row_devices * 2, slab_width)
-    whole_rows = lax.all_gather(received_rows, "cols", axis=2, tiled=True)
+    received_rows = arriving.reshape(row_devices, CAPB, 2, slab_width).transpose(1, 3, 0, 2)
+    received_rows = received_rows.reshape(CAPB, slab_width, row_devices * 2)
+    whole_rows = lax.all_gather(received_rows, "cols", axis=0, tiled=False)
     owned_total = jnp.sum((owner_list == processor_number).astype(jnp.int32))
     scalars = jnp.stack([lax.axis_index("cols").astype(jnp.int32), owned_total.astype(jnp.int32)])
     return cholesky_upper(scalars, whole_rows, slab_width)

time: 87.6 us -> 86.8 us (level)
    all_gather x1 -> x0, local copies, waits for them, and re-layouts: 1.02 us -> none  [per_device(): whole_rows = lax.all_gather(received_rows, 'cols', axis=2, tiled=True)]
where the time goes in v13:
time: 86.8 us; the launch traced here: 86.5 us
  waiting for transfers between devices  34.4 us (40%)
  starting transfers between devices  22.5 us (26%)
  Pallas kernels  11 us (13%)
  local copies, waits for them, and re-layouts  7.94 us (9%)
  blocking collectives  5.68 us (7%)
  matrix products  2.45 us (3%)
  other arithmetic  2.3 us (3%)
    all_to_all x1, waiting for transfers between devices, per_device(): lax.all_to_all(outgoing, 'rows', split_axis=0, concat_axis=0, tiled=True)  23 us
    all_to_all x1, starting transfers between devices, per_device(): lax.all_to_all(outgoing, 'rows', split_axis=0, concat_axis=0, tiled=True)  16.3 us
    all_to_all x1, waiting for transfers between devices, per_device(): lax.all_to_all(bundled, 'rows', split_axis=0, concat_axis=0, tiled=True)  11.4 us
    pallas_call x1, Pallas kernels, cholesky_upper(): pl.pallas_call(cholesky_kernel, out_shape=jax.ShapeDtypeStruct((blocks, s...  8.12 us
    all_to_all x1, starting transfers between devices, per_device(): lax.all_to_all(bundled, 'rows', split_axis=0, concat_axis=0, tiled=True)  6.18 us
    all_gather x1, blocking collectives, per_device(): whole_rows = lax.all_gather(received_rows, 'cols', axis=0, tiled=False)  5.68 us
    gather x7, local copies, waits for them, and re-layouts, per_device(): sample_values = jnp.take_along_axis(samples, picks, axis=1)  5.22 us
    pallas_call x1, Pallas kernels, local_mix(): pl.pallas_call(local_mix_kernel, out_shape=jax.ShapeDtypeStruct((row_devi...  2.84 us
  transfers between devices with their start and end apart: 2, of which 2 were waited for; matrix products, arithmetic and copies ran while one was open for 9% of the time, Pallas kernels for 0%

profile of v13, /device:TPU:1, one launch (start us, length us, event | category | flops | bytes accessed | tf_op | source)
XLA Modules:
  0.0 86.5 jit_solution(1926621632340879559)
XLA Ops:
  0.0 0.0 copy-start
  0.0 2.8 %shard_map.64 = f32[128,16,128]{2,1,0:T(8,128)} custom-call(bf16[64,4096]{1,0:T(8,128)(2,1)} %matrix_ref.1, s32[1,4096]{1,0:T(1,128)} %bitcast.31, bf16[2,64,128]{2,1,0:T(8,128)(2,1)} %constant.99.clone.table_ref), custom_call_target="tpu_custom_call" | custom-call | tf_op jit(solution)/shard_map/pallas_call | solution.py:115
  2.8 16.3 %all-to-all-start = ((f32[128,16,128]{2,1,0:T(8,128)}), f32[128,16,128]{2,1,0:T(8,128)S(1)}, u32[]{:S(2)}, u32[]{:S(2)}) async-start(f32[128,16,128]{2,1,0:T(8,128)} %shard_map.64), calls=%async_computation | async-start | bytes 2097152 | tf_op jit(solution)/shard_map/all_to_all | solution.py:141
  19.2 0.1 copy.56
  19.4 0.1 reshape.400
  19.5 0.0 copy-done
  19.5 4.5 %gather_fusion.1 = s32[512]{0:T(512)S(1)} fusion(s32[256,256]{1,0:T(8,128)S(1)} %copy-done, s32[512]{0:T(512)S(1)} %reshape.400), kind=kCustom, calls=%fused_computation.1 | custom fusion | bytes 8192 | tf_op jit(solution)/shard_map/jit(take_along_axis)/gather | solution.py:151
  24.0 0.1 gather.11
  24.2 0.1 reshape.403
  24.3 0.1 copy.59
  24.5 0.1 copy.60
  24.6 0.1 reshape.394
  24.8 0.0 copy-start.1
  24.8 0.1 copy.57
  24.9 0.0 copy-start.2
  24.9 0.7 copy-done.2
  25.6 0.2 convert_reduce_fusion
  25.7 0.6 multiply_add_fusion
  26.4 23.0 %all-to-all-done = f32[128,16,128]{2,1,0:T(8,128)S(1)} async-done(((f32[128,16,128]{2,1,0:T(8,128)}), f32[128,16,128]{2,1,0:T(8,128)S(1)}, u32[]{:S(2)}, u32[]{:S(2)}) %all-to-all-start) | async-done | bytes 1048608 | tf_op jit(solution)/shard_map/all_to_all | solution.py:141
  49.5 0.0 copy-done.1
  49.5 1.4 %fusion = f32[16,128,128]{1,2,0:T(8,128)S(1)} fusion(f32[128,128,1]{1,0,2:T(8,128)S(1)} %copy-done.1, f32[128,16,128]{2,1,0:T(8,128)S(1)} %all-to-all-done), kind=kOutput, calls=%fused_computation.2 | convolution fusion | flops 402653184 | bytes 2162688 | tf_op jit(solution)/shard_map/st,tvl->vsl/dot_general | solution.py:143
  50.8 1.0 %gather_fusion = f32[512,128]{1,0:T(8,128)S(1)} fusion(f32[2048,128]{1,0:T(8,128)S(1)} %bitcast.26, s32[1024]{0:T(1024)S(1)} %pad_clamp_fusion), kind=kCustom, calls=%fused_computation | custom fusion | bytes 526336 | tf_op jit(solution)/shard_map/jit(_take)/gather | solution.py:154
  51.9 0.1 copy.61
  52.1 1.1 %fusion.2 = f32[512,128]{1,0:T(8,128)} fusion(f32[256,128]{0,1:T(8,128)S(1)} %bitcast.30, s32[256]{0:T(256)S(1)} %get-tuple-element.8), kind=kOutput, calls=%fused_computation.5 | convolution fusion | flops 201457664 | bytes 394240
  53.2 6.2 %all-to-all-start.1 = ((f32[128,4,128]{2,1,0:T(4,128)}), f32[128,4,128]{2,1,0:T(4,128)S(1)}, u32[]{:S(2)}, u32[]{:S(2)}) async-start(f32[128,4,128]{2,1,0:T(4,128)} %bitcast.17), calls=%async_computation.1 | async-start | bytes 524288 | tf_op jit(solution)/shard_map/all_to_all | solution.py:170
  59.4 1.3 %pad_add_fusion.2.scalar_ref = s32[2]{0:T(128)} fusion(s32[1]{0:T(128)} %bitcast.2, s32[1]{0:T(128)} %bitcast), kind=kLoop, calls=%fused_computation.53 | loop fusion | flops 2 | bytes 16 | tf_op jit(solution)/shard_map/stack | solution.py:175
  60.7 11.4 %all-to-all-done.1 = f32[128,4,128]{2,1,0:T(4,128)S(1)} async-done(((f32[128,4,128]{2,1,0:T(4,128)}), f32[128,4,128]{2,1,0:T(4,128)S(1)}, u32[]{:S(2)}, u32[]{:S(2)}) %all-to-all-start.1) | async-done | bytes 262176 | tf_op jit(solution)/shard_map/all_to_all | solution.py:170
  72.1 0.1 copy.63
  72.2 0.3 copy.64
  72.5 0.2 copy.65
  72.6 5.7 %all_gather.3.rows_ref = f32[2,4,64,256]{3,2,1,0:T(8,128)} all-gather(f32[1,4,64,256]{3,2,1,0:T(8,128)S(1)} %copy.65), channel_id=1, replica_groups=mesh['rows'=128,'cols'=2] {'cols'}, dimensions={0}, use_global_device_ids=true | all-gather | bytes 786432 | tf_op jit(solution)/shard_map/all_gather | solution.py:173
  78.3 8.1 %shard_map.65 = f32[4,64,128]{2,1,0:T(8,128)} custom-call(s32[2]{0:T(128)} %pad_add_fusion.2.scalar_ref, f32[2,4,64,256]{3,2,1,0:T(8,128)} %all_gather.3.rows_ref), custom_call_target="tpu_custom_call" | custom-call | tf_op jit(solution)/shard_map/pallas_call | solution.py:76
  (9 shorter events, 0.2 us)
Async XLA Ops:
  0.0 19.5 %copy-start = (s32[256,256]{1,0:T(8,128)S(1)}, s32[256,256]{1,0:T(8,128)}, u32[]{:S(2)}) copy-start(s32[256,256]{1,0:T(8,128)} %param.8) | copy-start | bytes 786436
  2.8 46.6 %all-to-all-start = ((f32[128,16,128]{2,1,0:T(8,128)}), f32[128,16,128]{2,1,0:T(8,128)S(1)}, u32[]{:S(2)}, u32[]{:S(2)}) async-start(f32[128,16,128]{2,1,0:T(8,128)} %shard_map.64), calls=%async_computation | async-start | bytes 2097152 | tf_op jit(solution)/shard_map/all_to_all | solution.py:141
  24.8 24.7 %copy-start.1 = (f32[128,128,1]{1,0,2:T(8,128)S(1)}, f32[128,128,1]{1,0,2:T(8,128)}, u32[]{:S(2)}) copy-start(f32[128,128,1]{1,0,2:T(8,128)} %constant.114) | copy-start | bytes 196612
  24.9 0.7 copy-start.2
  53.2 18.9 %all-to-all-start.1 = ((f32[128,4,128]{2,1,0:T(4,128)}), f32[128,4,128]{2,1,0:T(4,128)S(1)}, u32[]{:S(2)}, u32[]{:S(2)}) async-start(f32[128,4,128]{2,1,0:T(4,128)} %bitcast.17), calls=%async_computation.1 | async-start | bytes 524288 | tf_op jit(solution)/shard_map/all_to_all | solution.py:170

commit v14 on v13

--- a/solution.py
+++ b/solution.py
@@ -89,20 +89,21 @@
 def local_mix_kernel(matrix_ref, signs_ref, table_ref, out_ref):
     slab_width = matrix_ref.shape[0]
     rows = out_ref.shape[1]
-    groups = table_ref.shape[1] // rows
+    groups = table_ref.shape[0] // (2 * rows)
 
     def body(blk, carry):
         start = pl.multiple_of(blk * HB, HB)
         flips = (1 - 2 * signs_ref[:, pl.ds(start, HB)]).astype(jnp.float32)
         flipped = (matrix_ref[:, pl.ds(start, HB)].astype(jnp.float32) * flips).astype(jnp.bfloat16)
+        mixed = lax.dot_general(
+            table_ref[...], flipped, (((1,), (1,)), ((), ())),
+            preferred_element_type=jnp.float32,
+        )
         for parity in range(2):
-            mixed = lax.dot_general(
-                table_ref[parity], flipped, (((1,), (1,)), ((), ())),
-                preferred_element_type=jnp.float32,
-            )
             for h in range(groups):
+                first = parity * groups * rows + h * rows
                 out_ref[blk * groups + h, :, parity * slab_width:(parity + 1) * slab_width] = (
-                    mixed[h * rows:(h + 1) * rows, :]
+                    mixed[first:first + rows, :]
                 )
         return carry
 
@@ -136,7 +137,7 @@
     processor_number = lax.axis_index("rows")
     sub_rows = shard_rows // row_devices
     scale = 1.0 / math.sqrt(HB * row_devices)
-    table = (walsh_sign_matrix(HB) * scale).reshape(HB // 2, 2, HB).transpose(1, 0, 2)
+    table = (walsh_sign_matrix(HB) * scale).reshape(HB // 2, 2, HB).transpose(1, 0, 2).reshape(HB, HB)
     outgoing = local_mix(matrix, signs.reshape(1, shard_rows), jnp.asarray(table, jnp.bfloat16), row_devices)
     received = lax.all_to_all(outgoing, "rows", split_axis=0, concat_axis=0, tiled=True)
     across = jnp.asarray(walsh_sign_matrix(row_devices))

time: 86.8 us -> 86.5 us (level)
  no operation moved by 1% of the time
where the time goes in v14:
time: 86.5 us; the launch traced here: 86.2 us
  waiting for transfers between devices  34.4 us (40%)
  starting transfers between devices  22.5 us (26%)
  Pallas kernels  10.7 us (12%)
  local copies, waits for them, and re-layouts  7.94 us (9%)
  blocking collectives  5.68 us (7%)
  matrix products  2.45 us (3%)
  other arithmetic  2.3 us (3%)
    all_to_all x1, waiting for transfers between devices, per_device(): lax.all_to_all(outgoing, 'rows', split_axis=0, concat_axis=0, tiled=True)  23 us
    all_to_all x1, starting transfers between devices, per_device(): lax.all_to_all(outgoing, 'rows', split_axis=0, concat_axis=0, tiled=True)  16.3 us
    all_to_all x1, waiting for transfers between devices, per_device(): lax.all_to_all(bundled, 'rows', split_axis=0, concat_axis=0, tiled=True)  11.4 us
    pallas_call x1, Pallas kernels, cholesky_upper(): pl.pallas_call(cholesky_kernel, out_shape=jax.ShapeDtypeStruct((blocks, s...  8.12 us
    all_to_all x1, starting transfers between devices, per_device(): lax.all_to_all(bundled, 'rows', split_axis=0, concat_axis=0, tiled=True)  6.18 us
    all_gather x1, blocking collectives, per_device(): whole_rows = lax.all_gather(received_rows, 'cols', axis=0, tiled=False)  5.68 us
    gather x7, local copies, waits for them, and re-layouts, per_device(): sample_values = jnp.take_along_axis(samples, picks, axis=1)  5.22 us
    pallas_call x1, Pallas kernels, local_mix(): pl.pallas_call(local_mix_kernel, out_shape=jax.ShapeDtypeStruct((row_devi...  2.59 us
  transfers between devices with their start and end apart: 2, of which 2 were waited for; matrix products, arithmetic and copies ran while one was open for 9% of the time, Pallas kernels for 0%

profile of v14, /device:TPU:1, one launch (start us, length us, event | category | flops | bytes accessed | tf_op | source)
XLA Modules:
  0.0 86.2 jit_solution(3518016437336972381)
XLA Ops:
  0.0 0.0 copy-start
  0.0 2.6 %shard_map.64 = f32[128,16,128]{2,1,0:T(8,128)} custom-call(bf16[64,4096]{1,0:T(8,128)(2,1)} %matrix_ref.1, s32[1,4096]{1,0:T(1,128)} %bitcast.31, bf16[128,128]{1,0:T(8,128)(2,1)} %constant.99.clone.table_ref), custom_call_target="tpu_custom_call" | custom-call | tf_op jit(solution)/shard_map/pallas_call | solution.py:116
  2.6 16.3 %all-to-all-start = ((f32[128,16,128]{2,1,0:T(8,128)}), f32[128,16,128]{2,1,0:T(8,128)S(1)}, u32[]{:S(2)}, u32[]{:S(2)}) async-start(f32[128,16,128]{2,1,0:T(8,128)} %shard_map.64), calls=%async_computation | async-start | bytes 2097152 | tf_op jit(solution)/shard_map/all_to_all | solution.py:142
  19.0 0.1 copy.56
  19.1 0.1 reshape.400
  19.3 0.0 copy-done
  19.3 4.5 %gather_fusion.1 = s32[512]{0:T(512)S(1)} fusion(s32[256,256]{1,0:T(8,128)S(1)} %copy-done, s32[512]{0:T(512)S(1)} %reshape.400), kind=kCustom, calls=%fused_computation.1 | custom fusion | bytes 8192 | tf_op jit(solution)/shard_map/jit(take_along_axis)/gather | solution.py:152
  23.8 0.1 gather.11
  23.9 0.1 reshape.403
  24.1 0.1 copy.59
  24.2 0.1 copy.60
  24.4 0.1 reshape.394
  24.5 0.0 copy-start.1
  24.5 0.1 copy.57
  24.6 0.0 copy-start.2
  24.6 0.7 copy-done.2
  25.3 0.2 convert_reduce_fusion
  25.5 0.6 multiply_add_fusion
  26.2 23.0 %all-to-all-done = f32[128,16,128]{2,1,0:T(8,128)S(1)} async-done(((f32[128,16,128]{2,1,0:T(8,128)}), f32[128,16,128]{2,1,0:T(8,128)S(1)}, u32[]{:S(2)}, u32[]{:S(2)}) %all-to-all-start) | async-done | bytes 1048608 | tf_op jit(solution)/shard_map/all_to_all | solution.py:142
  49.2 0.0 copy-done.1
  49.2 1.4 %fusion = f32[16,128,128]{1,2,0:T(8,128)S(1)} fusion(f32[128,128,1]{1,0,2:T(8,128)S(1)} %copy-done.1, f32[128,16,128]{2,1,0:T(8,128)S(1)} %all-to-all-done), kind=kOutput, calls=%fused_computation.2 | convolution fusion | flops 402653184 | bytes 2162688 | tf_op jit(solution)/shard_map/st,tvl->vsl/dot_general | solution.py:144
  50.6 1.0 %gather_fusion = f32[512,128]{1,0:T(8,128)S(1)} fusion(f32[2048,128]{1,0:T(8,128)S(1)} %bitcast.26, s32[1024]{0:T(1024)S(1)} %pad_clamp_fusion), kind=kCustom, calls=%fused_computation | custom fusion | bytes 526336 | tf_op jit(solution)/shard_map/jit(_take)/gather | solution.py:155
  51.6 0.1 copy.61
  51.8 1.1 %fusion.2 = f32[512,128]{1,0:T(8,128)} fusion(f32[256,128]{0,1:T(8,128)S(1)} %bitcast.30, s32[256]{0:T(256)S(1)} %get-tuple-element.8), kind=kOutput, calls=%fused_computation.5 | convolution fusion | flops 201457664 | bytes 394240
  52.9 6.2 %all-to-all-start.1 = ((f32[128,4,128]{2,1,0:T(4,128)}), f32[128,4,128]{2,1,0:T(4,128)S(1)}, u32[]{:S(2)}, u32[]{:S(2)}) async-start(f32[128,4,128]{2,1,0:T(4,128)} %bitcast.17), calls=%async_computation.1 | async-start | bytes 524288 | tf_op jit(solution)/shard_map/all_to_all | solution.py:171
  59.1 1.3 %pad_add_fusion.2.scalar_ref = s32[2]{0:T(128)} fusion(s32[1]{0:T(128)} %bitcast.2, s32[1]{0:T(128)} %bitcast), kind=kLoop, calls=%fused_computation.53 | loop fusion | flops 2 | bytes 16 | tf_op jit(solution)/shard_map/stack | solution.py:176
  60.4 11.4 %all-to-all-done.1 = f32[128,4,128]{2,1,0:T(4,128)S(1)} async-done(((f32[128,4,128]{2,1,0:T(4,128)}), f32[128,4,128]{2,1,0:T(4,128)S(1)}, u32[]{:S(2)}, u32[]{:S(2)}) %all-to-all-start.1) | async-done | bytes 262176 | tf_op jit(solution)/shard_map/all_to_all | solution.py:171
  71.8 0.1 copy.63
  71.9 0.3 copy.64
  72.2 0.2 copy.65
  72.4 5.7 %all_gather.3.rows_ref = f32[2,4,64,256]{3,2,1,0:T(8,128)} all-gather(f32[1,4,64,256]{3,2,1,0:T(8,128)S(1)} %copy.65), channel_id=1, replica_groups=mesh['rows'=128,'cols'=2] {'cols'}, dimensions={0}, use_global_device_ids=true | all-gather | bytes 786432 | tf_op jit(solution)/shard_map/all_gather | solution.py:174
  78.1 8.1 %shard_map.65 = f32[4,64,128]{2,1,0:T(8,128)} custom-call(s32[2]{0:T(128)} %pad_add_fusion.2.scalar_ref, f32[2,4,64,256]{3,2,1,0:T(8,128)} %all_gather.3.rows_ref), custom_call_target="tpu_custom_call" | custom-call | tf_op jit(solution)/shard_map/pallas_call | solution.py:76
  (9 shorter events, 0.2 us)
Async XLA Ops:
  0.0 19.3 %copy-start = (s32[256,256]{1,0:T(8,128)S(1)}, s32[256,256]{1,0:T(8,128)}, u32[]{:S(2)}) copy-start(s32[256,256]{1,0:T(8,128)} %param.8) | copy-start | bytes 786436
  2.6 46.6 %all-to-all-start = ((f32[128,16,128]{2,1,0:T(8,128)}), f32[128,16,128]{2,1,0:T(8,128)S(1)}, u32[]{:S(2)}, u32[]{:S(2)}) async-start(f32[128,16,128]{2,1,0:T(8,128)} %shard_map.64), calls=%async_computation | async-start | bytes 2097152 | tf_op jit(solution)/shard_map/all_to_all | solution.py:142
  24.5 24.7 %copy-start.1 = (f32[128,128,1]{1,0,2:T(8,128)S(1)}, f32[128,128,1]{1,0,2:T(8,128)}, u32[]{:S(2)}) copy-start(f32[128,128,1]{1,0,2:T(8,128)} %constant.114) | copy-start | bytes 196612
  24.6 0.7 copy-start.2
  52.9 18.9 %all-to-all-start.1 = ((f32[128,4,128]{2,1,0:T(4,128)}), f32[128,4,128]{2,1,0:T(4,128)S(1)}, u32[]{:S(2)}, u32[]{:S(2)}) async-start(f32[128,4,128]{2,1,0:T(4,128)} %bitcast.17), calls=%async_computation.1 | async-start | bytes 524288 | tf_op jit(solution)/shard_map/all_to_all | solution.py:171

commit v15 on v14

--- a/solution.py
+++ b/solution.py
@@ -16,11 +16,13 @@
 STEP = 8
 
 
-def cholesky_kernel(scalar_ref, rows_ref, out_ref, work_ref):
-    cores, blocks, width, samples = rows_ref.shape
-    order = cores * width
+def cholesky_kernel(scalar_ref, own_ref, other_ref, out_ref, work_ref):
+    blocks, width, samples = own_ref.shape
+    order = 2 * width
     for b in range(blocks):
-        columns = jnp.concatenate([rows_ref[core, b] for core in range(cores)], axis=0)
+        first = jnp.where(scalar_ref[0] == 0, own_ref[b], other_ref[b])
+        second = jnp.where(scalar_ref[0] == 0, other_ref[b], own_ref[b])
+        columns = jnp.concatenate([first, second], axis=0)
         gram = lax.dot_general(
             columns, columns, (((1,), (1,)), ((), ())),
             precision=lax.Precision.HIGHEST, preferred_element_type=jnp.float32,
@@ -70,20 +72,20 @@
         out_ref[b] = jnp.where(b < scalar_ref[1], work_ref[b, pl.ds(start, out_ref.shape[1]), :], 0.0)
 
 
-def cholesky_upper(scalars, whole_rows, slab_width):
-    cores, blocks, width, samples = whole_rows.shape
-    order = cores * width
+def cholesky_upper(scalars, own_rows, other_rows, slab_width):
+    blocks, width, samples = own_rows.shape
+    order = 2 * width
     return pl.pallas_call(
         cholesky_kernel,
         out_shape=jax.ShapeDtypeStruct((blocks, slab_width, order), jnp.float32),
         grid_spec=pltpu.PrefetchScalarGridSpec(
             num_scalar_prefetch=1,
             grid=(1,),
-            in_specs=[pl.BlockSpec(memory_space=pltpu.VMEM)],
+            in_specs=[pl.BlockSpec(memory_space=pltpu.VMEM)] * 2,
             out_specs=pl.BlockSpec(memory_space=pltpu.VMEM),
             scratch_shapes=[pltpu.VMEM((blocks, order, order), jnp.float32)],
         ),
-    )(scalars, whole_rows)
+    )(scalars, own_rows, other_rows)
 
 
 def local_mix_kernel(matrix_ref, signs_ref, table_ref, out_ref):
@@ -171,10 +173,10 @@
     arriving = lax.all_to_all(bundled, "rows", split_axis=0, concat_axis=0, tiled=True)
     received_rows = arriving.reshape(row_devices, CAPB, 2, slab_width).transpose(1, 3, 0, 2)
     received_rows = received_rows.reshape(CAPB, slab_width, row_devices * 2)
-    whole_rows = lax.all_gather(received_rows, "cols", axis=0, tiled=False)
+    other_rows = lax.ppermute(received_rows, "cols", [(0, 1), (1, 0)])
     owned_total = jnp.sum((owner_list == processor_number).astype(jnp.int32))
     scalars = jnp.stack([lax.axis_index("cols").astype(jnp.int32), owned_total.astype(jnp.int32)])
-    return cholesky_upper(scalars, whole_rows, slab_width)
+    return cholesky_upper(scalars, received_rows, other_rows, slab_width)
 
 
 def solution(mesh):

time: 86.5 us -> 85.2 us (0.985)
  blocking collectives: 5.68 us -> 18.5 us
  waiting for transfers between devices: 34.4 us -> 23 us
  starting transfers between devices: 22.5 us -> 19.9 us
    all_to_all x0 -> x1, blocking collectives: none -> 18.5 us  [per_device(): lax.all_to_all(bundled, 'rows', split_axis=0, concat_axis=0, tiled=True)]
    all_to_all x1 -> x0, waiting for transfers between devices: 11.4 us -> none  [per_device(): lax.all_to_all(bundled, 'rows', split_axis=0, concat_axis=0, tiled=True)]
    all_to_all x1 -> x0, starting transfers between devices: 6.18 us -> none  [per_device(): lax.all_to_all(bundled, 'rows', split_axis=0, concat_axis=0, tiled=True)]
    all_gather x1 -> x0, blocking collectives: 5.68 us -> none  [per_device(): whole_rows = lax.all_gather(received_rows, 'cols', axis=0, tiled=False)]
    ppermute x0 -> x1, starting transfers between devices: none -> 3.59 us  [per_device(): other_rows = lax.ppermute(received_rows, 'cols', [(0, 1), (1, 0)])]
  transfers between devices with their start and end apart: 2 -> 2, of which waited for: 2 -> 1; matrix products, arithmetic and copies ran while one was open for 9% -> 9% of each run, Pallas kernels for 0% -> 0%
where the time goes in v15:
time: 85.2 us; the launch traced here: 84.9 us
  waiting for transfers between devices  23 us (27%)
  starting transfers between devices  19.9 us (23%)
  blocking collectives  18.5 us (22%)
  Pallas kernels  10.7 us (13%)
  local copies, waits for them, and re-layouts  8.64 us (10%)
  other arithmetic  2.22 us (3%)
  matrix products  1.75 us (2%)
    all_to_all x1, waiting for transfers between devices, per_device(): lax.all_to_all(outgoing, 'rows', split_axis=0, concat_axis=0, tiled=True)  23 us
    all_to_all x1, blocking collectives, per_device(): lax.all_to_all(bundled, 'rows', split_axis=0, concat_axis=0, tiled=True)  18.5 us
    all_to_all x1, starting transfers between devices, per_device(): lax.all_to_all(outgoing, 'rows', split_axis=0, concat_axis=0, tiled=True)  16.3 us
    pallas_call x1, Pallas kernels, cholesky_upper(): pl.pallas_call(cholesky_kernel, out_shape=jax.ShapeDtypeStruct((blocks, s...  8.13 us
    gather x7, local copies, waits for them, and re-layouts, per_device(): sample_values = jnp.take_along_axis(samples, picks, axis=1)  5.22 us
    ppermute x1, starting transfers between devices, per_device(): other_rows = lax.ppermute(received_rows, 'cols', [(0, 1), (1, 0)])  3.59 us
    pallas_call x1, Pallas kernels, local_mix(): pl.pallas_call(local_mix_kernel, out_shape=jax.ShapeDtypeStruct((row_devi...  2.58 us
  transfers between devices with their start and end apart: 2, of which 1 were waited for; matrix products, arithmetic and copies ran while one was open for 9% of the time, Pallas kernels for 0%

profile of v15, /device:TPU:1, one launch (start us, length us, event | category | flops | bytes accessed | tf_op | source)
XLA Modules:
  0.0 84.9 jit_solution(9751479152037964441)
XLA Ops:
  0.0 0.0 copy-start
  0.0 2.6 %shard_map.64 = f32[128,16,128]{2,1,0:T(8,128)} custom-call(bf16[64,4096]{1,0:T(8,128)(2,1)} %matrix_ref.1, s32[1,4096]{1,0:T(1,128)} %bitcast.32, bf16[128,128]{1,0:T(8,128)(2,1)} %constant.99.clone.table_ref), custom_call_target="tpu_custom_call" | custom-call | tf_op jit(solution)/shard_map/pallas_call | solution.py:118
  2.6 16.3 %all-to-all-start = ((f32[128,16,128]{2,1,0:T(8,128)}), f32[128,16,128]{2,1,0:T(8,128)S(1)}, u32[]{:S(2)}, u32[]{:S(2)}) async-start(f32[128,16,128]{2,1,0:T(8,128)} %shard_map.64), calls=%async_computation | async-start | bytes 2097152 | tf_op jit(solution)/shard_map/all_to_all | solution.py:144
  19.0 0.1 copy.59
  19.1 0.1 reshape.404
  19.3 0.0 copy-done
  19.3 4.5 %gather_fusion.1 = s32[512]{0:T(512)S(1)} fusion(s32[256,256]{1,0:T(8,128)S(1)} %copy-done, s32[512]{0:T(512)S(1)} %reshape.404), kind=kCustom, calls=%fused_computation.1 | custom fusion | bytes 8192 | tf_op jit(solution)/shard_map/jit(take_along_axis)/gather | solution.py:154
  23.8 0.1 gather.11
  23.9 0.1 reshape.407
  24.1 0.1 copy.62
  24.2 0.1 copy.63
  24.4 0.1 reshape.398
  24.5 0.0 copy-start.3
  24.5 0.1 copy.60
  24.6 0.0 copy-start.4
  24.6 0.7 copy-done.4
  25.3 0.2 convert_reduce_fusion
  25.5 0.6 multiply_add_fusion
  26.2 23.0 %all-to-all-done = f32[128,16,128]{2,1,0:T(8,128)S(1)} async-done(((f32[128,16,128]{2,1,0:T(8,128)}), f32[128,16,128]{2,1,0:T(8,128)S(1)}, u32[]{:S(2)}, u32[]{:S(2)}) %all-to-all-start) | async-done | bytes 1048608 | tf_op jit(solution)/shard_map/all_to_all | solution.py:144
  49.2 0.0 copy-done.3
  49.2 1.4 %fusion = f32[16,128,128]{1,2,0:T(8,128)S(1)} fusion(f32[128,128,1]{1,0,2:T(8,128)S(1)} %copy-done.3, f32[128,16,128]{2,1,0:T(8,128)S(1)} %all-to-all-done), kind=kOutput, calls=%fused_computation.2 | convolution fusion | flops 402653184 | bytes 2162688 | tf_op jit(solution)/shard_map/st,tvl->vsl/dot_general | solution.py:146
  50.6 1.0 %gather_fusion = f32[512,128]{1,0:T(8,128)S(1)} fusion(f32[2048,128]{1,0:T(8,128)S(1)} %bitcast.26, s32[1024]{0:T(1024)S(1)} %pad_clamp_fusion), kind=kCustom, calls=%fused_computation | custom fusion | bytes 526336 | tf_op jit(solution)/shard_map/jit(_take)/gather | solution.py:157
  51.6 0.1 copy.64
  51.8 0.4 fusion.2
  52.2 18.5 %all_to_all.10 = f32[128,4,128]{2,1,0:T(4,128)S(1)} all-to-all(f32[128,4,128]{2,1,0:T(4,128)S(1)} %bitcast.30), channel_id=1, replica_groups=mesh['rows'=128,'cols'=2] {'rows'}, dimensions={0} | all-to-all | bytes 524288 | tf_op jit(solution)/shard_map/all_to_all | solution.py:173
  70.7 0.1 copy.66
  70.8 0.3 copy.67
  71.1 0.2 copy.69.own_ref
  71.3 0.0 copy-start.1
  71.3 3.6 %collective-permute-start = (f32[4,64,256]{2,1,0:T(8,128)S(1)}, f32[4,64,256]{2,1,0:T(8,128)S(1)}, u32[]{:S(2)}, u32[]{:S(2)}) collective-permute-start(f32[4,64,256]{2,1,0:T(8,128)S(1)} %copy.69.own_ref), channel_id=1, source_target_pairs={{0,1},{1,0},{2,3},{3,2},{4,5},{5,4},{6,7},{7,6},{8,9},{9,8},{10,11... | collective-permute-start | bytes 786440 | tf_op jit(solution)/shard_map/ppermute | solution.py:176
  74.9 1.2 %pad_add_fusion.2.scalar_ref = s32[2]{0:T(128)} fusion(s32[1]{0:T(128)} %bitcast.2, s32[1]{0:T(128)} %bitcast), kind=kLoop, calls=%fused_computation.53 | loop fusion | flops 2 | bytes 16 | tf_op jit(solution)/shard_map/stack | solution.py:178
  76.1 0.0 collective-permute-done.other_ref
  76.1 0.0 copy-done.1
  76.1 0.0 copy-start.2
  76.1 0.7 copy-done.2
  76.8 8.1 %shard_map.65 = f32[4,64,128]{2,1,0:T(8,128)} custom-call(s32[2]{0:T(128)} %pad_add_fusion.2.scalar_ref, f32[4,64,256]{2,1,0:T(8,128)} %copy-done.1, f32[4,64,256]{2,1,0:T(8,128)} %copy-done.2), custom_call_target="tpu_custom_call" | custom-call | tf_op jit(solution)/shard_map/pallas_call | solution.py:78
  (9 shorter events, 0.2 us)
Async XLA Ops:
  0.0 19.3 %copy-start = (s32[256,256]{1,0:T(8,128)S(1)}, s32[256,256]{1,0:T(8,128)}, u32[]{:S(2)}) copy-start(s32[256,256]{1,0:T(8,128)} %param.8) | copy-start | bytes 786436
  2.6 46.6 %all-to-all-start = ((f32[128,16,128]{2,1,0:T(8,128)}), f32[128,16,128]{2,1,0:T(8,128)S(1)}, u32[]{:S(2)}, u32[]{:S(2)}) async-start(f32[128,16,128]{2,1,0:T(8,128)} %shard_map.64), calls=%async_computation | async-start | bytes 2097152 | tf_op jit(solution)/shard_map/all_to_all | solution.py:144
  24.5 24.7 %copy-start.3 = (f32[128,128,1]{1,0,2:T(8,128)S(1)}, f32[128,128,1]{1,0,2:T(8,128)}, u32[]{:S(2)}) copy-start(f32[128,128,1]{1,0,2:T(8,128)} %constant.114) | copy-start | bytes 196612
  24.6 0.7 copy-start.4
  71.3 4.8 %copy-start.1 = (f32[4,64,256]{2,1,0:T(8,128)}, f32[4,64,256]{2,1,0:T(8,128)S(1)}, u32[]{:S(2)}) copy-start(f32[4,64,256]{2,1,0:T(8,128)S(1)} %copy.69.own_ref) | copy-start | bytes 786436
  71.3 4.8 %collective-permute-start = (f32[4,64,256]{2,1,0:T(8,128)S(1)}, f32[4,64,256]{2,1,0:T(8,128)S(1)}, u32[]{:S(2)}, u32[]{:S(2)}) collective-permute-start(f32[4,64,256]{2,1,0:T(8,128)S(1)} %copy.69.own_ref), channel_id=1, source_target_pairs={{0,1},{1,0},{2,3},{3,2},{4,5},{5,4},{6,7},{7,6},{8,9},{9,8},{10,11... | collective-permute-start | bytes 786440 | tf_op jit(solution)/shard_map/ppermute | solution.py:176
  76.1 0.7 copy-start.2

commit v16 on v15

--- a/solution.py
+++ b/solution.py
@@ -16,9 +16,10 @@
 STEP = 8
 
 
-def cholesky_kernel(scalar_ref, own_ref, other_ref, out_ref, work_ref):
+def cholesky_kernel(scalar_ref, owners_ref, own_ref, other_ref, out_ref, work_ref):
     blocks, width, samples = own_ref.shape
     order = 2 * width
+    owned = jnp.sum(jnp.where(owners_ref[...] == scalar_ref[1], 1, 0))
     for b in range(blocks):
         first = jnp.where(scalar_ref[0] == 0, own_ref[b], other_ref[b])
         second = jnp.where(scalar_ref[0] == 0, other_ref[b], own_ref[b])
@@ -32,7 +33,7 @@
             == lax.broadcasted_iota(jnp.int32, (order, order), 1)
         )
         identity = jnp.where(diagonal, 1.0, 0.0)
-        work_ref[b] = jnp.where(b < scalar_ref[1], gram, identity)
+        work_ref[b] = jnp.where(b < owned, gram, identity)
     lane = lax.broadcasted_iota(jnp.int32, (blocks, 1, order), 2)
     sub_panel = lax.broadcasted_iota(jnp.int32, (blocks, PANEL, order), 1)
     for p in range(order // PANEL):
@@ -69,10 +70,10 @@
         work_ref[:, base:base + PANEL, :] = panel
     start = pl.multiple_of(scalar_ref[0] * out_ref.shape[1], out_ref.shape[1])
     for b in range(blocks):
-        out_ref[b] = jnp.where(b < scalar_ref[1], work_ref[b, pl.ds(start, out_ref.shape[1]), :], 0.0)
+        out_ref[b] = jnp.where(b < owned, work_ref[b, pl.ds(start, out_ref.shape[1]), :], 0.0)
 
 
-def cholesky_upper(scalars, own_rows, other_rows, slab_width):
+def cholesky_upper(scalars, owners, own_rows, other_rows, slab_width):
     blocks, width, samples = own_rows.shape
     order = 2 * width
     return pl.pallas_call(
@@ -81,11 +82,11 @@
         grid_spec=pltpu.PrefetchScalarGridSpec(
             num_scalar_prefetch=1,
             grid=(1,),
-            in_specs=[pl.BlockSpec(memory_space=pltpu.VMEM)] * 2,
+            in_specs=[pl.BlockSpec(memory_space=pltpu.VMEM)] * 3,
             out_specs=pl.BlockSpec(memory_space=pltpu.VMEM),
             scratch_shapes=[pltpu.VMEM((blocks, order, order), jnp.float32)],
         ),
-    )(scalars, own_rows, other_rows)
+    )(scalars, owners, own_rows, other_rows)
 
 
 def local_mix_kernel(matrix_ref, signs_ref, table_ref, out_ref):
@@ -174,9 +175,9 @@
     received_rows = arriving.reshape(row_devices, CAPB, 2, slab_width).transpose(1, 3, 0, 2)
     received_rows = received_rows.reshape(CAPB, slab_width, row_devices * 2)
     other_rows = lax.ppermute(received_rows, "cols", [(0, 1), (1, 0)])
-    owned_total = jnp.sum((owner_list == processor_number).astype(jnp.int32))
-    scalars = jnp.stack([lax.axis_index("cols").astype(jnp.int32), owned_total.astype(jnp.int32)])
-    return cholesky_upper(scalars, received_rows, other_rows, slab_width)
+    scalars = jnp.stack([lax.axis_index("cols").astype(jnp.int32), processor_number.astype(jnp.int32)])
+    owner_rows = owner_list.reshape(block_total // HB, HB)
+    return cholesky_upper(scalars, owner_rows, received_rows, other_rows, slab_width)
 
 
 def solution(mesh):

time: 85.2 us -> 85.2 us (level)
  other arithmetic: 2.22 us -> 1.01 us
  waiting for transfers between devices: 23 us -> 24.2 us
  transfers between devices with their start and end apart: 2 -> 2, of which waited for: 1 -> 2; matrix products, arithmetic and copies ran while one was open for 9% -> 8% of each run, Pallas kernels for 0% -> 0%
where the time goes in v16:
time: 85.2 us; the launch traced here: 84.9 us
  waiting for transfers between devices  24.2 us (28%)
  starting transfers between devices  19.9 us (23%)
  blocking collectives  18.5 us (22%)
  Pallas kernels  10.7 us (13%)
  local copies, waits for them, and re-layouts  8.65 us (10%)
  matrix products  1.75 us (2%)
  other arithmetic  1.01 us (1%)
    all_to_all x1, waiting for transfers between devices, per_device(): lax.all_to_all(outgoing, 'rows', split_axis=0, concat_axis=0, tiled=True)  23.6 us
    all_to_all x1, blocking collectives, per_device(): lax.all_to_all(bundled, 'rows', split_axis=0, concat_axis=0, tiled=True)  18.5 us
    all_to_all x1, starting transfers between devices, per_device(): lax.all_to_all(outgoing, 'rows', split_axis=0, concat_axis=0, tiled=True)  16.3 us
    pallas_call x1, Pallas kernels, cholesky_upper(): pl.pallas_call(cholesky_kernel, out_shape=jax.ShapeDtypeStruct((blocks, s...  8.17 us
    gather x7, local copies, waits for them, and re-layouts, per_device(): sample_values = jnp.take_along_axis(samples, picks, axis=1)  5.22 us
    ppermute x1, starting transfers between devices, per_device(): other_rows = lax.ppermute(received_rows, 'cols', [(0, 1), (1, 0)])  3.59 us
    pallas_call x1, Pallas kernels, local_mix(): pl.pallas_call(local_mix_kernel, out_shape=jax.ShapeDtypeStruct((row_devi...  2.58 us
  transfers between devices with their start and end apart: 2, of which 2 were waited for; matrix products, arithmetic and copies ran while one was open for 8% of the time, Pallas kernels for 0%

profile of v16, /device:TPU:1, one launch (start us, length us, event | category | flops | bytes accessed | tf_op | source)
XLA Modules:
  0.0 84.9 jit_solution(17549072697913674075)
XLA Ops:
  0.0 0.0 copy-start
  0.0 2.6 %shard_map.64 = f32[128,16,128]{2,1,0:T(8,128)} custom-call(bf16[64,4096]{1,0:T(8,128)(2,1)} %matrix_ref.1, s32[1,4096]{1,0:T(1,128)} %bitcast.33, bf16[128,128]{1,0:T(8,128)(2,1)} %constant.99.clone.table_ref), custom_call_target="tpu_custom_call" | custom-call | tf_op jit(solution)/shard_map/pallas_call | solution.py:119
  2.6 16.3 %all-to-all-start = ((f32[128,16,128]{2,1,0:T(8,128)}), f32[128,16,128]{2,1,0:T(8,128)S(1)}, u32[]{:S(2)}, u32[]{:S(2)}) async-start(f32[128,16,128]{2,1,0:T(8,128)} %shard_map.64), calls=%async_computation | async-start | bytes 2097152 | tf_op jit(solution)/shard_map/all_to_all | solution.py:145
  19.0 0.1 copy.59
  19.1 0.1 reshape.404
  19.2 0.0 copy-done
  19.3 4.5 %gather_fusion.1 = s32[512]{0:T(512)S(1)} fusion(s32[256,256]{1,0:T(8,128)S(1)} %copy-done, s32[512]{0:T(512)S(1)} %reshape.404), kind=kCustom, calls=%fused_computation.1 | custom fusion | bytes 8192 | tf_op jit(solution)/shard_map/jit(take_along_axis)/gather | solution.py:155
  23.8 0.1 gather.11
  23.9 0.1 reshape.407
  24.1 0.1 copy.62
  24.2 0.1 copy.63
  24.4 0.1 reshape.398
  24.5 0.0 copy-start.3
  24.5 0.1 copy.60
  24.6 0.0 copy-start.4
  24.6 0.7 copy-done.4
  25.3 0.2 convert_reduce_fusion
  25.6 23.6 %all-to-all-done = f32[128,16,128]{2,1,0:T(8,128)S(1)} async-done(((f32[128,16,128]{2,1,0:T(8,128)}), f32[128,16,128]{2,1,0:T(8,128)S(1)}, u32[]{:S(2)}, u32[]{:S(2)}) %all-to-all-start) | async-done | bytes 1048608 | tf_op jit(solution)/shard_map/all_to_all | solution.py:145
  49.2 0.0 copy-done.3
  49.2 1.4 %fusion = f32[16,128,128]{1,2,0:T(8,128)S(1)} fusion(f32[128,128,1]{1,0,2:T(8,128)S(1)} %copy-done.3, f32[128,16,128]{2,1,0:T(8,128)S(1)} %all-to-all-done), kind=kOutput, calls=%fused_computation.2 | convolution fusion | flops 402653184 | bytes 2162688 | tf_op jit(solution)/shard_map/st,tvl->vsl/dot_general | solution.py:147
  50.6 1.0 %gather_fusion = f32[512,128]{1,0:T(8,128)S(1)} fusion(f32[2048,128]{1,0:T(8,128)S(1)} %bitcast.27, s32[1024]{0:T(1024)S(1)} %pad_clamp_fusion), kind=kCustom, calls=%fused_computation | custom fusion | bytes 526336 | tf_op jit(solution)/shard_map/jit(_take)/gather | solution.py:158
  51.6 0.1 copy.64
  51.8 0.4 fusion.2
  52.2 18.5 %all_to_all.10 = f32[128,4,128]{2,1,0:T(4,128)S(1)} all-to-all(f32[128,4,128]{2,1,0:T(4,128)S(1)} %bitcast.31), channel_id=1, replica_groups=mesh['rows'=128,'cols'=2] {'rows'}, dimensions={0} | all-to-all | bytes 524288 | tf_op jit(solution)/shard_map/all_to_all | solution.py:174
  70.7 0.1 copy.66
  70.8 0.3 copy.67
  71.1 0.2 copy.69.own_ref
  71.3 0.0 copy-start.1
  71.3 3.6 %collective-permute-start = (f32[4,64,256]{2,1,0:T(8,128)S(1)}, f32[4,64,256]{2,1,0:T(8,128)S(1)}, u32[]{:S(2)}, u32[]{:S(2)}) collective-permute-start(f32[4,64,256]{2,1,0:T(8,128)S(1)} %copy.69.own_ref), channel_id=1, source_target_pairs={{0,1},{1,0},{2,3},{3,2},{4,5},{5,4},{6,7},{7,6},{8,9},{9,8},{10,11... | collective-permute-start | bytes 786440 | tf_op jit(solution)/shard_map/ppermute | solution.py:177
  74.9 0.6 pad_add_fusion.2.scalar_ref
  75.5 0.5 collective-permute-done.other_ref
  76.0 0.0 copy-start.2
  76.0 0.0 copy-done.1
  76.0 0.7 copy-done.2
  76.8 8.2 %shard_map.65 = f32[4,64,128]{2,1,0:T(8,128)} custom-call(s32[2]{0:T(128)} %pad_add_fusion.2.scalar_ref, s32[2,128]{1,0:T(2,128)} %bitcast.34, f32[4,64,256]{2,1,0:T(8,128)} %copy-done.1, f32[4,64,256]{2,1,0:T(8,128)} %copy-done.2), custom_call_target="tpu_custom_call" | custom-call | tf_op jit(solution)/shard_map/pallas_call | solution.py:79
  (10 shorter events, 0.2 us)
Async XLA Ops:
  0.0 19.2 %copy-start = (s32[256,256]{1,0:T(8,128)S(1)}, s32[256,256]{1,0:T(8,128)}, u32[]{:S(2)}) copy-start(s32[256,256]{1,0:T(8,128)} %param.8) | copy-start | bytes 786436
  2.6 46.6 %all-to-all-start = ((f32[128,16,128]{2,1,0:T(8,128)}), f32[128,16,128]{2,1,0:T(8,128)S(1)}, u32[]{:S(2)}, u32[]{:S(2)}) async-start(f32[128,16,128]{2,1,0:T(8,128)} %shard_map.64), calls=%async_computation | async-start | bytes 2097152 | tf_op jit(solution)/shard_map/all_to_all | solution.py:145
  24.5 24.7 %copy-start.3 = (f32[128,128,1]{1,0,2:T(8,128)S(1)}, f32[128,128,1]{1,0,2:T(8,128)}, u32[]{:S(2)}) copy-start(f32[128,128,1]{1,0,2:T(8,128)} %constant.114) | copy-start | bytes 196612
  24.6 0.7 copy-start.4
  71.3 4.8 %copy-start.1 = (f32[4,64,256]{2,1,0:T(8,128)}, f32[4,64,256]{2,1,0:T(8,128)S(1)}, u32[]{:S(2)}) copy-start(f32[4,64,256]{2,1,0:T(8,128)S(1)} %copy.69.own_ref) | copy-start | bytes 786436
  71.3 4.8 %collective-permute-start = (f32[4,64,256]{2,1,0:T(8,128)S(1)}, f32[4,64,256]{2,1,0:T(8,128)S(1)}, u32[]{:S(2)}, u32[]{:S(2)}) collective-permute-start(f32[4,64,256]{2,1,0:T(8,128)S(1)} %copy.69.own_ref), channel_id=1, source_target_pairs={{0,1},{1,0},{2,3},{3,2},{4,5},{5,4},{6,7},{7,6},{8,9},{9,8},{10,11... | collective-permute-start | bytes 786440 | tf_op jit(solution)/shard_map/ppermute | solution.py:177
  76.0 0.7 copy-start.2

commit v17 on v15

--- a/solution.py
+++ b/solution.py
@@ -174,7 +174,7 @@
     received_rows = arriving.reshape(row_devices, CAPB, 2, slab_width).transpose(1, 3, 0, 2)
     received_rows = received_rows.reshape(CAPB, slab_width, row_devices * 2)
     other_rows = lax.ppermute(received_rows, "cols", [(0, 1), (1, 0)])
-    owned_total = jnp.sum((owner_list == processor_number).astype(jnp.int32))
+    owned_total = jnp.max(jnp.where(owner_list == processor_number, ranks + 1, 0))
     scalars = jnp.stack([lax.axis_index("cols").astype(jnp.int32), owned_total.astype(jnp.int32)])
     return cholesky_upper(scalars, received_rows, other_rows, slab_width)
 

time: 85.2 us -> 85.2 us (level)
  no operation moved by 1% of the time
where the time goes in v17:
time: 85.2 us; the launch traced here: 84.9 us
  waiting for transfers between devices  23 us (27%)
  starting transfers between devices  19.9 us (23%)
  blocking collectives  18.5 us (22%)
  Pallas kernels  10.7 us (13%)
  local copies, waits for them, and re-layouts  8.64 us (10%)
  other arithmetic  2.23 us (3%)
  matrix products  1.75 us (2%)
    all_to_all x1, waiting for transfers between devices, per_device(): lax.all_to_all(outgoing, 'rows', split_axis=0, concat_axis=0, tiled=True)  23 us
    all_to_all x1, blocking collectives, per_device(): lax.all_to_all(bundled, 'rows', split_axis=0, concat_axis=0, tiled=True)  18.5 us
    all_to_all x1, starting transfers between devices, per_device(): lax.all_to_all(outgoing, 'rows', split_axis=0, concat_axis=0, tiled=True)  16.3 us
    pallas_call x1, Pallas kernels, cholesky_upper(): pl.pallas_call(cholesky_kernel, out_shape=jax.ShapeDtypeStruct((blocks, s...  8.13 us
    gather x7, local copies, waits for them, and re-layouts, per_device(): sample_values = jnp.take_along_axis(samples, picks, axis=1)  5.22 us
    ppermute x1, starting transfers between devices, per_device(): other_rows = lax.ppermute(received_rows, 'cols', [(0, 1), (1, 0)])  3.59 us
    pallas_call x1, Pallas kernels, local_mix(): pl.pallas_call(local_mix_kernel, out_shape=jax.ShapeDtypeStruct((row_devi...  2.58 us
  transfers between devices with their start and end apart: 2, of which 1 were waited for; matrix products, arithmetic and copies ran while one was open for 9% of the time, Pallas kernels for 0%

profile of v17, /device:TPU:1, one launch (start us, length us, event | category | flops | bytes accessed | tf_op | source)
XLA Modules:
  0.0 84.9 jit_solution(12423437003615555581)
XLA Ops:
  0.0 0.0 copy-start
  0.0 2.6 %shard_map.64 = f32[128,16,128]{2,1,0:T(8,128)} custom-call(bf16[64,4096]{1,0:T(8,128)(2,1)} %matrix_ref.1, s32[1,4096]{1,0:T(1,128)} %bitcast.32, bf16[128,128]{1,0:T(8,128)(2,1)} %constant.101.clone.table_ref), custom_call_target="tpu_custom_call" | custom-call | tf_op jit(solution)/shard_map/pallas_call | solution.py:118
  2.6 16.3 %all-to-all-start = ((f32[128,16,128]{2,1,0:T(8,128)}), f32[128,16,128]{2,1,0:T(8,128)S(1)}, u32[]{:S(2)}, u32[]{:S(2)}) async-start(f32[128,16,128]{2,1,0:T(8,128)} %shard_map.64), calls=%async_computation | async-start | bytes 2097152 | tf_op jit(solution)/shard_map/all_to_all | solution.py:144
  19.0 0.1 copy.59
  19.1 0.1 reshape.404
  19.3 0.0 copy-done
  19.3 4.5 %gather_fusion.1 = s32[512]{0:T(512)S(1)} fusion(s32[256,256]{1,0:T(8,128)S(1)} %copy-done, s32[512]{0:T(512)S(1)} %reshape.404), kind=kCustom, calls=%fused_computation.1 | custom fusion | bytes 8192 | tf_op jit(solution)/shard_map/jit(take_along_axis)/gather | solution.py:154
  23.8 0.1 gather.11
  23.9 0.1 reshape.407
  24.1 0.1 copy.62
  24.2 0.1 copy.63
  24.4 0.1 reshape.398
  24.5 0.0 copy-start.3
  24.5 0.1 copy.60
  24.6 0.0 copy-start.4
  24.6 0.7 copy-done.4
  25.3 0.2 convert_reduce_fusion
  25.5 0.6 multiply_add_fusion
  26.2 23.0 %all-to-all-done = f32[128,16,128]{2,1,0:T(8,128)S(1)} async-done(((f32[128,16,128]{2,1,0:T(8,128)}), f32[128,16,128]{2,1,0:T(8,128)S(1)}, u32[]{:S(2)}, u32[]{:S(2)}) %all-to-all-start) | async-done | bytes 1048608 | tf_op jit(solution)/shard_map/all_to_all | solution.py:144
  49.2 0.0 copy-done.3
  49.2 1.4 %fusion = f32[16,128,128]{1,2,0:T(8,128)S(1)} fusion(f32[128,128,1]{1,0,2:T(8,128)S(1)} %copy-done.3, f32[128,16,128]{2,1,0:T(8,128)S(1)} %all-to-all-done), kind=kOutput, calls=%fused_computation.2 | convolution fusion | flops 402653184 | bytes 2162688 | tf_op jit(solution)/shard_map/st,tvl->vsl/dot_general | solution.py:146
  50.6 1.0 %gather_fusion = f32[512,128]{1,0:T(8,128)S(1)} fusion(f32[2048,128]{1,0:T(8,128)S(1)} %bitcast.26, s32[1024]{0:T(1024)S(1)} %pad_clamp_fusion), kind=kCustom, calls=%fused_computation | custom fusion | bytes 526336 | tf_op jit(solution)/shard_map/jit(_take)/gather | solution.py:157
  51.6 0.1 copy.64
  51.8 0.4 fusion.2
  52.2 18.5 %all_to_all.10 = f32[128,4,128]{2,1,0:T(4,128)S(1)} all-to-all(f32[128,4,128]{2,1,0:T(4,128)S(1)} %bitcast.30), channel_id=1, replica_groups=mesh['rows'=128,'cols'=2] {'rows'}, dimensions={0} | all-to-all | bytes 524288 | tf_op jit(solution)/shard_map/all_to_all | solution.py:173
  70.7 0.1 copy.66
  70.8 0.3 copy.67
  71.1 0.2 copy.69.own_ref
  71.3 0.0 copy-start.1
  71.3 3.6 %collective-permute-start = (f32[4,64,256]{2,1,0:T(8,128)S(1)}, f32[4,64,256]{2,1,0:T(8,128)S(1)}, u32[]{:S(2)}, u32[]{:S(2)}) collective-permute-start(f32[4,64,256]{2,1,0:T(8,128)S(1)} %copy.69.own_ref), channel_id=1, source_target_pairs={{0,1},{1,0},{2,3},{3,2},{4,5},{5,4},{6,7},{7,6},{8,9},{9,8},{10,11... | collective-permute-start | bytes 786440 | tf_op jit(solution)/shard_map/ppermute | solution.py:176
  74.9 1.2 %pad_add_fusion.2.scalar_ref = s32[2]{0:T(128)} fusion(s32[1]{0:T(128)} %bitcast.2, s32[1]{0:T(128)} %bitcast), kind=kLoop, calls=%fused_computation.53 | loop fusion | flops 2 | bytes 16 | tf_op jit(solution)/shard_map/stack | solution.py:178
  76.1 0.0 collective-permute-done.other_ref
  76.1 0.0 copy-done.1
  76.1 0.0 copy-start.2
  76.1 0.7 copy-done.2
  76.8 8.1 %shard_map.65 = f32[4,64,128]{2,1,0:T(8,128)} custom-call(s32[2]{0:T(128)} %pad_add_fusion.2.scalar_ref, f32[4,64,256]{2,1,0:T(8,128)} %copy-done.1, f32[4,64,256]{2,1,0:T(8,128)} %copy-done.2), custom_call_target="tpu_custom_call" | custom-call | tf_op jit(solution)/shard_map/pallas_call | solution.py:78
  (9 shorter events, 0.2 us)
Async XLA Ops:
  0.0 19.3 %copy-start = (s32[256,256]{1,0:T(8,128)S(1)}, s32[256,256]{1,0:T(8,128)}, u32[]{:S(2)}) copy-start(s32[256,256]{1,0:T(8,128)} %param.8) | copy-start | bytes 786436
  2.6 46.6 %all-to-all-start = ((f32[128,16,128]{2,1,0:T(8,128)}), f32[128,16,128]{2,1,0:T(8,128)S(1)}, u32[]{:S(2)}, u32[]{:S(2)}) async-start(f32[128,16,128]{2,1,0:T(8,128)} %shard_map.64), calls=%async_computation | async-start | bytes 2097152 | tf_op jit(solution)/shard_map/all_to_all | solution.py:144
  24.5 24.7 %copy-start.3 = (f32[128,128,1]{1,0,2:T(8,128)S(1)}, f32[128,128,1]{1,0,2:T(8,128)}, u32[]{:S(2)}) copy-start(f32[128,128,1]{1,0,2:T(8,128)} %constant.116) | copy-start | bytes 196612
  24.6 0.7 copy-start.4
  71.3 4.8 %copy-start.1 = (f32[4,64,256]{2,1,0:T(8,128)}, f32[4,64,256]{2,1,0:T(8,128)S(1)}, u32[]{:S(2)}) copy-start(f32[4,64,256]{2,1,0:T(8,128)S(1)} %copy.69.own_ref) | copy-start | bytes 786436
  71.3 4.8 %collective-permute-start = (f32[4,64,256]{2,1,0:T(8,128)S(1)}, f32[4,64,256]{2,1,0:T(8,128)S(1)}, u32[]{:S(2)}, u32[]{:S(2)}) collective-permute-start(f32[4,64,256]{2,1,0:T(8,128)S(1)} %copy.69.own_ref), channel_id=1, source_target_pairs={{0,1},{1,0},{2,3},{3,2},{4,5},{5,4},{6,7},{7,6},{8,9},{9,8},{10,11... | collective-permute-start | bytes 786440 | tf_op jit(solution)/shard_map/ppermute | solution.py:176
  76.1 0.7 copy-start.2

commit v18 on v17

--- a/solution.py
+++ b/solution.py
@@ -170,12 +170,13 @@
     )
     bundled = jnp.einsum("kb,bps->kps", placing, chosen, precision=lax.Precision.HIGHEST)
     bundled = bundled.reshape(row_devices, CAPB, 2 * slab_width)
+    owned_total = jnp.sum((owner_list == processor_number).astype(jnp.int32))
+    scalars = jnp.stack([lax.axis_index("cols").astype(jnp.int32), owned_total.astype(jnp.int32)])
+    bundled, scalars = lax.optimization_barrier((bundled, scalars))
     arriving = lax.all_to_all(bundled, "rows", split_axis=0, concat_axis=0, tiled=True)
     received_rows = arriving.reshape(row_devices, CAPB, 2, slab_width).transpose(1, 3, 0, 2)
     received_rows = received_rows.reshape(CAPB, slab_width, row_devices * 2)
     other_rows = lax.ppermute(received_rows, "cols", [(0, 1), (1, 0)])
-    owned_total = jnp.max(jnp.where(owner_list == processor_number, ranks + 1, 0))
-    scalars = jnp.stack([lax.axis_index("cols").astype(jnp.int32), owned_total.astype(jnp.int32)])
     return cholesky_upper(scalars, received_rows, other_rows, slab_width)
 
 

time: 85.2 us -> 85.2 us (level)
    all_to_all x1, waiting for transfers between devices: 23 us -> 21.8 us  [per_device(): lax.all_to_all(outgoing, 'rows', split_axis=0, concat_axis=0, tiled=True)]
    ppermute x1, waiting for transfers between devices: 0.01 us -> 1.16 us  [per_device(): other_rows = lax.ppermute(received_rows, 'cols', [(0, 1), (1, 0)])]
  transfers between devices with their start and end apart: 2 -> 2, of which waited for: 1 -> 2; matrix products, arithmetic and copies ran while one was open for 9% -> 9% of each run, Pallas kernels for 0% -> 0%
where the time goes in v18:
time: 85.2 us; the launch traced here: 84.9 us
  waiting for transfers between devices  22.9 us (27%)
  starting transfers between devices  19.9 us (23%)
  blocking collectives  18.5 us (22%)
  Pallas kernels  10.7 us (13%)
  local copies, waits for them, and re-layouts  8.66 us (10%)
  other arithmetic  2.25 us (3%)
  matrix products  1.75 us (2%)
    all_to_all x1, waiting for transfers between devices, per_device(): lax.all_to_all(outgoing, 'rows', split_axis=0, concat_axis=0, tiled=True)  21.8 us
    all_to_all x1, blocking collectives, per_device(): lax.all_to_all(bundled, 'rows', split_axis=0, concat_axis=0, tiled=True)  18.5 us
    all_to_all x1, starting transfers between devices, per_device(): lax.all_to_all(outgoing, 'rows', split_axis=0, concat_axis=0, tiled=True)  16.3 us
    pallas_call x1, Pallas kernels, cholesky_upper(): pl.pallas_call(cholesky_kernel, out_shape=jax.ShapeDtypeStruct((blocks, s...  8.13 us
    gather x7, local copies, waits for them, and re-layouts, per_device(): sample_values = jnp.take_along_axis(samples, picks, axis=1)  5.22 us
    ppermute x1, starting transfers between devices, per_device(): other_rows = lax.ppermute(received_rows, 'cols', [(0, 1), (1, 0)])  3.59 us
    pallas_call x1, Pallas kernels, local_mix(): pl.pallas_call(local_mix_kernel, out_shape=jax.ShapeDtypeStruct((row_devi...  2.58 us
  transfers between devices with their start and end apart: 2, of which 2 were waited for; matrix products, arithmetic and copies ran while one was open for 9% of the time, Pallas kernels for 0%

profile of v18, /device:TPU:1, one launch (start us, length us, event | category | flops | bytes accessed | tf_op | source)
XLA Modules:
  0.0 84.9 jit_solution(13595021456020202910)
XLA Ops:
  0.0 0.0 copy-start
  0.0 2.6 %shard_map.64 = f32[128,16,128]{2,1,0:T(8,128)} custom-call(bf16[64,4096]{1,0:T(8,128)(2,1)} %matrix_ref.1, s32[1,4096]{1,0:T(1,128)} %bitcast.32, bf16[128,128]{1,0:T(8,128)(2,1)} %constant.99.clone.table_ref), custom_call_target="tpu_custom_call" | custom-call | tf_op jit(solution)/shard_map/pallas_call | solution.py:118
  2.6 16.3 %all-to-all-start = ((f32[128,16,128]{2,1,0:T(8,128)}), f32[128,16,128]{2,1,0:T(8,128)S(1)}, u32[]{:S(2)}, u32[]{:S(2)}) async-start(f32[128,16,128]{2,1,0:T(8,128)} %shard_map.64), calls=%async_computation | async-start | bytes 2097152 | tf_op jit(solution)/shard_map/all_to_all | solution.py:144
  19.0 0.1 copy.59
  19.1 0.1 reshape.404
  19.3 0.0 copy-done
  19.3 4.5 %gather_fusion.1 = s32[512]{0:T(512)S(1)} fusion(s32[256,256]{1,0:T(8,128)S(1)} %copy-done, s32[512]{0:T(512)S(1)} %reshape.404), kind=kCustom, calls=%fused_computation.1 | custom fusion | bytes 8192 | tf_op jit(solution)/shard_map/jit(take_along_axis)/gather | solution.py:154
  23.8 0.1 gather.11
  23.9 0.1 reshape.407
  24.1 0.1 copy.62
  24.2 0.1 copy.63
  24.4 0.1 reshape.398
  24.5 0.0 copy-start.3
  24.5 0.1 copy.60
  24.6 0.0 copy-start.4
  24.6 0.7 copy-done.4
  25.3 0.2 convert_reduce_fusion
  25.5 0.6 fusion.9
  26.1 1.3 %pad_add_fusion.2.scalar_ref = s32[2]{0:T(128)} fusion(s32[1]{0:T(128)} %bitcast.11, s32[1]{0:T(128)} %bitcast.10), kind=kLoop, calls=%fused_computation.53 | loop fusion | flops 2 | bytes 16 | tf_op jit(solution)/shard_map/stack | solution.py:174
  27.4 21.8 %all-to-all-done = f32[128,16,128]{2,1,0:T(8,128)S(1)} async-done(((f32[128,16,128]{2,1,0:T(8,128)}), f32[128,16,128]{2,1,0:T(8,128)S(1)}, u32[]{:S(2)}, u32[]{:S(2)}) %all-to-all-start) | async-done | bytes 1048608 | tf_op jit(solution)/shard_map/all_to_all | solution.py:144
  49.2 0.0 copy-done.3
  49.2 1.4 %fusion = f32[16,128,128]{1,2,0:T(8,128)S(1)} fusion(f32[128,128,1]{1,0,2:T(8,128)S(1)} %copy-done.3, f32[128,16,128]{2,1,0:T(8,128)S(1)} %all-to-all-done), kind=kOutput, calls=%fused_computation.2 | convolution fusion | flops 402653184 | bytes 2162688 | tf_op jit(solution)/shard_map/st,tvl->vsl/dot_general | solution.py:146
  50.6 1.0 %gather_fusion = f32[512,128]{1,0:T(8,128)S(1)} fusion(f32[2048,128]{1,0:T(8,128)S(1)} %bitcast.26, s32[1024]{0:T(1024)S(1)} %pad_clamp_fusion), kind=kCustom, calls=%fused_computation | custom fusion | bytes 526336 | tf_op jit(solution)/shard_map/jit(_take)/gather | solution.py:157
  51.6 0.1 copy.64
  51.8 0.4 fusion.2
  52.2 18.5 %all_to_all.10 = f32[128,4,128]{2,1,0:T(4,128)S(1)} all-to-all(f32[128,4,128]{2,1,0:T(4,128)S(1)} %bitcast.30), channel_id=1, replica_groups=mesh['rows'=128,'cols'=2] {'rows'}, dimensions={0} | all-to-all | bytes 524288 | tf_op jit(solution)/shard_map/all_to_all | solution.py:176
  70.7 0.1 copy.66
  70.8 0.3 copy.67
  71.1 0.2 copy.69.own_ref
  71.3 0.0 copy-start.1
  71.3 3.6 %collective-permute-start = (f32[4,64,256]{2,1,0:T(8,128)S(1)}, f32[4,64,256]{2,1,0:T(8,128)S(1)}, u32[]{:S(2)}, u32[]{:S(2)}) collective-permute-start(f32[4,64,256]{2,1,0:T(8,128)S(1)} %copy.69.own_ref), channel_id=1, source_target_pairs={{0,1},{1,0},{2,3},{3,2},{4,5},{5,4},{6,7},{7,6},{8,9},{9,8},{10,11... | collective-permute-start | bytes 786440 | tf_op jit(solution)/shard_map/ppermute | solution.py:179
  74.9 1.2 %collective-permute-done.other_ref = f32[4,64,256]{2,1,0:T(8,128)S(1)} collective-permute-done((f32[4,64,256]{2,1,0:T(8,128)S(1)}, f32[4,64,256]{2,1,0:T(8,128)S(1)}, u32[]{:S(2)}, u32[]{:S(2)}) %collective-permute-start) | collective-permute-done | bytes 262176 | tf_op jit(solution)/shard_map/ppermute | solution.py:179
  76.0 0.0 copy-done.1
  76.0 0.0 copy-start.2
  76.0 0.7 copy-done.2
  76.7 8.1 %shard_map.65 = f32[4,64,128]{2,1,0:T(8,128)} custom-call(s32[2]{0:T(128)} %pad_add_fusion.2.scalar_ref, f32[4,64,256]{2,1,0:T(8,128)} %copy-done.1, f32[4,64,256]{2,1,0:T(8,128)} %copy-done.2), custom_call_target="tpu_custom_call" | custom-call | tf_op jit(solution)/shard_map/pallas_call | solution.py:78
  (9 shorter events, 0.2 us)
Async XLA Ops:
  0.0 19.3 %copy-start = (s32[256,256]{1,0:T(8,128)S(1)}, s32[256,256]{1,0:T(8,128)}, u32[]{:S(2)}) copy-start(s32[256,256]{1,0:T(8,128)} %param.8) | copy-start | bytes 786436
  2.6 46.6 %all-to-all-start = ((f32[128,16,128]{2,1,0:T(8,128)}), f32[128,16,128]{2,1,0:T(8,128)S(1)}, u32[]{:S(2)}, u32[]{:S(2)}) async-start(f32[128,16,128]{2,1,0:T(8,128)} %shard_map.64), calls=%async_computation | async-start | bytes 2097152 | tf_op jit(solution)/shard_map/all_to_all | solution.py:144
  24.5 24.7 %copy-start.3 = (f32[128,128,1]{1,0,2:T(8,128)S(1)}, f32[128,128,1]{1,0,2:T(8,128)}, u32[]{:S(2)}) copy-start(f32[128,128,1]{1,0,2:T(8,128)} %constant.114) | copy-start | bytes 196612
  24.6 0.7 copy-start.4
  71.3 4.8 %copy-start.1 = (f32[4,64,256]{2,1,0:T(8,128)}, f32[4,64,256]{2,1,0:T(8,128)S(1)}, u32[]{:S(2)}) copy-start(f32[4,64,256]{2,1,0:T(8,128)S(1)} %copy.69.own_ref) | copy-start | bytes 786436
  71.3 4.8 %collective-permute-start = (f32[4,64,256]{2,1,0:T(8,128)S(1)}, f32[4,64,256]{2,1,0:T(8,128)S(1)}, u32[]{:S(2)}, u32[]{:S(2)}) collective-permute-start(f32[4,64,256]{2,1,0:T(8,128)S(1)} %copy.69.own_ref), channel_id=1, source_target_pairs={{0,1},{1,0},{2,3},{3,2},{4,5},{5,4},{6,7},{7,6},{8,9},{9,8},{10,11... | collective-permute-start | bytes 786440 | tf_op jit(solution)/shard_map/ppermute | solution.py:179
  76.0 0.7 copy-start.2
